TPU v7x, 512 devices: a whole 4x4x16 slice. The times are simulated.
512 devices in a mesh: grp: 8 (over x, y_lo), dom: 64 (over y_hi, z, core).
Axes of the slice: x: 4, y: 4 (y_hi: 2, y_lo: 2; y = y_hi * 2 + y_lo), z: 16, core: 2. Of those that a mesh axis runs over, the one named last changes fastest.
Arguments:
- state: float32 [56, 9, 65536], P(None, None, ('grp', 'dom')), may hold values from -6 to 6
- star: float32 [3, 9, 9, 65536], P(None, None, None, ('grp', 'dom')), may hold values from -1.75 to 1.75
- flux_own: float32 [4, 9, 9, 65536], P(None, None, None, ('grp', 'dom')), may hold values from -0.875 to 0.875
- flux_nbr: float32 [4, 9, 9, 65536], P(None, None, None, ('grp', 'dom')), may hold values from -0.875 to 0.875
- stiff: float32 [3, 56, 56], replicated, may hold values from -0.75 to 0.75
- trace: float32 [4, 21, 56], replicated, may hold values from -0.75 to 0.75
- lift: float32 [4, 56, 21], replicated, may hold values from -1.25 to 1.25
- nbr_slot: int32 [4, 65536], P(None, ('grp', 'dom')), may hold values from 0 to 511, as said below
- nbr_face: int32 [4, 65536], P(None, ('grp', 'dom')), may hold values from 0 to 3, as said below
- send_slot: int32 [196608], P(('grp', 'dom')), may hold values from 0 to 511, as said below
Outputs:
- new_state: float32 [56, 9, 65536], P(None, None, ('grp', 'dom'))
Inputs may be any that keep to these rules, and one draw needn't show every extreme that they name: `nbr_slot`: on each device, the values below 128 name a local element whose face nbr_face[f, e] names element e back through face f; the value 128 + s names received slot s, and every slot 0 to 383 is named by exactly one face of the device. For a face that names a received slot whose sending device exists, nbr_face is the face c // 128 of the sender's send_slot entry c for that slot; where the sender does not exist it is arbitrary. `send_slot`: on each device, 384 distinct values f * 128 + e naming faces of its own elements; none of these faces has a local neighbour.
All inputs are finite; a program needn't handle non-finite values.
Results may differ from a plain program's by a relative error of at most 0.0003.
Values sent between devices are 32-bit elements; how exact they have to be, the bound alone decides.
No kernel may reach another device: no remote copies, remote signals or barrier semaphores. Data moves between devices by JAX's collectives and lax.ppermute only.
A program may use at most 64 MiB of HBM per device.

v0:
```python
import math

import jax
import jax.numpy as jnp
from jax import lax
from jax.experimental import pallas as pl
from jax.experimental.pallas import tpu as pltpu
from jax.sharding import PartitionSpec as P

ORDER = 6
NB = 56
NQ = 9
NF = 21
FP = 24
E = 128
LN = NQ * E
TR = NQ * FP
KP = 256

HI = lax.Precision.HIGHEST
F32 = jnp.float32

W_FIRST = [0.5 ** (k + 1) / math.factorial(k + 1) for k in range(ORDER)]
W_LATER = [(1.0 - 0.5 ** (k + 1)) / math.factorial(k + 1) for k in range(ORDER)]


def _dot(a, b):
    return jnp.dot(a, b, precision=HI, preferred_element_type=F32)


def _mix_vol(x_ref, star_ref, y_ref):
    for d in range(3):
        for q in range(NQ):
            acc = None
            for p in range(NQ):
                t = x_ref[:, p * E:(p + 1) * E] * star_ref[d, p, q:q + 1, :]
                acc = t if acc is None else acc + t
            y_ref[d * NB:(d + 1) * NB, q * E:(q + 1) * E] = acc


def _taylor(x_ref, star_ref, stiffc, d_ref, y_ref, accs):
    x = x_ref[...]
    for ref, w in accs:
        ref[...] = w[0] * x
    d_ref[...] = x
    for k in range(ORDER - 1):
        _mix_vol(d_ref, star_ref, y_ref)
        dn = -_dot(stiffc, y_ref[...])
        d_ref[...] = dn
        for ref, w in accs:
            ref[...] = ref[...] + w[k + 1] * dn


def _table(x_ref, trace_ref, yt_ref, t_ref):
    yt_ref[...] = _dot(trace_ref[...], x_ref[...])
    for f in range(4):
        for p in range(NQ):
            t_ref[p * FP:(p + 1) * FP, f * E:(f + 1) * E] = yt_ref[f * FP:(f + 1) * FP, p * E:(p + 1) * E]


def _send(t_ref, send_ref, lo_ref, hi_ref, g_ref):
    rows = lax.broadcasted_iota(jnp.int32, (4 * E, 3 * E), 0)
    onehot = jnp.where(rows == send_ref[...], 1.0, 0.0).astype(F32)
    s = _dot(t_ref[...], onehot)
    lo_ref[...] = s[:, 0:E]
    hi_ref[...] = s[:, E:2 * E]
    g_ref[...] = s[:, 2 * E:3 * E]


def _gather(comb, slot_ref, face_ref, g_ref):
    rows = lax.broadcasted_iota(jnp.int32, (8 * E, E), 0)
    for f in range(4):
        v = slot_ref[f:f + 1, :]
        nf = face_ref[f:f + 1, :]
        s = v - E
        src = jnp.where(v < E, nf * E + v, 4 * E + s + jnp.where(s >= 2 * E, 64, 0))
        onehot = jnp.where(rows == src, 1.0, 0.0).astype(F32)
        g_ref[:, f * E:(f + 1) * E] = _dot(comb, onehot)


def _update(b_ref, x_ref, s_ref, g_ref, star_ref, fo_ref, fn_ref, stiffT, lift, y_ref, yf_ref, out_ref):
    _mix_vol(x_ref, star_ref, y_ref)
    vol = _dot(stiffT, y_ref[...])
    for f in range(4):
        for q in range(NQ):
            acc = None
            for p in range(NQ):
                t = (s_ref[p * FP:(p + 1) * FP, f * E:(f + 1) * E] * fo_ref[f, p, q:q + 1, :]
                     + g_ref[p * FP:(p + 1) * FP, f * E:(f + 1) * E] * fn_ref[f, p, q:q + 1, :])
                acc = t if acc is None else acc + t
            yf_ref[f * FP:(f + 1) * FP, q * E:(q + 1) * E] = acc
    ftot = _dot(lift, yf_ref[...])
    out_ref[...] = (b_ref[...] + vol) - ftot


def _kernel_a(x_ref, star_ref, consts_ref, trace_ref, send_ref,
              first_ref, fl_ref, t1_ref, t1l_ref, s1lo, s1hi, s1g, sllo, slhi, slg,
              d_ref, y_ref, yt_ref, later_ref, tl_ref):
    y_ref[3 * NB:KP, :] = jnp.zeros((KP - 3 * NB, LN), F32)
    stiffc = consts_ref[:, 0:KP]
    _taylor(x_ref, star_ref, stiffc, d_ref, y_ref, [(first_ref, W_FIRST), (later_ref, W_LATER)])
    fl_ref[...] = first_ref[...] + later_ref[...]
    _table(first_ref, trace_ref, yt_ref, t1_ref)
    _table(later_ref, trace_ref, yt_ref, tl_ref)
    t1l_ref[...] = t1_ref[...] + tl_ref[...]
    _send(t1_ref, send_ref, s1lo, s1hi, s1g)
    _send(tl_ref, send_ref, sllo, slhi, slg)


def _kernel_b(flag_ref, x_ref, first_ref, fl_ref, t1_ref, t1l_ref, sllo, slhi, slg,
              r1lo, r1hi, r1glo, r1ghi, slot_ref, face_ref, star_ref, fo_ref, fn_ref,
              consts_ref, trace_ref, send_ref,
              base_ref, integ_ref, own_ref, s2lo, s2hi, s2g,
              d_ref, y_ref, yt_ref, yf_ref, g_ref):
    fault = flag_ref[0] == 1

    @pl.when(fault)
    def _():
        y_ref[3 * NB:KP, :] = jnp.zeros((KP - 3 * NB, LN), F32)
        comb = jnp.concatenate([t1_ref[...], r1lo[...], r1hi[...], r1glo[...], r1ghi[...]], axis=1)
        _gather(comb, slot_ref, face_ref, g_ref)
        _update(x_ref, first_ref, t1_ref, g_ref, star_ref, fo_ref, fn_ref,
                consts_ref[:, KP:2 * KP], consts_ref[:, 2 * KP:2 * KP + 4 * FP], y_ref, yf_ref, base_ref)
        _taylor(base_ref, star_ref, consts_ref[:, 0:KP], d_ref, y_ref, [(integ_ref, W_FIRST)])
        _table(integ_ref, trace_ref, yt_ref, own_ref)
        _send(own_ref, send_ref, s2lo, s2hi, s2g)

    @pl.when(jnp.logical_not(fault))
    def _():
        base_ref[...] = x_ref[...]
        integ_ref[...] = fl_ref[...]
        own_ref[...] = t1l_ref[...]
        s2lo[...] = sllo[...]
        s2hi[...] = slhi[...]
        s2g[...] = slg[...]


def _kernel_c(flag_ref, base_ref, integ_ref, own_ref, r1lo, r1hi, r1glo, r1ghi,
              r2lo, r2hi, r2glo, r2ghi, slot_ref, face_ref, star_ref, fo_ref, fn_ref, consts_ref,
              out_ref, y_ref, yf_ref, g_ref):
    keep = (1 - flag_ref[0]).astype(F32)
    y_ref[3 * NB:KP, :] = jnp.zeros((KP - 3 * NB, LN), F32)
    comb = jnp.concatenate(
        [own_ref[...], r2lo[...] + keep * r1lo[...], r2hi[...] + keep * r1hi[...],
         r2glo[...] + keep * r1glo[...], r2ghi[...] + keep * r1ghi[...]], axis=1)
    _gather(comb, slot_ref, face_ref, g_ref)
    _update(base_ref, integ_ref, own_ref, g_ref, star_ref, fo_ref, fn_ref,
            consts_ref[:, KP:2 * KP], consts_ref[:, 2 * KP:2 * KP + 4 * FP], y_ref, yf_ref, out_ref)


def _vmem():
    return pl.BlockSpec(memory_space=pltpu.VMEM)


def _smem():
    return pl.BlockSpec(memory_space=pltpu.SMEM)


def _sds(shape):
    return jax.ShapeDtypeStruct(shape, F32)


def exchange(lo, hi, g):
    n_dom = lax.axis_size("dom")
    n_grp = lax.axis_size("grp")
    from_lo = lax.ppermute(hi, "dom", [(i, i + 1) for i in range(n_dom - 1)])
    from_hi = lax.ppermute(lo, "dom", [(i + 1, i) for i in range(n_dom - 1)])
    from_glo = lax.ppermute(g, "grp", [(i, i + 1) for i in range(n_grp - 1)])
    from_ghi = lax.ppermute(g, "grp", [(i + 1, i) for i in range(n_grp - 1)])
    return from_lo, from_hi, from_glo, from_ghi


def local(state, star, flux_own, flux_nbr, stiff, trace, lift, nbr_slot, nbr_face, send_slot):
    flag = (lax.axis_index("grp") == 0).astype(jnp.int32).reshape(1)
    x0 = state.reshape(NB, LN)
    stiff_cat = jnp.concatenate([stiff[0], stiff[1], stiff[2]], axis=1)
    stiff_t_cat = jnp.concatenate([stiff[0].T, stiff[1].T, stiff[2].T], axis=1)
    lift_cat = jnp.transpose(jnp.pad(lift, ((0, 0), (0, 0), (0, FP - NF))), (1, 0, 2)).reshape(NB, 4 * FP)
    consts = jnp.concatenate(
        [jnp.pad(stiff_cat, ((0, 0), (0, KP - 3 * NB))),
         jnp.pad(stiff_t_cat, ((0, 0), (0, KP - 3 * NB))),
         jnp.pad(lift_cat, ((0, 0), (0, 128 - 4 * FP)))], axis=1)
    trace_pad = jnp.pad(trace, ((0, 0), (0, FP - NF), (0, 0))).reshape(4 * FP, NB)
    send = send_slot.reshape(1, 3 * E)

    field = _sds((NB, LN))
    table = _sds((TR, 4 * E))
    part = _sds((TR, E))
    outs_a = pl.pallas_call(
        _kernel_a,
        out_shape=(field, field, table, table, part, part, part, part, part, part),
        in_specs=[_vmem()] * 5,
        out_specs=tuple([_vmem()] * 10),
        scratch_shapes=[pltpu.VMEM((NB, LN), F32), pltpu.VMEM((KP, LN), F32), pltpu.VMEM((4 * FP, LN), F32),
                        pltpu.VMEM((NB, LN), F32), pltpu.VMEM((TR, 4 * E), F32)],
    )(x0, star, consts, trace_pad, send)
    first, fl, t1, t1l, s1lo, s1hi, s1g, sllo, slhi, slg = outs_a

    r1 = exchange(s1lo, s1hi, s1g)

    outs_b = pl.pallas_call(
        _kernel_b,
        out_shape=(field, field, table, part, part, part),
        in_specs=[_smem()] + [_vmem()] * 20,
        out_specs=tuple([_vmem()] * 6),
        scratch_shapes=[pltpu.VMEM((NB, LN), F32), pltpu.VMEM((KP, LN), F32), pltpu.VMEM((4 * FP, LN), F32),
                        pltpu.VMEM((4 * FP, LN), F32), pltpu.VMEM((TR, 4 * E), F32)],
    )(flag, x0, first, fl, t1, t1l, sllo, slhi, slg, *r1, nbr_slot, nbr_face, star, flux_own, flux_nbr,
      consts, trace_pad, send)
    base, integ, own, s2lo, s2hi, s2g = outs_b

    r2 = exchange(s2lo, s2hi, s2g)

    out = pl.pallas_call(
        _kernel_c,
        out_shape=field,
        in_specs=[_smem()] + [_vmem()] * 17,
        out_specs=_vmem(),
        scratch_shapes=[pltpu.VMEM((KP, LN), F32), pltpu.VMEM((4 * FP, LN), F32), pltpu.VMEM((TR, 4 * E), F32)],
    )(flag, base, integ, own, *r1, *r2, nbr_slot, nbr_face, star, flux_own, flux_nbr, consts)
    return out.reshape(NB, NQ, E)


def solution(mesh):
    in_specs = (
        P(None, None, ("grp", "dom")),
        P(None, None, None, ("grp", "dom")),
        P(None, None, None, ("grp", "dom")),
        P(None, None, None, ("grp", "dom")),
        P(),
        P(),
        P(),
        P(None, ("grp", "dom")),
        P(None, ("grp", "dom")),
        P(("grp", "dom")),
    )
    out_specs = P(None, None, ("grp", "dom"))
    return jax.shard_map(local, mesh=mesh, in_specs=in_specs, out_specs=out_specs, check_vma=False)
```

profile of v0, /device:TPU:24, one launch (start us, length us, event | category | flops | bytes accessed | tf_op | source)
XLA Modules:
  0.0 78.3 jit_solution(15177042002406524656)
XLA Ops:
  0.0 1.3 %reshape.25.send_ref = s32[1,384]{1,0:T(1,128)} reshape(s32[384]{0:T(512)} %param.19) | data formatting | bytes 3072 | tf_op jit(solution)/shard_map/reshape | solution.py:184
  1.3 0.8 %copy.46 = f32[4,21,56]{2,1,0:T(8,128)S(1)} copy(f32[4,21,56]{2,0,1:T(4,128)} %param.15) | data formatting | bytes 37632
  2.2 0.8 %copy-done.12 = f32[3,56,56]{2,1,0:T(8,128)S(1)} copy-done((f32[3,56,56]{2,1,0:T(8,128)S(1)}, f32[3,56,56]{2,1,0:T(8,128)}, u32[]{:S(2)}) %copy-start.12) | copy-done | bytes 37656
  3.3 0.8 %copy-done.7 = f32[3,9,9,128]{3,0,2,1:T(4,128)S(1)} copy-done((f32[3,9,9,128]{3,0,2,1:T(4,128)S(1)}, f32[3,9,9,128]{3,0,2,1:T(4,128)}, u32[]{:S(2)}) %copy-start.7) | copy-done | bytes 124440
  4.2 0.7 copy.34.star_ref
  4.9 0.7 copy_bitcast_fusion.x_ref
  6.3 0.7 select_maximum_fusion.consts_ref
  7.0 8.7 %shard_map.100 = (f32[56,1152]{1,0:T(8,128)}, f32[56,1152]{1,0:T(8,128)}, f32[216,512]{1,0:T(8,128)}, f32[216,512]{1,0:T(8,128)}, f32[216,128]{1,0:T(8,128)}, /*...) custom-call(f32[56,1152]{1,0:T(8,128)} %copy_bitcast_fusion.x_ref, ...), custom_call_target="tpu_custom_call" | custom-call | tf_op jit(solution)/shard_map/pallas_call | solution.py:189
  15.7 1.9 %collective-permute-start = (f32[216,128]{1,0:T(8,128)}, f32[216,128]{1,0:T(8,128)S(1)}, u32[]{:S(2)}, u32[]{:S(2)}) collective-permute-start(f32[216,128]{1,0:T(8,128)} %get-tuple-element.28), channel_id=1, source_target_pairs={{0,1},{1,2},{2,3},{3,4},{4,5},{5,6},{6,7},{7,8},{8,9},{9,10},{10,1... | collective-permute-start | bytes 331784 | tf_op jit(solution)/shard_map/ppermute | solution.py:166
  17.6 11.5 %collective-permute-start.1 = (f32[216,128]{1,0:T(8,128)}, f32[216,128]{1,0:T(8,128)S(1)}, u32[]{:S(2)}, u32[]{:S(2)}) collective-permute-start(f32[216,128]{1,0:T(8,128)} %get-tuple-element.29), channel_id=1, source_target_pairs={{1,0},{2,1},{3,2},{4,3},{5,4},{6,5},{7,6},{8,7},{9,8},{10,9},{11,1... | collective-permute-start | bytes 331784 | tf_op jit(solution)/shard_map/ppermute | solution.py:167
  29.1 1.9 %collective-permute-start.3 = (f32[216,128]{1,0:T(8,128)}, f32[216,128]{1,0:T(8,128)S(1)}, u32[]{:S(2)}, u32[]{:S(2)}) collective-permute-start(f32[216,128]{1,0:T(8,128)} %get-tuple-element.30), channel_id=1, source_target_pairs={{64,0},{128,64},{192,128},{256,192},{320,256},{384,320},{448,384},... | collective-permute-start | bytes 331784 | tf_op jit(solution)/shard_map/ppermute | solution.py:169
  31.0 4.8 %collective-permute-start.2 = (f32[216,128]{1,0:T(8,128)}, f32[216,128]{1,0:T(8,128)S(1)}, u32[]{:S(2)}, u32[]{:S(2)}) collective-permute-start(f32[216,128]{1,0:T(8,128)} %get-tuple-element.30), channel_id=1, source_target_pairs={{0,64},{64,128},{128,192},{192,256},{256,320},{320,384},{384,448},... | collective-permute-start | bytes 331784 | tf_op jit(solution)/shard_map/ppermute | solution.py:168
  35.9 0.7 copy.36.fo_ref
  36.8 0.8 copy.37.fn_ref
  37.6 0.8 %collective-permute-done.2.r1glo = f32[216,128]{1,0:T(8,128)S(1)} collective-permute-done((f32[216,128]{1,0:T(8,128)}, f32[216,128]{1,0:T(8,128)S(1)}, u32[]{:S(2)}, u32[]{:S(2)}) %collective-permute-start.2) | collective-permute-done | bytes 110624 | tf_op jit(solution)/shard_map/ppermute | solution.py:168
  38.5 0.6 copy-done.4
  39.1 3.1 %shard_map.101 = (f32[56,1152]{1,0:T(8,128)}, f32[56,1152]{1,0:T(8,128)}, f32[216,512]{1,0:T(8,128)}, f32[216,128]{1,0:T(8,128)}, f32[216,128]{1,0:T(8,128)}, /*index=5*/f32[216,128]{1,0:T(8,128)}) custom-call(s32[1]{0:T(128)} %bitcast.flag_ref, f32[56,1152]{1,0:T(8,128)} %copy_bitcast_fusion.x_ref, f32[56,1152]{1,0:T(8,128)} %get-tuple-element.21.first_ref, ...), custom_call_target="tpu_custom_call" | custom-call | tf_op jit(solution)/shard_map/pallas_call | solution.py:201
  42.2 1.9 %collective-permute-start.4 = (f32[216,128]{1,0:T(8,128)}, f32[216,128]{1,0:T(8,128)S(1)}, u32[]{:S(2)}, u32[]{:S(2)}) collective-permute-start(f32[216,128]{1,0:T(8,128)} %get-tuple-element.34), channel_id=1, source_target_pairs={{0,1},{1,2},{2,3},{3,4},{4,5},{5,6},{6,7},{7,8},{8,9},{9,10},{10,1... | collective-permute-start | bytes 331784 | tf_op jit(solution)/shard_map/ppermute | solution.py:166
  44.1 7.3 %collective-permute-start.5 = (f32[216,128]{1,0:T(8,128)}, f32[216,128]{1,0:T(8,128)S(1)}, u32[]{:S(2)}, u32[]{:S(2)}) collective-permute-start(f32[216,128]{1,0:T(8,128)} %get-tuple-element.35), channel_id=1, source_target_pairs={{1,0},{2,1},{3,2},{4,3},{5,4},{6,5},{7,6},{8,7},{9,8},{10,9},{11,1... | collective-permute-start | bytes 331784 | tf_op jit(solution)/shard_map/ppermute | solution.py:167
  51.4 11.1 %collective-permute-start.7 = (f32[216,128]{1,0:T(8,128)}, f32[216,128]{1,0:T(8,128)S(1)}, u32[]{:S(2)}, u32[]{:S(2)}) collective-permute-start(f32[216,128]{1,0:T(8,128)} %get-tuple-element.36), channel_id=1, source_target_pairs={{64,0},{128,64},{192,128},{256,192},{320,256},{384,320},{448,384},... | collective-permute-start | bytes 331784 | tf_op jit(solution)/shard_map/ppermute | solution.py:169
  62.5 2.1 %collective-permute-start.6 = (f32[216,128]{1,0:T(8,128)}, f32[216,128]{1,0:T(8,128)S(1)}, u32[]{:S(2)}, u32[]{:S(2)}) collective-permute-start(f32[216,128]{1,0:T(8,128)} %get-tuple-element.36), channel_id=1, source_target_pairs={{0,64},{64,128},{128,192},{192,256},{256,320},{320,384},{384,448},... | collective-permute-start | bytes 331784 | tf_op jit(solution)/shard_map/ppermute | solution.py:168
  65.1 4.2 %collective-permute-done.6.r2glo = f32[216,128]{1,0:T(8,128)S(1)} collective-permute-done((f32[216,128]{1,0:T(8,128)}, f32[216,128]{1,0:T(8,128)S(1)}, u32[]{:S(2)}, u32[]{:S(2)}) %collective-permute-start.6) | collective-permute-done | bytes 110624 | tf_op jit(solution)/shard_map/ppermute | solution.py:168
  70.0 6.7 %shard_map.102 = f32[56,1152]{1,0:T(8,128)} custom-call(s32[1]{0:T(128)} %bitcast.flag_ref, f32[56,1152]{1,0:T(8,128)} %get-tuple-element.31.base_ref, f32[56,1152]{1,0:T(8,128)} %get-tuple-element.32.integ_ref, f32[216,512]{1,0:T(8,128)} %get-tuple-element.33.own_ref, f32[216,128]{1,0:T(8,128)} %copy-done.1, f32[216,128]{1,0:T(8,128)} %copy-done.2, ...), custom_call_target="tpu_custom_call" | custom-call | tf_op jit(solution)/shard_map/pallas_call | solution.py:214
  76.7 1.7 %copy_bitcast_fusion.1 = f32[56,9,128]{2,0,1:T(8,128)} fusion(f32[56,1152]{1,0:T(8,128)} %shard_map.102), kind=kLoop, calls=%fused_computation.1 | loop fusion | bytes 516096 | tf_op jit(solution)/shard_map/reshape | solution.py:221
  (42 shorter events, 2.5 us)
Async XLA Ops:
  0.0 4.9 %copy-start = (f32[56,9,128]{2,0,1:T(8,128)S(1)}, f32[56,9,128]{2,0,1:T(8,128)}, u32[]{:S(2)}) copy-start(f32[56,9,128]{2,0,1:T(8,128)} %param.10) | copy-start | bytes 774148
  1.3 0.8 %copy-start.13 = (f32[4,56,21]{1,0,2:T(4,128)S(1)}, f32[4,56,21]{1,0,2:T(4,128)}, u32[]{:S(2)}) copy-start(f32[4,56,21]{1,0,2:T(4,128)} %param.16) | copy-start | bytes 56452
  2.1 0.9 %copy-start.12 = (f32[3,56,56]{2,1,0:T(8,128)S(1)}, f32[3,56,56]{2,1,0:T(8,128)}, u32[]{:S(2)}) copy-start(f32[3,56,56]{2,1,0:T(8,128)} %param.14) | copy-start | bytes 112900
  3.2 0.9 %copy-start.7 = (f32[3,9,9,128]{3,0,2,1:T(4,128)S(1)}, f32[3,9,9,128]{3,0,2,1:T(4,128)}, u32[]{:S(2)}) copy-start(f32[3,9,9,128]{3,0,2,1:T(4,128)} %param.11) | copy-start | bytes 373252
  7.0 28.9 %copy-start.5 = (f32[4,9,9,128]{3,0,2,1:T(4,128)S(1)}, f32[4,9,9,128]{3,0,2,1:T(4,128)}, u32[]{:S(2)}) copy-start(f32[4,9,9,128]{3,0,2,1:T(4,128)} %param.12) | copy-start | bytes 497668
  15.7 21.9 %collective-permute-start = (f32[216,128]{1,0:T(8,128)}, f32[216,128]{1,0:T(8,128)S(1)}, u32[]{:S(2)}, u32[]{:S(2)}) collective-permute-start(f32[216,128]{1,0:T(8,128)} %get-tuple-element.28), channel_id=1, source_target_pairs={{0,1},{1,2},{2,3},{3,4},{4,5},{5,6},{6,7},{7,8},{8,9},{9,10},{10,1... | collective-permute-start | bytes 331784 | tf_op jit(solution)/shard_map/ppermute | solution.py:166
  17.6 20.0 %collective-permute-start.1 = (f32[216,128]{1,0:T(8,128)}, f32[216,128]{1,0:T(8,128)S(1)}, u32[]{:S(2)}, u32[]{:S(2)}) collective-permute-start(f32[216,128]{1,0:T(8,128)} %get-tuple-element.29), channel_id=1, source_target_pairs={{1,0},{2,1},{3,2},{4,3},{5,4},{6,5},{7,6},{8,7},{9,8},{10,9},{11,1... | collective-permute-start | bytes 331784 | tf_op jit(solution)/shard_map/ppermute | solution.py:167
  29.1 8.5 %collective-permute-start.3 = (f32[216,128]{1,0:T(8,128)}, f32[216,128]{1,0:T(8,128)S(1)}, u32[]{:S(2)}, u32[]{:S(2)}) collective-permute-start(f32[216,128]{1,0:T(8,128)} %get-tuple-element.30), channel_id=1, source_target_pairs={{64,0},{128,64},{192,128},{256,192},{320,256},{384,320},{448,384},... | collective-permute-start | bytes 331784 | tf_op jit(solution)/shard_map/ppermute | solution.py:169
  31.0 7.5 %collective-permute-start.2 = (f32[216,128]{1,0:T(8,128)}, f32[216,128]{1,0:T(8,128)S(1)}, u32[]{:S(2)}, u32[]{:S(2)}) collective-permute-start(f32[216,128]{1,0:T(8,128)} %get-tuple-element.30), channel_id=1, source_target_pairs={{0,64},{64,128},{128,192},{192,256},{256,320},{320,384},{384,448},... | collective-permute-start | bytes 331784 | tf_op jit(solution)/shard_map/ppermute | solution.py:168
  35.9 1.0 %copy-start.6 = (f32[4,9,9,128]{3,0,2,1:T(4,128)S(1)}, f32[4,9,9,128]{3,0,2,1:T(4,128)}, u32[]{:S(2)}) copy-start(f32[4,9,9,128]{3,0,2,1:T(4,128)} %param.13) | copy-start | bytes 497668
  37.6 0.9 %copy-start.1 = (f32[216,128]{1,0:T(8,128)}, f32[216,128]{1,0:T(8,128)S(1)}, u32[]{:S(2)}) copy-start(f32[216,128]{1,0:T(8,128)S(1)} %collective-permute-done.r1lo) | copy-start | bytes 331780
  37.6 0.9 %copy-start.2 = (f32[216,128]{1,0:T(8,128)}, f32[216,128]{1,0:T(8,128)S(1)}, u32[]{:S(2)}) copy-start(f32[216,128]{1,0:T(8,128)S(1)} %collective-permute-done.1.r1hi) | copy-start | bytes 331780
  37.6 0.9 %copy-start.3 = (f32[216,128]{1,0:T(8,128)}, f32[216,128]{1,0:T(8,128)S(1)}, u32[]{:S(2)}) copy-start(f32[216,128]{1,0:T(8,128)S(1)} %collective-permute-done.3.r1ghi) | copy-start | bytes 331780
  38.5 0.6 copy-start.4
  42.2 22.4 %collective-permute-start.4 = (f32[216,128]{1,0:T(8,128)}, f32[216,128]{1,0:T(8,128)S(1)}, u32[]{:S(2)}, u32[]{:S(2)}) collective-permute-start(f32[216,128]{1,0:T(8,128)} %get-tuple-element.34), channel_id=1, source_target_pairs={{0,1},{1,2},{2,3},{3,4},{4,5},{5,6},{6,7},{7,8},{8,9},{9,10},{10,1... | collective-permute-start | bytes 331784 | tf_op jit(solution)/shard_map/ppermute | solution.py:166
  44.1 20.5 %collective-permute-start.5 = (f32[216,128]{1,0:T(8,128)}, f32[216,128]{1,0:T(8,128)S(1)}, u32[]{:S(2)}, u32[]{:S(2)}) collective-permute-start(f32[216,128]{1,0:T(8,128)} %get-tuple-element.35), channel_id=1, source_target_pairs={{1,0},{2,1},{3,2},{4,3},{5,4},{6,5},{7,6},{8,7},{9,8},{10,9},{11,1... | collective-permute-start | bytes 331784 | tf_op jit(solution)/shard_map/ppermute | solution.py:167
  51.4 13.7 %collective-permute-start.7 = (f32[216,128]{1,0:T(8,128)}, f32[216,128]{1,0:T(8,128)S(1)}, u32[]{:S(2)}, u32[]{:S(2)}) collective-permute-start(f32[216,128]{1,0:T(8,128)} %get-tuple-element.36), channel_id=1, source_target_pairs={{64,0},{128,64},{192,128},{256,192},{320,256},{384,320},{448,384},... | collective-permute-start | bytes 331784 | tf_op jit(solution)/shard_map/ppermute | solution.py:169
  62.5 6.9 %collective-permute-start.6 = (f32[216,128]{1,0:T(8,128)}, f32[216,128]{1,0:T(8,128)S(1)}, u32[]{:S(2)}, u32[]{:S(2)}) collective-permute-start(f32[216,128]{1,0:T(8,128)} %get-tuple-element.36), channel_id=1, source_target_pairs={{0,64},{64,128},{128,192},{192,256},{256,320},{320,384},{384,448},... | collective-permute-start | bytes 331784 | tf_op jit(solution)/shard_map/ppermute | solution.py:168
  64.6 4.7 %copy-start.8 = (f32[216,128]{1,0:T(8,128)}, f32[216,128]{1,0:T(8,128)S(1)}, u32[]{:S(2)}) copy-start(f32[216,128]{1,0:T(8,128)S(1)} %collective-permute-done.4.r2lo) | copy-start | bytes 331780
  64.6 4.7 %copy-start.9 = (f32[216,128]{1,0:T(8,128)}, f32[216,128]{1,0:T(8,128)S(1)}, u32[]{:S(2)}) copy-start(f32[216,128]{1,0:T(8,128)S(1)} %collective-permute-done.5.r2hi) | copy-start | bytes 331780
  65.1 4.2 %copy-start.10 = (f32[216,128]{1,0:T(8,128)}, f32[216,128]{1,0:T(8,128)S(1)}, u32[]{:S(2)}) copy-start(f32[216,128]{1,0:T(8,128)S(1)} %collective-permute-done.7.r2ghi) | copy-start | bytes 331780
  69.3 0.6 copy-start.11
where the time goes:
time: 78.9 us; the launch traced here: 78.3 us
  starting transfers between devices  42.5 us (54%)
  Pallas kernels  18.5 us (23%)
  local copies, waits for them, and re-layouts  10.8 us (14%)
  waiting for transfers between devices  5.5 us (7%)
    ppermute x2, starting transfers between devices, exchange(): from_hi = lax.ppermute(lo, 'dom', [(i + 1, i) for i in range(n_dom - 1)])  18.8 us
    ppermute x2, starting transfers between devices, exchange(): from_ghi = lax.ppermute(g, 'grp', [(i + 1, i) for i in range(n_grp - 1)])  13 us
    pallas_call x1, Pallas kernels, local(): pl.pallas_call(_kernel_a, out_shape=(field, field, table, table, part, pa...  8.69 us
    ppermute x2, starting transfers between devices, exchange(): from_glo = lax.ppermute(g, 'grp', [(i, i + 1) for i in range(n_grp - 1)])  6.96 us
    pallas_call x1, Pallas kernels, local(): pl.pallas_call(_kernel_c, out_shape=field, in_specs=[_smem()] + [_vmem()]...  6.7 us
    unnamed x36, local copies, waits for them, and re-layouts  6.44 us
    ppermute x2, waiting for transfers between devices, exchange(): from_glo = lax.ppermute(g, 'grp', [(i, i + 1) for i in range(n_grp - 1)])  5.06 us
    ppermute x2, starting transfers between devices, exchange(): from_lo = lax.ppermute(hi, 'dom', [(i, i + 1) for i in range(n_dom - 1)])  3.82 us
  transfers between devices with their start and end apart: 8, of which 3 were waited for; matrix products, arithmetic and copies ran while one was open for 2% of the time, Pallas kernels for 0%

commit v1 on v0

v1 whole, which is shorter than its diff:
```python
import math

import jax
import jax.numpy as jnp
from jax import lax
from jax.experimental import pallas as pl
from jax.experimental.pallas import tpu as pltpu
from jax.sharding import PartitionSpec as P

ORDER = 6
NB = 56
NQ = 9
NF = 21
FP = 24
E = 128
LN = NQ * E
TR = NQ * FP

F32 = jnp.float32

W_FIRST = [0.5 ** (k + 1) / math.factorial(k + 1) for k in range(ORDER)]
W_LATER = [(1.0 - 0.5 ** (k + 1)) / math.factorial(k + 1) for k in range(ORDER)]


BF = jnp.bfloat16


def _bdot(a, b):
    return jnp.dot(a, b, preferred_element_type=F32)


def _split2(x):
    hi = x.astype(BF)
    return hi, (x - hi.astype(F32)).astype(BF)


def _dot3(a, b):
    return _bdot(a[0], b[0]) + (_bdot(a[0], b[1]) + _bdot(a[1], b[0]))


def _split3(x):
    hi = x.astype(BF)
    r = x - hi.astype(F32)
    mid = r.astype(BF)
    return hi, mid, (r - mid.astype(F32)).astype(BF)


def _sel(parts, onehot):
    return (_bdot(parts[0], onehot) + _bdot(parts[1], onehot)) + _bdot(parts[2], onehot)


def _load_field(ref):
    return jnp.concatenate([ref[p] for p in range(NQ)], axis=1)


def _store_field(ref, val):
    for q in range(NQ):
        ref[q] = val[:, q * E:(q + 1) * E]


def _mix_vol(a_ref, star_ref, out_ref, sign):
    for q in range(NQ):
        acc = None
        for d in range(3):
            for p in range(NQ):
                t = a_ref[d * NB:(d + 1) * NB, p * E:(p + 1) * E] * star_ref[d, p, q:q + 1, :]
                acc = t if acc is None else acc + t
        out_ref[:, q * E:(q + 1) * E] = acc if sign > 0 else -acc


def _taylor(x, star_ref, stiff_p, d_ref, a_ref, accs):
    for ref, w in accs:
        ref[...] = w[0] * x
    d_ref[...] = x
    for k in range(ORDER - 1):
        a_ref[...] = _dot3(stiff_p, _split2(d_ref[...]))
        _mix_vol(a_ref, star_ref, d_ref, -1)
        dn = d_ref[...]
        for ref, w in accs:
            ref[...] = ref[...] + w[k + 1] * dn


def _table(x, trace_ref, t_ref):
    xp = _split2(x)
    t_ref[...] = jnp.zeros(t_ref.shape, F32)
    for f in range(4):
        yt = _dot3(_split2(trace_ref[f]), xp)
        for p in range(NQ):
            t_ref[p * FP:p * FP + NF, f * E:(f + 1) * E] = yt[:, p * E:(p + 1) * E]


def _send(tables, send_ref, outs):
    rows = lax.broadcasted_iota(jnp.int32, (4 * E, 3 * E), 0)
    onehot = jnp.where(rows == send_ref[...], 1.0, 0.0).astype(BF)
    s = _sel(_split3(jnp.concatenate(tables, axis=0)), onehot)
    for i, (lo_ref, hi_ref, g_ref) in enumerate(outs):
        blk = s[i * TR:(i + 1) * TR]
        lo_ref[...] = blk[:, 0:E]
        hi_ref[...] = blk[:, E:2 * E]
        g_ref[...] = blk[:, 2 * E:3 * E]


def _gather(comb, slot_ref, face_ref, g_ref):
    rows = lax.broadcasted_iota(jnp.int32, (8 * E, E), 0)
    parts = _split3(comb)
    for f in range(4):
        v = slot_ref[f:f + 1, :]
        nf = face_ref[f:f + 1, :]
        s = v - E
        src = jnp.where(v < E, nf * E + v, 4 * E + s + jnp.where(s >= 2 * E, 64, 0))
        onehot = jnp.where(rows == src, 1.0, 0.0).astype(BF)
        g_ref[:, f * E:(f + 1) * E] = _sel(parts, onehot)


def _update(b, x, s_ref, g_ref, star_ref, fo_ref, fn_ref, stiff_t_p, lift_p, a_ref, v_ref, yf_ref):
    a_ref[...] = _dot3(stiff_t_p, _split2(x))
    _mix_vol(a_ref, star_ref, v_ref, 1)
    for f in range(4):
        for q in range(NQ):
            acc = None
            for p in range(NQ):
                t = (s_ref[p * FP:(p + 1) * FP, f * E:(f + 1) * E] * fo_ref[f, p, q:q + 1, :]
                     + g_ref[p * FP:(p + 1) * FP, f * E:(f + 1) * E] * fn_ref[f, p, q:q + 1, :])
                acc = t if acc is None else acc + t
            yf_ref[f * FP:(f + 1) * FP, q * E:(q + 1) * E] = acc
    ftot = _dot3(lift_p, _split2(yf_ref[...]))
    return (b + v_ref[...]) - ftot


def _kernel_a(x_ref, star_ref, stiff_ref, trace_ref, send_ref,
              first_ref, fl_ref, t1_ref, t1l_ref, s1lo, s1hi, s1g, sllo, slhi, slg,
              d_ref, a_ref, acc1_ref, acc2_ref, tl_ref):
    x = _load_field(x_ref)
    _taylor(x, star_ref, _split2(stiff_ref[...]), d_ref, a_ref, [(acc1_ref, W_FIRST), (acc2_ref, W_LATER)])
    first = acc1_ref[...]
    later = acc2_ref[...]
    _store_field(first_ref, first)
    _store_field(fl_ref, first + later)
    _table(first, trace_ref, t1_ref)
    _table(later, trace_ref, tl_ref)
    t1l_ref[...] = t1_ref[...] + tl_ref[...]
    _send([t1_ref[...], tl_ref[...]], send_ref, [(s1lo, s1hi, s1g), (sllo, slhi, slg)])


def _kernel_b(flag_ref, x_ref, first_ref, fl_ref, t1_ref, t1l_ref, sllo, slhi, slg,
              r1lo, r1hi, r1glo, r1ghi, slot_ref, face_ref, star_ref, fo_ref, fn_ref,
              stiff_ref, stiff_t_ref, lift_ref, trace_ref, send_ref,
              base_ref, integ_ref, own_ref, s2lo, s2hi, s2g,
              d_ref, a_ref, v_ref, yf_ref, g_ref, acc_ref):
    fault = flag_ref[0] == 1

    @pl.when(fault)
    def _():
        comb = jnp.concatenate([t1_ref[...], r1lo[...], r1hi[...], r1glo[...], r1ghi[...]], axis=1)
        _gather(comb, slot_ref, face_ref, g_ref)
        mid = _update(_load_field(x_ref), _load_field(first_ref), t1_ref, g_ref, star_ref, fo_ref, fn_ref,
                      _split2(stiff_t_ref[...]), _split2(lift_ref[...]), a_ref, v_ref, yf_ref)
        _store_field(base_ref, mid)
        _taylor(mid, star_ref, _split2(stiff_ref[...]), d_ref, a_ref, [(acc_ref, W_FIRST)])
        second = acc_ref[...]
        _store_field(integ_ref, second)
        _table(second, trace_ref, own_ref)
        _send([own_ref[...]], send_ref, [(s2lo, s2hi, s2g)])

    @pl.when(jnp.logical_not(fault))
    def _():
        base_ref[...] = x_ref[...]
        integ_ref[...] = fl_ref[...]
        own_ref[...] = t1l_ref[...]
        s2lo[...] = sllo[...]
        s2hi[...] = slhi[...]
        s2g[...] = slg[...]


def _kernel_c(flag_ref, base_ref, integ_ref, own_ref, r1lo, r1hi, r1glo, r1ghi,
              r2lo, r2hi, r2glo, r2ghi, slot_ref, face_ref, star_ref, fo_ref, fn_ref,
              stiff_t_ref, lift_ref,
              out_ref, a_ref, v_ref, yf_ref, g_ref):
    keep = (1 - flag_ref[0]).astype(F32)
    comb = jnp.concatenate(
        [own_ref[...], r2lo[...] + keep * r1lo[...], r2hi[...] + keep * r1hi[...],
         r2glo[...] + keep * r1glo[...], r2ghi[...] + keep * r1ghi[...]], axis=1)
    _gather(comb, slot_ref, face_ref, g_ref)
    out = _update(_load_field(base_ref), _load_field(integ_ref), own_ref, g_ref, star_ref, fo_ref, fn_ref,
                  _split2(stiff_t_ref[...]), _split2(lift_ref[...]), a_ref, v_ref, yf_ref)
    _store_field(out_ref, out)


def _vmem():
    return pl.BlockSpec(memory_space=pltpu.VMEM)


def _smem():
    return pl.BlockSpec(memory_space=pltpu.SMEM)


def _sds(shape):
    return jax.ShapeDtypeStruct(shape, F32)


def exchange(lo, hi, g):
    n_dom = lax.axis_size("dom")
    n_grp = lax.axis_size("grp")
    from_lo = lax.ppermute(hi, "dom", [(i, i + 1) for i in range(n_dom - 1)])
    from_hi = lax.ppermute(lo, "dom", [(i + 1, i) for i in range(n_dom - 1)])
    from_glo = lax.ppermute(g, "grp", [(i, i + 1) for i in range(n_grp - 1)])
    from_ghi = lax.ppermute(g, "grp", [(i + 1, i) for i in range(n_grp - 1)])
    return from_lo, from_hi, from_glo, from_ghi


def local(state, star, flux_own, flux_nbr, stiff, trace, lift, nbr_slot, nbr_face, send_slot):
    flag = (lax.axis_index("grp") == 0).astype(jnp.int32).reshape(1)
    x0 = jnp.transpose(state, (1, 0, 2))
    stiff_st = stiff.reshape(3 * NB, NB)
    stiff_t_st = jnp.transpose(stiff, (0, 2, 1)).reshape(3 * NB, NB)
    lift_cat = jnp.transpose(jnp.pad(lift, ((0, 0), (0, 0), (0, FP - NF))), (1, 0, 2)).reshape(NB, 4 * FP)
    send = send_slot.reshape(1, 3 * E)

    field = _sds((NQ, NB, E))
    table = _sds((TR, 4 * E))
    part = _sds((TR, E))
    wide = pltpu.VMEM((NB, LN), F32)
    outs_a = pl.pallas_call(
        _kernel_a,
        out_shape=(field, field, table, table, part, part, part, part, part, part),
        in_specs=[_vmem()] * 5,
        out_specs=tuple([_vmem()] * 10),
        scratch_shapes=[wide, pltpu.VMEM((3 * NB, LN), F32), wide, wide, pltpu.VMEM((TR, 4 * E), F32)],
    )(x0, star, stiff_st, trace, send)
    first, fl, t1, t1l, s1lo, s1hi, s1g, sllo, slhi, slg = outs_a

    r1 = exchange(s1lo, s1hi, s1g)

    outs_b = pl.pallas_call(
        _kernel_b,
        out_shape=(field, field, table, part, part, part),
        in_specs=[_smem()] + [_vmem()] * 22,
        out_specs=tuple([_vmem()] * 6),
        scratch_shapes=[wide, pltpu.VMEM((3 * NB, LN), F32), wide, pltpu.VMEM((4 * FP, LN), F32),
                        pltpu.VMEM((TR, 4 * E), F32), wide],
    )(flag, x0, first, fl, t1, t1l, sllo, slhi, slg, *r1, nbr_slot, nbr_face, star, flux_own, flux_nbr,
      stiff_st, stiff_t_st, lift_cat, trace, send)
    base, integ, own, s2lo, s2hi, s2g = outs_b

    r2 = exchange(s2lo, s2hi, s2g)

    out = pl.pallas_call(
        _kernel_c,
        out_shape=field,
        in_specs=[_smem()] + [_vmem()] * 18,
        out_specs=_vmem(),
        scratch_shapes=[pltpu.VMEM((3 * NB, LN), F32), wide, pltpu.VMEM((4 * FP, LN), F32),
                        pltpu.VMEM((TR, 4 * E), F32)],
    )(flag, base, integ, own, *r1, *r2, nbr_slot, nbr_face, star, flux_own, flux_nbr, stiff_t_st, lift_cat)
    return jnp.transpose(out, (1, 0, 2))


def solution(mesh):
    in_specs = (
        P(None, None, ("grp", "dom")),
        P(None, None, None, ("grp", "dom")),
        P(None, None, None, ("grp", "dom")),
        P(None, None, None, ("grp", "dom")),
        P(),
        P(),
        P(),
        P(None, ("grp", "dom")),
        P(None, ("grp", "dom")),
        P(("grp", "dom")),
    )
    out_specs = P(None, None, ("grp", "dom"))
    return jax.shard_map(local, mesh=mesh, in_specs=in_specs, out_specs=out_specs, check_vma=False)
```

time: 78.9 us -> 71.7 us (0.909)
  starting transfers between devices: 42.5 us -> 40 us
  local copies, waits for them, and re-layouts: 10.8 us -> 9.01 us
  Pallas kernels: 18.5 us -> 17.1 us
    reshape x2 -> x0, local copies, waits for them, and re-layouts: 2.38 us -> none  [the longest x1 1.66 us: local(): return out.reshape(NB, NQ, E)]
    pallas_call x1, Pallas kernels: 6.7 us -> 5.25 us  [local(): pl.pallas_call(_kernel_c, out_shape=field, in_specs=[_smem()] + [_vmem()]...]
    ppermute x2, starting transfers between devices: 13 us -> 12 us  [exchange(): from_ghi = lax.ppermute(g, 'grp', [(i + 1, i) for i in range(n_grp - 1)])]
    ppermute x2, starting transfers between devices: 6.96 us -> 6.01 us  [exchange(): from_glo = lax.ppermute(g, 'grp', [(i, i + 1) for i in range(n_grp - 1)])]
    ppermute x2, waiting for transfers between devices: 5.06 us -> 4.23 us  [exchange(): from_glo = lax.ppermute(g, 'grp', [(i, i + 1) for i in range(n_grp - 1)])]
    unnamed x36 -> x28, local copies, waits for them, and re-layouts: 6.44 us -> 6.32 us
  transfers between devices with their start and end apart: 8 -> 8, of which waited for: 3 -> 2; matrix products, arithmetic and copies ran while one was open for 2% -> 4% of each run, Pallas kernels for 0% -> 0%
where the time goes in v1:
time: 71.7 us; the launch traced here: 71.2 us
  starting transfers between devices  40 us (56%)
  Pallas kernels  17.1 us (24%)
  local copies, waits for them, and re-layouts  9.01 us (13%)
  waiting for transfers between devices  4.9 us (7%)
    ppermute x2, starting transfers between devices, exchange(): from_hi = lax.ppermute(lo, 'dom', [(i + 1, i) for i in range(n_dom - 1)])  18.2 us
    ppermute x2, starting transfers between devices, exchange(): from_ghi = lax.ppermute(g, 'grp', [(i + 1, i) for i in range(n_grp - 1)])  12 us
    pallas_call x1, Pallas kernels, local(): pl.pallas_call(_kernel_a, out_shape=(field, field, table, table, part, pa...  8.66 us
    unnamed x28, local copies, waits for them, and re-layouts  6.32 us
    ppermute x2, starting transfers between devices, exchange(): from_glo = lax.ppermute(g, 'grp', [(i, i + 1) for i in range(n_grp - 1)])  6.01 us
    pallas_call x1, Pallas kernels, local(): pl.pallas_call(_kernel_c, out_shape=field, in_specs=[_smem()] + [_vmem()]...  5.25 us
    ppermute x2, waiting for transfers between devices, exchange(): from_glo = lax.ppermute(g, 'grp', [(i, i + 1) for i in range(n_grp - 1)])  4.23 us
    ppermute x2, starting transfers between devices, exchange(): from_lo = lax.ppermute(hi, 'dom', [(i, i + 1) for i in range(n_dom - 1)])  3.84 us
  transfers between devices with their start and end apart: 8, of which 2 were waited for; matrix products, arithmetic and copies ran while one was open for 4% of the time, Pallas kernels for 0%

profile of v1, /device:TPU:24, one launch (start us, length us, event | category | flops | bytes accessed | tf_op | source)
XLA Modules:
  0.0 71.2 jit_solution(15469683706550089017)
XLA Ops:
  0.0 1.3 %reshape.20.send_ref = s32[1,384]{1,0:T(1,128)} reshape(s32[384]{0:T(512)} %param.19) | data formatting | bytes 3072 | tf_op jit(solution)/shard_map/reshape | solution.py:217
  1.3 1.4 %copy.23.trace_ref = f32[4,21,56]{2,1,0:T(8,128)} copy(f32[4,21,56]{2,0,1:T(4,128)} %param.15) | data formatting | bytes 37632 | tf_op args[5]
  2.7 1.6 %copy.22.star_ref = f32[3,9,9,128]{3,2,1,0:T(8,128)} copy(f32[3,9,9,128]{3,0,2,1:T(4,128)} %param.11) | data formatting | bytes 248832 | tf_op args[1]
  4.3 8.7 %shard_map.100 = (f32[9,56,128]{2,1,0:T(8,128)}, f32[9,56,128]{2,1,0:T(8,128)}, f32[216,512]{1,0:T(8,128)}, f32[216,512]{1,0:T(8,128)}, f32[216,128]{1,0:T(8,128...) custom-call(f32[9,56,128]{2,1,0:T(8,128)} %bitcast.9, ...), custom_call_target="tpu_custom_call" | custom-call | tf_op jit(solution)/shard_map/pallas_call | solution.py:223
  13.0 2.6 %collective-permute-start.3 = (f32[216,128]{1,0:T(8,128)}, f32[216,128]{1,0:T(8,128)S(1)}, u32[]{:S(2)}, u32[]{:S(2)}) collective-permute-start(f32[216,128]{1,0:T(8,128)} %get-tuple-element.30), channel_id=1, source_target_pairs={{64,0},{128,64},{192,128},{256,192},{320,256},{384,320},{448,384},... | collective-permute-start | bytes 331784 | tf_op jit(solution)/shard_map/ppermute | solution.py:207
  15.6 4.1 %collective-permute-start.2 = (f32[216,128]{1,0:T(8,128)}, f32[216,128]{1,0:T(8,128)S(1)}, u32[]{:S(2)}, u32[]{:S(2)}) collective-permute-start(f32[216,128]{1,0:T(8,128)} %get-tuple-element.30), channel_id=1, source_target_pairs={{0,64},{64,128},{128,192},{192,256},{256,320},{320,384},{384,448},... | collective-permute-start | bytes 331784 | tf_op jit(solution)/shard_map/ppermute | solution.py:206
  19.7 1.9 %collective-permute-start = (f32[216,128]{1,0:T(8,128)}, f32[216,128]{1,0:T(8,128)S(1)}, u32[]{:S(2)}, u32[]{:S(2)}) collective-permute-start(f32[216,128]{1,0:T(8,128)} %get-tuple-element.28), channel_id=1, source_target_pairs={{0,1},{1,2},{2,3},{3,4},{4,5},{5,6},{6,7},{7,8},{8,9},{9,10},{10,1... | collective-permute-start | bytes 331784 | tf_op jit(solution)/shard_map/ppermute | solution.py:204
  21.6 11.0 %collective-permute-start.1 = (f32[216,128]{1,0:T(8,128)}, f32[216,128]{1,0:T(8,128)S(1)}, u32[]{:S(2)}, u32[]{:S(2)}) collective-permute-start(f32[216,128]{1,0:T(8,128)} %get-tuple-element.29), channel_id=1, source_target_pairs={{1,0},{2,1},{3,2},{4,3},{5,4},{6,5},{7,6},{8,7},{9,8},{10,9},{11,1... | collective-permute-start | bytes 331784 | tf_op jit(solution)/shard_map/ppermute | solution.py:205
  32.7 0.7 copy.29.lift_ref
  33.3 0.2 copy-done
  33.5 0.7 %copy.24 = f32[3,56,56]{2,1,0:T(8,128)} copy(f32[3,56,56]{1,2,0:T(8,128)S(1)} %bitcast.15) | data formatting | bytes 75264 | tf_op jit(solution)/shard_map/transpose | solution.py:215
  34.2 0.7 %copy.27.fo_ref = f32[4,9,9,128]{3,2,1,0:T(8,128)} copy(f32[4,9,9,128]{3,0,2,1:T(4,128)S(1)} %copy-done.5) | data formatting | bytes 331776 | tf_op args[2]
  35.0 0.3 copy-done.6
  35.2 0.8 %copy.28.fn_ref = f32[4,9,9,128]{3,2,1,0:T(8,128)} copy(f32[4,9,9,128]{3,0,2,1:T(4,128)S(1)} %copy-done.6) | data formatting | bytes 331776 | tf_op args[3]
  36.1 0.6 copy-done.3
  36.8 3.2 %shard_map.101 = (f32[9,56,128]{2,1,0:T(8,128)}, f32[9,56,128]{2,1,0:T(8,128)}, f32[216,512]{1,0:T(8,128)}, f32[216,128]{1,0:T(8,128)}, f32[216,128]{1,0:T(8,128)}, /*index=5*/f32[216,128]{1,0:T(8,128)}) custom-call(s32[1]{0:T(128)} %bitcast.flag_ref, f32[9,56,128]{2,1,0:T(8,128)} %bitcast.10, f32[9,56,128]{2,1,0:T(8,128)} %get-tuple-element.21.first_ref, ...), custom_call_target="tpu_custom_call" | custom-call | tf_op jit(solution)/shard_map/pallas_call | solution.py:234
  39.9 1.9 %collective-permute-start.4 = (f32[216,128]{1,0:T(8,128)}, f32[216,128]{1,0:T(8,128)S(1)}, u32[]{:S(2)}, u32[]{:S(2)}) collective-permute-start(f32[216,128]{1,0:T(8,128)} %get-tuple-element.34), channel_id=1, source_target_pairs={{0,1},{1,2},{2,3},{3,4},{4,5},{5,6},{6,7},{7,8},{8,9},{9,10},{10,1... | collective-permute-start | bytes 331784 | tf_op jit(solution)/shard_map/ppermute | solution.py:204
  41.8 7.3 %collective-permute-start.5 = (f32[216,128]{1,0:T(8,128)}, f32[216,128]{1,0:T(8,128)S(1)}, u32[]{:S(2)}, u32[]{:S(2)}) collective-permute-start(f32[216,128]{1,0:T(8,128)} %get-tuple-element.35), channel_id=1, source_target_pairs={{1,0},{2,1},{3,2},{4,3},{5,4},{6,5},{7,6},{8,7},{9,8},{10,9},{11,1... | collective-permute-start | bytes 331784 | tf_op jit(solution)/shard_map/ppermute | solution.py:205
  49.1 9.3 %collective-permute-start.7 = (f32[216,128]{1,0:T(8,128)}, f32[216,128]{1,0:T(8,128)S(1)}, u32[]{:S(2)}, u32[]{:S(2)}) collective-permute-start(f32[216,128]{1,0:T(8,128)} %get-tuple-element.36), channel_id=1, source_target_pairs={{64,0},{128,64},{192,128},{256,192},{320,256},{384,320},{448,384},... | collective-permute-start | bytes 331784 | tf_op jit(solution)/shard_map/ppermute | solution.py:207
  58.4 1.9 %collective-permute-start.6 = (f32[216,128]{1,0:T(8,128)}, f32[216,128]{1,0:T(8,128)S(1)}, u32[]{:S(2)}, u32[]{:S(2)}) collective-permute-start(f32[216,128]{1,0:T(8,128)} %get-tuple-element.36), channel_id=1, source_target_pairs={{0,64},{64,128},{128,192},{192,256},{256,320},{320,384},{384,448},... | collective-permute-start | bytes 331784 | tf_op jit(solution)/shard_map/ppermute | solution.py:206
  60.4 0.7 collective-permute-done.7.r2ghi
  61.1 4.2 %collective-permute-done.6.r2glo = f32[216,128]{1,0:T(8,128)S(1)} collective-permute-done((f32[216,128]{1,0:T(8,128)}, f32[216,128]{1,0:T(8,128)S(1)}, u32[]{:S(2)}, u32[]{:S(2)}) %collective-permute-start.6) | collective-permute-done | bytes 110624 | tf_op jit(solution)/shard_map/ppermute | solution.py:206
  65.3 0.6 copy-done.10
  65.9 5.2 %shard_map.102 = f32[9,56,128]{2,1,0:T(8,128)} custom-call(s32[1]{0:T(128)} %bitcast.flag_ref, f32[9,56,128]{2,1,0:T(8,128)} %get-tuple-element.31.base_ref, f32[9,56,128]{2,1,0:T(8,128)} %get-tuple-element.32.integ_ref, f32[216,512]{1,0:T(8,128)} %get-tuple-element.33.own_ref, f32[216,128]{1,0:T(8,128)} %copy-done.3, f32[216,128]{1,0:T(8,128)} %copy-done.4, ...), custom_call_target="tpu_custom_call" | custom-call | tf_op jit(solution)/shard_map/pallas_call | solution.py:247
  (28 shorter events, 0.2 us)
Async XLA Ops:
  4.3 28.3 %copy-start.11 = (f32[4,56,21]{1,0,2:T(4,128)S(1)}, f32[4,56,21]{1,0,2:T(4,128)}, u32[]{:S(2)}) copy-start(f32[4,56,21]{1,0,2:T(4,128)} %param.16) | copy-start | bytes 56452
  13.0 23.1 %collective-permute-start.3 = (f32[216,128]{1,0:T(8,128)}, f32[216,128]{1,0:T(8,128)S(1)}, u32[]{:S(2)}, u32[]{:S(2)}) collective-permute-start(f32[216,128]{1,0:T(8,128)} %get-tuple-element.30), channel_id=1, source_target_pairs={{64,0},{128,64},{192,128},{256,192},{320,256},{384,320},{448,384},... | collective-permute-start | bytes 331784 | tf_op jit(solution)/shard_map/ppermute | solution.py:207
  15.6 20.4 %collective-permute-start.2 = (f32[216,128]{1,0:T(8,128)}, f32[216,128]{1,0:T(8,128)S(1)}, u32[]{:S(2)}, u32[]{:S(2)}) collective-permute-start(f32[216,128]{1,0:T(8,128)} %get-tuple-element.30), channel_id=1, source_target_pairs={{0,64},{64,128},{128,192},{192,256},{256,320},{320,384},{384,448},... | collective-permute-start | bytes 331784 | tf_op jit(solution)/shard_map/ppermute | solution.py:206
  19.7 16.3 %collective-permute-start = (f32[216,128]{1,0:T(8,128)}, f32[216,128]{1,0:T(8,128)S(1)}, u32[]{:S(2)}, u32[]{:S(2)}) collective-permute-start(f32[216,128]{1,0:T(8,128)} %get-tuple-element.28), channel_id=1, source_target_pairs={{0,1},{1,2},{2,3},{3,4},{4,5},{5,6},{6,7},{7,8},{8,9},{9,10},{10,1... | collective-permute-start | bytes 331784 | tf_op jit(solution)/shard_map/ppermute | solution.py:204
  21.6 14.4 %collective-permute-start.1 = (f32[216,128]{1,0:T(8,128)}, f32[216,128]{1,0:T(8,128)S(1)}, u32[]{:S(2)}, u32[]{:S(2)}) collective-permute-start(f32[216,128]{1,0:T(8,128)} %get-tuple-element.29), channel_id=1, source_target_pairs={{1,0},{2,1},{3,2},{4,3},{5,4},{6,5},{7,6},{8,7},{9,8},{10,9},{11,1... | collective-permute-start | bytes 331784 | tf_op jit(solution)/shard_map/ppermute | solution.py:205
  32.6 0.9 %copy-start = (f32[3,56,56]{2,1,0:T(8,128)S(1)}, f32[3,56,56]{2,1,0:T(8,128)}, u32[]{:S(2)}) copy-start(f32[3,56,56]{2,1,0:T(8,128)} %param.14) | copy-start | bytes 112900
  32.6 1.6 %copy-start.5 = (f32[4,9,9,128]{3,0,2,1:T(4,128)S(1)}, f32[4,9,9,128]{3,0,2,1:T(4,128)}, u32[]{:S(2)}) copy-start(f32[4,9,9,128]{3,0,2,1:T(4,128)} %param.12) | copy-start | bytes 497668
  34.2 1.0 %copy-start.6 = (f32[4,9,9,128]{3,0,2,1:T(4,128)S(1)}, f32[4,9,9,128]{3,0,2,1:T(4,128)}, u32[]{:S(2)}) copy-start(f32[4,9,9,128]{3,0,2,1:T(4,128)} %param.13) | copy-start | bytes 497668
  36.0 0.6 copy-start.3
  36.0 0.7 copy-start.4
  36.0 0.7 copy-start.1
  36.0 0.7 %copy-start.2 = (f32[216,128]{1,0:T(8,128)}, f32[216,128]{1,0:T(8,128)S(1)}, u32[]{:S(2)}) copy-start(f32[216,128]{1,0:T(8,128)S(1)} %collective-permute-done.2.r1glo) | copy-start | bytes 331780
  39.9 20.5 %collective-permute-start.4 = (f32[216,128]{1,0:T(8,128)}, f32[216,128]{1,0:T(8,128)S(1)}, u32[]{:S(2)}, u32[]{:S(2)}) collective-permute-start(f32[216,128]{1,0:T(8,128)} %get-tuple-element.34), channel_id=1, source_target_pairs={{0,1},{1,2},{2,3},{3,4},{4,5},{5,6},{6,7},{7,8},{8,9},{9,10},{10,1... | collective-permute-start | bytes 331784 | tf_op jit(solution)/shard_map/ppermute | solution.py:204
  41.8 18.6 %collective-permute-start.5 = (f32[216,128]{1,0:T(8,128)}, f32[216,128]{1,0:T(8,128)S(1)}, u32[]{:S(2)}, u32[]{:S(2)}) collective-permute-start(f32[216,128]{1,0:T(8,128)} %get-tuple-element.35), channel_id=1, source_target_pairs={{1,0},{2,1},{3,2},{4,3},{5,4},{6,5},{7,6},{8,7},{9,8},{10,9},{11,1... | collective-permute-start | bytes 331784 | tf_op jit(solution)/shard_map/ppermute | solution.py:205
  49.1 12.0 %collective-permute-start.7 = (f32[216,128]{1,0:T(8,128)}, f32[216,128]{1,0:T(8,128)S(1)}, u32[]{:S(2)}, u32[]{:S(2)}) collective-permute-start(f32[216,128]{1,0:T(8,128)} %get-tuple-element.36), channel_id=1, source_target_pairs={{64,0},{128,64},{192,128},{256,192},{320,256},{384,320},{448,384},... | collective-permute-start | bytes 331784 | tf_op jit(solution)/shard_map/ppermute | solution.py:207
  58.4 6.9 %collective-permute-start.6 = (f32[216,128]{1,0:T(8,128)}, f32[216,128]{1,0:T(8,128)S(1)}, u32[]{:S(2)}, u32[]{:S(2)}) collective-permute-start(f32[216,128]{1,0:T(8,128)} %get-tuple-element.36), channel_id=1, source_target_pairs={{0,64},{64,128},{128,192},{192,256},{256,320},{320,384},{384,448},... | collective-permute-start | bytes 331784 | tf_op jit(solution)/shard_map/ppermute | solution.py:206
  60.4 4.9 %copy-start.7 = (f32[216,128]{1,0:T(8,128)}, f32[216,128]{1,0:T(8,128)S(1)}, u32[]{:S(2)}) copy-start(f32[216,128]{1,0:T(8,128)S(1)} %collective-permute-done.4.r2lo) | copy-start | bytes 331780
  60.4 4.9 %copy-start.8 = (f32[216,128]{1,0:T(8,128)}, f32[216,128]{1,0:T(8,128)S(1)}, u32[]{:S(2)}) copy-start(f32[216,128]{1,0:T(8,128)S(1)} %collective-permute-done.5.r2hi) | copy-start | bytes 331780
  61.1 4.2 %copy-start.9 = (f32[216,128]{1,0:T(8,128)}, f32[216,128]{1,0:T(8,128)S(1)}, u32[]{:S(2)}) copy-start(f32[216,128]{1,0:T(8,128)S(1)} %collective-permute-done.7.r2ghi) | copy-start | bytes 331780
  65.3 0.7 copy-start.10

commit v2 on v1

--- a/solution.py
+++ b/solution.py
@@ -38,6 +38,18 @@
     return _bdot(a[0], b[0]) + (_bdot(a[0], b[1]) + _bdot(a[1], b[0]))
 
 
+def _tdot(a, b):
+    return lax.dot_general(a, b, (((0,), (0,)), ((), ())), preferred_element_type=F32)
+
+
+def _dot3_t(a, b):
+    return _tdot(a[0], b[0]) + (_tdot(a[0], b[1]) + _tdot(a[1], b[0]))
+
+
+def _rows84(ref):
+    return jnp.concatenate([ref[r] for r in range(NF)], axis=0)
+
+
 def _split3(x):
     hi = x.astype(BF)
     r = x - hi.astype(F32)
@@ -61,9 +73,10 @@
 def _mix_vol(a_ref, star_ref, out_ref, sign):
     for q in range(NQ):
         acc = None
-        for d in range(3):
-            for p in range(NQ):
-                t = a_ref[d * NB:(d + 1) * NB, p * E:(p + 1) * E] * star_ref[d, p, q:q + 1, :]
+        for p in range(NQ):
+            srow = star_ref[p, q]
+            for d in range(3):
+                t = a_ref[d * NB:(d + 1) * NB, p * E:(p + 1) * E] * srow[d:d + 1, :]
                 acc = t if acc is None else acc + t
         out_ref[:, q * E:(q + 1) * E] = acc if sign > 0 else -acc
 
@@ -80,13 +93,14 @@
             ref[...] = ref[...] + w[k + 1] * dn
 
 
-def _table(x, trace_ref, t_ref):
-    xp = _split2(x)
+def _table(x, trace_p, yt_ref, t_ref):
+    yt = _dot3(trace_p, _split2(x))
+    for p in range(NQ):
+        yt_ref[p] = yt[:, p * E:(p + 1) * E]
     t_ref[...] = jnp.zeros(t_ref.shape, F32)
     for f in range(4):
-        yt = _dot3(_split2(trace_ref[f]), xp)
         for p in range(NQ):
-            t_ref[p * FP:p * FP + NF, f * E:(f + 1) * E] = yt[:, p * E:(p + 1) * E]
+            t_ref[p * FP:p * FP + NF, f * E:(f + 1) * E] = yt_ref[p, pl.ds(f, NF, stride=4), :]
 
 
 def _send(tables, send_ref, outs):
@@ -112,41 +126,56 @@
         g_ref[:, f * E:(f + 1) * E] = _sel(parts, onehot)
 
 
-def _update(b, x, s_ref, g_ref, star_ref, fo_ref, fn_ref, stiff_t_p, lift_p, a_ref, v_ref, yf_ref):
-    a_ref[...] = _dot3(stiff_t_p, _split2(x))
+def _lift_parts(lift_ref, lt_ref):
+    lt_ref[:, 0:NB] = _rows84(lift_ref)
+    return [_split2(lt_ref[pl.ds(f, NF, stride=4), 0:NB]) for f in range(4)]
+
+
+def _update(b, x, s_ref, g_ref, star_ref, fo_ref, fn_ref, stiff_ref, lift_p, a_ref, v_ref, yf_ref):
+    xp = _split2(x)
+    for d in range(3):
+        a_ref[d * NB:(d + 1) * NB, :] = _dot3_t(_split2(stiff_ref[d]), xp)
     _mix_vol(a_ref, star_ref, v_ref, 1)
+    for q in range(NQ):
+        accs = [None] * 4
+        for p in range(NQ):
+            orow = fo_ref[p, q]
+            nrow = fn_ref[p, q]
+            for f in range(4):
+                t = (s_ref[p * FP:(p + 1) * FP, f * E:(f + 1) * E] * orow[f:f + 1, :]
+                     + g_ref[p * FP:(p + 1) * FP, f * E:(f + 1) * E] * nrow[f:f + 1, :])
+                accs[f] = t if accs[f] is None else accs[f] + t
+        for f in range(4):
+            yf_ref[f * FP:(f + 1) * FP, q * E:(q + 1) * E] = accs[f]
+    ftot = None
     for f in range(4):
-        for q in range(NQ):
-            acc = None
-            for p in range(NQ):
-                t = (s_ref[p * FP:(p + 1) * FP, f * E:(f + 1) * E] * fo_ref[f, p, q:q + 1, :]
-                     + g_ref[p * FP:(p + 1) * FP, f * E:(f + 1) * E] * fn_ref[f, p, q:q + 1, :])
-                acc = t if acc is None else acc + t
-            yf_ref[f * FP:(f + 1) * FP, q * E:(q + 1) * E] = acc
-    ftot = _dot3(lift_p, _split2(yf_ref[...]))
+        t = _dot3_t(lift_p[f], _split2(yf_ref[f * FP:f * FP + NF, :]))
+        ftot = t if ftot is None else ftot + t
     return (b + v_ref[...]) - ftot
 
 
 def _kernel_a(x_ref, star_ref, stiff_ref, trace_ref, send_ref,
               first_ref, fl_ref, t1_ref, t1l_ref, s1lo, s1hi, s1g, sllo, slhi, slg,
-              d_ref, a_ref, acc1_ref, acc2_ref, tl_ref):
+              d_ref, a_ref, acc1_ref, acc2_ref, tl_ref, yt_ref):
     x = _load_field(x_ref)
-    _taylor(x, star_ref, _split2(stiff_ref[...]), d_ref, a_ref, [(acc1_ref, W_FIRST), (acc2_ref, W_LATER)])
+    stiff_st = jnp.concatenate([stiff_ref[d] for d in range(3)], axis=0)
+    _taylor(x, star_ref, _split2(stiff_st), d_ref, a_ref, [(acc1_ref, W_FIRST), (acc2_ref, W_LATER)])
     first = acc1_ref[...]
     later = acc2_ref[...]
     _store_field(first_ref, first)
     _store_field(fl_ref, first + later)
-    _table(first, trace_ref, t1_ref)
-    _table(later, trace_ref, tl_ref)
+    trace_p = _split2(_rows84(trace_ref))
+    _table(first, trace_p, yt_ref, t1_ref)
+    _table(later, trace_p, yt_ref, tl_ref)
     t1l_ref[...] = t1_ref[...] + tl_ref[...]
     _send([t1_ref[...], tl_ref[...]], send_ref, [(s1lo, s1hi, s1g), (sllo, slhi, slg)])
 
 
 def _kernel_b(flag_ref, x_ref, first_ref, fl_ref, t1_ref, t1l_ref, sllo, slhi, slg,
               r1lo, r1hi, r1glo, r1ghi, slot_ref, face_ref, star_ref, fo_ref, fn_ref,
-              stiff_ref, stiff_t_ref, lift_ref, trace_ref, send_ref,
+              stiff_ref, lift_ref, trace_ref, send_ref,
               base_ref, integ_ref, own_ref, s2lo, s2hi, s2g,
-              d_ref, a_ref, v_ref, yf_ref, g_ref, acc_ref):
+              d_ref, a_ref, v_ref, yf_ref, g_ref, acc_ref, yt_ref, lt_ref):
     fault = flag_ref[0] == 1
 
     @pl.when(fault)
@@ -154,12 +183,13 @@
         comb = jnp.concatenate([t1_ref[...], r1lo[...], r1hi[...], r1glo[...], r1ghi[...]], axis=1)
         _gather(comb, slot_ref, face_ref, g_ref)
         mid = _update(_load_field(x_ref), _load_field(first_ref), t1_ref, g_ref, star_ref, fo_ref, fn_ref,
-                      _split2(stiff_t_ref[...]), _split2(lift_ref[...]), a_ref, v_ref, yf_ref)
+                      stiff_ref, _lift_parts(lift_ref, lt_ref), a_ref, v_ref, yf_ref)
         _store_field(base_ref, mid)
-        _taylor(mid, star_ref, _split2(stiff_ref[...]), d_ref, a_ref, [(acc_ref, W_FIRST)])
+        stiff_st = jnp.concatenate([stiff_ref[d] for d in range(3)], axis=0)
+        _taylor(mid, star_ref, _split2(stiff_st), d_ref, a_ref, [(acc_ref, W_FIRST)])
         second = acc_ref[...]
         _store_field(integ_ref, second)
-        _table(second, trace_ref, own_ref)
+        _table(second, _split2(_rows84(trace_ref)), yt_ref, own_ref)
         _send([own_ref[...]], send_ref, [(s2lo, s2hi, s2g)])
 
     @pl.when(jnp.logical_not(fault))
@@ -174,15 +204,15 @@
 
 def _kernel_c(flag_ref, base_ref, integ_ref, own_ref, r1lo, r1hi, r1glo, r1ghi,
               r2lo, r2hi, r2glo, r2ghi, slot_ref, face_ref, star_ref, fo_ref, fn_ref,
-              stiff_t_ref, lift_ref,
-              out_ref, a_ref, v_ref, yf_ref, g_ref):
+              stiff_ref, lift_ref,
+              out_ref, a_ref, v_ref, yf_ref, g_ref, lt_ref):
     keep = (1 - flag_ref[0]).astype(F32)
     comb = jnp.concatenate(
         [own_ref[...], r2lo[...] + keep * r1lo[...], r2hi[...] + keep * r1hi[...],
          r2glo[...] + keep * r1glo[...], r2ghi[...] + keep * r1ghi[...]], axis=1)
     _gather(comb, slot_ref, face_ref, g_ref)
     out = _update(_load_field(base_ref), _load_field(integ_ref), own_ref, g_ref, star_ref, fo_ref, fn_ref,
-                  _split2(stiff_t_ref[...]), _split2(lift_ref[...]), a_ref, v_ref, yf_ref)
+                  stiff_ref, _lift_parts(lift_ref, lt_ref), a_ref, v_ref, yf_ref)
     _store_field(out_ref, out)
 
 
@@ -211,9 +241,11 @@
 def local(state, star, flux_own, flux_nbr, stiff, trace, lift, nbr_slot, nbr_face, send_slot):
     flag = (lax.axis_index("grp") == 0).astype(jnp.int32).reshape(1)
     x0 = jnp.transpose(state, (1, 0, 2))
-    stiff_st = stiff.reshape(3 * NB, NB)
-    stiff_t_st = jnp.transpose(stiff, (0, 2, 1)).reshape(3 * NB, NB)
-    lift_cat = jnp.transpose(jnp.pad(lift, ((0, 0), (0, 0), (0, FP - NF))), (1, 0, 2)).reshape(NB, 4 * FP)
+    star = jnp.transpose(star, (1, 2, 0, 3))
+    flux_own = jnp.transpose(flux_own, (1, 2, 0, 3))
+    flux_nbr = jnp.transpose(flux_nbr, (1, 2, 0, 3))
+    trace = jnp.transpose(trace, (1, 0, 2))
+    lift = jnp.transpose(lift, (2, 0, 1))
     send = send_slot.reshape(1, 3 * E)
 
     field = _sds((NQ, NB, E))
@@ -225,8 +257,9 @@
         out_shape=(field, field, table, table, part, part, part, part, part, part),
         in_specs=[_vmem()] * 5,
         out_specs=tuple([_vmem()] * 10),
-        scratch_shapes=[wide, pltpu.VMEM((3 * NB, LN), F32), wide, wide, pltpu.VMEM((TR, 4 * E), F32)],
-    )(x0, star, stiff_st, trace, send)
+        scratch_shapes=[wide, pltpu.VMEM((3 * NB, LN), F32), wide, wide, pltpu.VMEM((TR, 4 * E), F32),
+                        pltpu.VMEM((NQ, 4 * NF, E), F32)],
+    )(x0, star, stiff, trace, send)
     first, fl, t1, t1l, s1lo, s1hi, s1g, sllo, slhi, slg = outs_a
 
     r1 = exchange(s1lo, s1hi, s1g)
@@ -234,12 +267,13 @@
     outs_b = pl.pallas_call(
         _kernel_b,
         out_shape=(field, field, table, part, part, part),
-        in_specs=[_smem()] + [_vmem()] * 22,
+        in_specs=[_smem()] + [_vmem()] * 21,
         out_specs=tuple([_vmem()] * 6),
         scratch_shapes=[wide, pltpu.VMEM((3 * NB, LN), F32), wide, pltpu.VMEM((4 * FP, LN), F32),
-                        pltpu.VMEM((TR, 4 * E), F32), wide],
+                        pltpu.VMEM((TR, 4 * E), F32), wide, pltpu.VMEM((NQ, 4 * NF, E), F32),
+                        pltpu.VMEM((4 * NF, E), F32)],
     )(flag, x0, first, fl, t1, t1l, sllo, slhi, slg, *r1, nbr_slot, nbr_face, star, flux_own, flux_nbr,
-      stiff_st, stiff_t_st, lift_cat, trace, send)
+      stiff, lift, trace, send)
     base, integ, own, s2lo, s2hi, s2g = outs_b
 
     r2 = exchange(s2lo, s2hi, s2g)
@@ -250,8 +284,8 @@
         in_specs=[_smem()] + [_vmem()] * 18,
         out_specs=_vmem(),
         scratch_shapes=[pltpu.VMEM((3 * NB, LN), F32), wide, pltpu.VMEM((4 * FP, LN), F32),
-                        pltpu.VMEM((TR, 4 * E), F32)],
-    )(flag, base, integ, own, *r1, *r2, nbr_slot, nbr_face, star, flux_own, flux_nbr, stiff_t_st, lift_cat)
+                        pltpu.VMEM((TR, 4 * E), F32), pltpu.VMEM((4 * NF, E), F32)],
+    )(flag, base, integ, own, *r1, *r2, nbr_slot, nbr_face, star, flux_own, flux_nbr, stiff, lift)
     return jnp.transpose(out, (1, 0, 2))
 
 

time: 71.7 us -> 68.1 us (0.950)
  local copies, waits for them, and re-layouts: 9.01 us -> 2.5 us
  waiting for transfers between devices: 4.9 us -> 7.46 us
  starting transfers between devices: 40 us -> 40.9 us
    unnamed x28 -> x16, local copies, waits for them, and re-layouts: 6.32 us -> 1.29 us
    ppermute x2, waiting for transfers between devices: 4.23 us -> 5.84 us  [exchange(): from_glo = lax.ppermute(g, 'grp', [(i, i + 1) for i in range(n_grp - 1)])]
    ppermute x2, waiting for transfers between devices: 0.66 us -> 1.61 us  [exchange(): from_ghi = lax.ppermute(g, 'grp', [(i + 1, i) for i in range(n_grp - 1)])]
    transpose x3 -> x0, local copies, waits for them, and re-layouts: 0.74 us -> none  [the longest x1 0.72 us: local(): stiff_t_st = jnp.transpose(stiff, (0, 2, 1)).reshape(3 * NB, NB)]
    ppermute x2, starting transfers between devices: 6.01 us -> 6.74 us  [exchange(): from_glo = lax.ppermute(g, 'grp', [(i, i + 1) for i in range(n_grp - 1)])]
  transfers between devices with their start and end apart: 8 -> 8, of which waited for: 2 -> 4; matrix products, arithmetic and copies ran while one was open for 4% -> 0% of each run, Pallas kernels for 0% -> 0%
where the time goes in v2:
time: 68.1 us; the launch traced here: 67.7 us
  starting transfers between devices  40.9 us (60%)
  Pallas kernels  16.7 us (25%)
  waiting for transfers between devices  7.46 us (11%)
  local copies, waits for them, and re-layouts  2.5 us (4%)
    ppermute x2, starting transfers between devices, exchange(): from_hi = lax.ppermute(lo, 'dom', [(i + 1, i) for i in range(n_dom - 1)])  18.8 us
    ppermute x2, starting transfers between devices, exchange(): from_ghi = lax.ppermute(g, 'grp', [(i + 1, i) for i in range(n_grp - 1)])  11.6 us
    pallas_call x1, Pallas kernels, local(): pl.pallas_call(_kernel_a, out_shape=(field, field, table, table, part, pa...  8.26 us
    ppermute x2, starting transfers between devices, exchange(): from_glo = lax.ppermute(g, 'grp', [(i, i + 1) for i in range(n_grp - 1)])  6.74 us
    ppermute x2, waiting for transfers between devices, exchange(): from_glo = lax.ppermute(g, 'grp', [(i, i + 1) for i in range(n_grp - 1)])  5.84 us
    pallas_call x1, Pallas kernels, local(): pl.pallas_call(_kernel_c, out_shape=field, in_specs=[_smem()] + [_vmem()]...  5.41 us
    ppermute x2, starting transfers between devices, exchange(): from_lo = lax.ppermute(hi, 'dom', [(i, i + 1) for i in range(n_dom - 1)])  3.82 us
    pallas_call x1, Pallas kernels, local(): pl.pallas_call(_kernel_b, out_shape=(field, field, table, part, part, par...  3.02 us
  transfers between devices with their start and end apart: 8, of which 4 were waited for; matrix products, arithmetic and copies ran while one was open for 0% of the time, Pallas kernels for 0%

profile of v2, /device:TPU:24, one launch (start us, length us, event | category | flops | bytes accessed | tf_op | source)
XLA Modules:
  0.0 67.7 jit_solution(12481583986385908007)
XLA Ops:
  0.0 1.2 %reshape.10.send_ref = s32[1,384]{1,0:T(1,128)} reshape(s32[384]{0:T(512)} %param.19) | data formatting | bytes 3072 | tf_op jit(solution)/shard_map/reshape | solution.py:249
  1.2 8.3 %shard_map.100 = (f32[9,56,128]{2,1,0:T(8,128)}, f32[9,56,128]{2,1,0:T(8,128)}, f32[216,512]{1,0:T(8,128)}, f32[216,512]{1,0:T(8,128)}, f32[216,128]{1,0:T(8,128...) custom-call(f32[9,56,128]{2,1,0:T(8,128)} %bitcast.11, ...), custom_call_target="tpu_custom_call" | custom-call | tf_op jit(solution)/shard_map/pallas_call | solution.py:255
  9.5 1.9 %collective-permute-start = (f32[216,128]{1,0:T(8,128)}, f32[216,128]{1,0:T(8,128)S(1)}, u32[]{:S(2)}, u32[]{:S(2)}) collective-permute-start(f32[216,128]{1,0:T(8,128)} %get-tuple-element.28), channel_id=1, source_target_pairs={{0,1},{1,2},{2,3},{3,4},{4,5},{5,6},{6,7},{7,8},{8,9},{9,10},{10,1... | collective-permute-start | bytes 331784 | tf_op jit(solution)/shard_map/ppermute | solution.py:234
  11.4 11.5 %collective-permute-start.1 = (f32[216,128]{1,0:T(8,128)}, f32[216,128]{1,0:T(8,128)S(1)}, u32[]{:S(2)}, u32[]{:S(2)}) collective-permute-start(f32[216,128]{1,0:T(8,128)} %get-tuple-element.29), channel_id=1, source_target_pairs={{1,0},{2,1},{3,2},{4,3},{5,4},{6,5},{7,6},{8,7},{9,8},{10,9},{11,1... | collective-permute-start | bytes 331784 | tf_op jit(solution)/shard_map/ppermute | solution.py:235
  22.9 1.9 %collective-permute-start.3 = (f32[216,128]{1,0:T(8,128)}, f32[216,128]{1,0:T(8,128)S(1)}, u32[]{:S(2)}, u32[]{:S(2)}) collective-permute-start(f32[216,128]{1,0:T(8,128)} %get-tuple-element.30), channel_id=1, source_target_pairs={{64,0},{128,64},{192,128},{256,192},{320,256},{384,320},{448,384},... | collective-permute-start | bytes 331784 | tf_op jit(solution)/shard_map/ppermute | solution.py:237
  24.8 4.8 %collective-permute-start.2 = (f32[216,128]{1,0:T(8,128)}, f32[216,128]{1,0:T(8,128)S(1)}, u32[]{:S(2)}, u32[]{:S(2)}) collective-permute-start(f32[216,128]{1,0:T(8,128)} %get-tuple-element.30), channel_id=1, source_target_pairs={{0,64},{64,128},{128,192},{192,256},{256,320},{320,384},{384,448},... | collective-permute-start | bytes 331784 | tf_op jit(solution)/shard_map/ppermute | solution.py:236
  29.7 0.0 collective-permute-done.r1lo
  29.7 0.0 collective-permute-done.1.r1hi
  29.7 0.0 copy-start.1
  29.7 1.0 %collective-permute-done.3.r1ghi = f32[216,128]{1,0:T(8,128)S(1)} collective-permute-done((f32[216,128]{1,0:T(8,128)}, f32[216,128]{1,0:T(8,128)S(1)}, u32[]{:S(2)}, u32[]{:S(2)}) %collective-permute-start.3) | collective-permute-done | bytes 110624 | tf_op jit(solution)/shard_map/ppermute | solution.py:237
  30.7 1.6 %collective-permute-done.2.r1glo = f32[216,128]{1,0:T(8,128)S(1)} collective-permute-done((f32[216,128]{1,0:T(8,128)}, f32[216,128]{1,0:T(8,128)S(1)}, u32[]{:S(2)}, u32[]{:S(2)}) %collective-permute-start.2) | collective-permute-done | bytes 110624 | tf_op jit(solution)/shard_map/ppermute | solution.py:236
  32.3 0.0 copy-done.1
  32.3 0.6 copy-done.3
  32.9 3.0 %shard_map.101 = (f32[9,56,128]{2,1,0:T(8,128)}, f32[9,56,128]{2,1,0:T(8,128)}, f32[216,512]{1,0:T(8,128)}, f32[216,128]{1,0:T(8,128)}, f32[216,128]{1,0:T(8,128)}, /*index=5*/f32[216,128]{1,0:T(8,128)}) custom-call(s32[1]{0:T(128)} %bitcast.flag_ref, f32[9,56,128]{2,1,0:T(8,128)} %bitcast.12, f32[9,56,128]{2,1,0:T(8,128)} %get-tuple-element.21.first_ref, ...), custom_call_target="tpu_custom_call" | custom-call | tf_op jit(solution)/shard_map/pallas_call | solution.py:267
  35.9 1.9 %collective-permute-start.4 = (f32[216,128]{1,0:T(8,128)}, f32[216,128]{1,0:T(8,128)S(1)}, u32[]{:S(2)}, u32[]{:S(2)}) collective-permute-start(f32[216,128]{1,0:T(8,128)} %get-tuple-element.34), channel_id=1, source_target_pairs={{0,1},{1,2},{2,3},{3,4},{4,5},{5,6},{6,7},{7,8},{8,9},{9,10},{10,1... | collective-permute-start | bytes 331784 | tf_op jit(solution)/shard_map/ppermute | solution.py:234
  37.9 7.3 %collective-permute-start.5 = (f32[216,128]{1,0:T(8,128)}, f32[216,128]{1,0:T(8,128)S(1)}, u32[]{:S(2)}, u32[]{:S(2)}) collective-permute-start(f32[216,128]{1,0:T(8,128)} %get-tuple-element.35), channel_id=1, source_target_pairs={{1,0},{2,1},{3,2},{4,3},{5,4},{6,5},{7,6},{8,7},{9,8},{10,9},{11,1... | collective-permute-start | bytes 331784 | tf_op jit(solution)/shard_map/ppermute | solution.py:235
  45.1 9.6 %collective-permute-start.7 = (f32[216,128]{1,0:T(8,128)}, f32[216,128]{1,0:T(8,128)S(1)}, u32[]{:S(2)}, u32[]{:S(2)}) collective-permute-start(f32[216,128]{1,0:T(8,128)} %get-tuple-element.36), channel_id=1, source_target_pairs={{64,0},{128,64},{192,128},{256,192},{320,256},{384,320},{448,384},... | collective-permute-start | bytes 331784 | tf_op jit(solution)/shard_map/ppermute | solution.py:237
  54.8 1.9 %collective-permute-start.6 = (f32[216,128]{1,0:T(8,128)}, f32[216,128]{1,0:T(8,128)S(1)}, u32[]{:S(2)}, u32[]{:S(2)}) collective-permute-start(f32[216,128]{1,0:T(8,128)} %get-tuple-element.36), channel_id=1, source_target_pairs={{0,64},{64,128},{128,192},{192,256},{256,320},{320,384},{384,448},... | collective-permute-start | bytes 331784 | tf_op jit(solution)/shard_map/ppermute | solution.py:236
  56.7 0.0 collective-permute-done.4.r2lo
  56.7 0.0 collective-permute-done.5.r2hi
  56.8 0.7 collective-permute-done.7.r2ghi
  57.4 4.2 %collective-permute-done.6.r2glo = f32[216,128]{1,0:T(8,128)S(1)} collective-permute-done((f32[216,128]{1,0:T(8,128)}, f32[216,128]{1,0:T(8,128)S(1)}, u32[]{:S(2)}, u32[]{:S(2)}) %collective-permute-start.6) | collective-permute-done | bytes 110624 | tf_op jit(solution)/shard_map/ppermute | solution.py:236
  61.6 0.6 copy-done.7
  62.3 5.4 %shard_map.102 = f32[9,56,128]{2,1,0:T(8,128)} custom-call(s32[1]{0:T(128)} %bitcast.flag_ref, f32[9,56,128]{2,1,0:T(8,128)} %get-tuple-element.31.base_ref, f32[9,56,128]{2,1,0:T(8,128)} %get-tuple-element.32.integ_ref, f32[216,512]{1,0:T(8,128)} %get-tuple-element.33.own_ref, f32[216,128]{1,0:T(8,128)} %copy-done, f32[216,128]{1,0:T(8,128)} %copy-done.1, ...), custom_call_target="tpu_custom_call" | custom-call | tf_op jit(solution)/shard_map/pallas_call | solution.py:281
  (12 shorter events, 0.0 us)
Async XLA Ops:
  9.5 20.2 %collective-permute-start = (f32[216,128]{1,0:T(8,128)}, f32[216,128]{1,0:T(8,128)S(1)}, u32[]{:S(2)}, u32[]{:S(2)}) collective-permute-start(f32[216,128]{1,0:T(8,128)} %get-tuple-element.28), channel_id=1, source_target_pairs={{0,1},{1,2},{2,3},{3,4},{4,5},{5,6},{6,7},{7,8},{8,9},{9,10},{10,1... | collective-permute-start | bytes 331784 | tf_op jit(solution)/shard_map/ppermute | solution.py:234
  11.4 18.3 %collective-permute-start.1 = (f32[216,128]{1,0:T(8,128)}, f32[216,128]{1,0:T(8,128)S(1)}, u32[]{:S(2)}, u32[]{:S(2)}) collective-permute-start(f32[216,128]{1,0:T(8,128)} %get-tuple-element.29), channel_id=1, source_target_pairs={{1,0},{2,1},{3,2},{4,3},{5,4},{6,5},{7,6},{8,7},{9,8},{10,9},{11,1... | collective-permute-start | bytes 331784 | tf_op jit(solution)/shard_map/ppermute | solution.py:235
  22.9 7.8 %collective-permute-start.3 = (f32[216,128]{1,0:T(8,128)}, f32[216,128]{1,0:T(8,128)S(1)}, u32[]{:S(2)}, u32[]{:S(2)}) collective-permute-start(f32[216,128]{1,0:T(8,128)} %get-tuple-element.30), channel_id=1, source_target_pairs={{64,0},{128,64},{192,128},{256,192},{320,256},{384,320},{448,384},... | collective-permute-start | bytes 331784 | tf_op jit(solution)/shard_map/ppermute | solution.py:237
  24.8 7.5 %collective-permute-start.2 = (f32[216,128]{1,0:T(8,128)}, f32[216,128]{1,0:T(8,128)S(1)}, u32[]{:S(2)}, u32[]{:S(2)}) collective-permute-start(f32[216,128]{1,0:T(8,128)} %get-tuple-element.30), channel_id=1, source_target_pairs={{0,64},{64,128},{128,192},{192,256},{256,320},{320,384},{384,448},... | collective-permute-start | bytes 331784 | tf_op jit(solution)/shard_map/ppermute | solution.py:236
  29.7 2.6 %copy-start = (f32[216,128]{1,0:T(8,128)}, f32[216,128]{1,0:T(8,128)S(1)}, u32[]{:S(2)}) copy-start(f32[216,128]{1,0:T(8,128)S(1)} %collective-permute-done.r1lo) | copy-start | bytes 331780
  29.7 2.6 %copy-start.1 = (f32[216,128]{1,0:T(8,128)}, f32[216,128]{1,0:T(8,128)S(1)}, u32[]{:S(2)}) copy-start(f32[216,128]{1,0:T(8,128)S(1)} %collective-permute-done.1.r1hi) | copy-start | bytes 331780
  30.7 1.6 %copy-start.2 = (f32[216,128]{1,0:T(8,128)}, f32[216,128]{1,0:T(8,128)S(1)}, u32[]{:S(2)}) copy-start(f32[216,128]{1,0:T(8,128)S(1)} %collective-permute-done.3.r1ghi) | copy-start | bytes 331780
  32.3 0.6 copy-start.3
  35.9 20.8 %collective-permute-start.4 = (f32[216,128]{1,0:T(8,128)}, f32[216,128]{1,0:T(8,128)S(1)}, u32[]{:S(2)}, u32[]{:S(2)}) collective-permute-start(f32[216,128]{1,0:T(8,128)} %get-tuple-element.34), channel_id=1, source_target_pairs={{0,1},{1,2},{2,3},{3,4},{4,5},{5,6},{6,7},{7,8},{8,9},{9,10},{10,1... | collective-permute-start | bytes 331784 | tf_op jit(solution)/shard_map/ppermute | solution.py:234
  37.9 18.9 %collective-permute-start.5 = (f32[216,128]{1,0:T(8,128)}, f32[216,128]{1,0:T(8,128)S(1)}, u32[]{:S(2)}, u32[]{:S(2)}) collective-permute-start(f32[216,128]{1,0:T(8,128)} %get-tuple-element.35), channel_id=1, source_target_pairs={{1,0},{2,1},{3,2},{4,3},{5,4},{6,5},{7,6},{8,7},{9,8},{10,9},{11,1... | collective-permute-start | bytes 331784 | tf_op jit(solution)/shard_map/ppermute | solution.py:235
  45.1 12.3 %collective-permute-start.7 = (f32[216,128]{1,0:T(8,128)}, f32[216,128]{1,0:T(8,128)S(1)}, u32[]{:S(2)}, u32[]{:S(2)}) collective-permute-start(f32[216,128]{1,0:T(8,128)} %get-tuple-element.36), channel_id=1, source_target_pairs={{64,0},{128,64},{192,128},{256,192},{320,256},{384,320},{448,384},... | collective-permute-start | bytes 331784 | tf_op jit(solution)/shard_map/ppermute | solution.py:237
  54.8 6.9 %collective-permute-start.6 = (f32[216,128]{1,0:T(8,128)}, f32[216,128]{1,0:T(8,128)S(1)}, u32[]{:S(2)}, u32[]{:S(2)}) collective-permute-start(f32[216,128]{1,0:T(8,128)} %get-tuple-element.36), channel_id=1, source_target_pairs={{0,64},{64,128},{128,192},{192,256},{256,320},{320,384},{384,448},... | collective-permute-start | bytes 331784 | tf_op jit(solution)/shard_map/ppermute | solution.py:236
  56.7 4.9 %copy-start.4 = (f32[216,128]{1,0:T(8,128)}, f32[216,128]{1,0:T(8,128)S(1)}, u32[]{:S(2)}) copy-start(f32[216,128]{1,0:T(8,128)S(1)} %collective-permute-done.4.r2lo) | copy-start | bytes 331780
  56.7 4.9 %copy-start.5 = (f32[216,128]{1,0:T(8,128)}, f32[216,128]{1,0:T(8,128)S(1)}, u32[]{:S(2)}) copy-start(f32[216,128]{1,0:T(8,128)S(1)} %collective-permute-done.5.r2hi) | copy-start | bytes 331780
  57.4 4.2 %copy-start.6 = (f32[216,128]{1,0:T(8,128)}, f32[216,128]{1,0:T(8,128)S(1)}, u32[]{:S(2)}) copy-start(f32[216,128]{1,0:T(8,128)S(1)} %collective-permute-done.7.r2ghi) | copy-start | bytes 331780
  61.6 0.6 copy-start.7

commit v3 on v2

--- a/solution.py
+++ b/solution.py
@@ -155,8 +155,9 @@
 
 
 def _kernel_a(x_ref, star_ref, stiff_ref, trace_ref, send_ref,
-              first_ref, fl_ref, t1_ref, t1l_ref, s1lo, s1hi, s1g, sllo, slhi, slg,
-              d_ref, a_ref, acc1_ref, acc2_ref, tl_ref, yt_ref):
+              first_ref, fl_ref, t1_ref, t1l_ref, s1lo, s1hi, s1g, plo, phi, pg, slg,
+              d_ref, a_ref, acc1_ref, acc2_ref, tl_ref, yt_ref,
+              sllo, slhi):
     x = _load_field(x_ref)
     stiff_st = jnp.concatenate([stiff_ref[d] for d in range(3)], axis=0)
     _taylor(x, star_ref, _split2(stiff_st), d_ref, a_ref, [(acc1_ref, W_FIRST), (acc2_ref, W_LATER)])
@@ -169,18 +170,21 @@
     _table(later, trace_p, yt_ref, tl_ref)
     t1l_ref[...] = t1_ref[...] + tl_ref[...]
     _send([t1_ref[...], tl_ref[...]], send_ref, [(s1lo, s1hi, s1g), (sllo, slhi, slg)])
-
-
-def _kernel_b(flag_ref, x_ref, first_ref, fl_ref, t1_ref, t1l_ref, sllo, slhi, slg,
-              r1lo, r1hi, r1glo, r1ghi, slot_ref, face_ref, star_ref, fo_ref, fn_ref,
+    plo[...] = s1lo[...] + sllo[...]
+    phi[...] = s1hi[...] + slhi[...]
+    pg[...] = s1g[...] + slg[...]
+
+
+def _kernel_b(grp_ref, x_ref, first_ref, fl_ref, t1_ref, t1l_ref, s1g, plo, phi, pg, slg,
+              r1lo, r1hi, r1ghi, slot_ref, face_ref, star_ref, fo_ref, fn_ref,
               stiff_ref, lift_ref, trace_ref, send_ref,
-              base_ref, integ_ref, own_ref, s2lo, s2hi, s2g,
+              base_ref, integ_ref, own_ref, elo, ehi, egup, egdn,
               d_ref, a_ref, v_ref, yf_ref, g_ref, acc_ref, yt_ref, lt_ref):
-    fault = flag_ref[0] == 1
-
-    @pl.when(fault)
+    grp = grp_ref[0]
+
+    @pl.when(grp == 0)
     def _():
-        comb = jnp.concatenate([t1_ref[...], r1lo[...], r1hi[...], r1glo[...], r1ghi[...]], axis=1)
+        comb = jnp.concatenate([t1_ref[...], r1lo[...], r1hi[...], jnp.zeros((TR, E), F32), r1ghi[...]], axis=1)
         _gather(comb, slot_ref, face_ref, g_ref)
         mid = _update(_load_field(x_ref), _load_field(first_ref), t1_ref, g_ref, star_ref, fo_ref, fn_ref,
                       stiff_ref, _lift_parts(lift_ref, lt_ref), a_ref, v_ref, yf_ref)
@@ -190,26 +194,31 @@
         second = acc_ref[...]
         _store_field(integ_ref, second)
         _table(second, _split2(_rows84(trace_ref)), yt_ref, own_ref)
-        _send([own_ref[...]], send_ref, [(s2lo, s2hi, s2g)])
-
-    @pl.when(jnp.logical_not(fault))
+        _send([own_ref[...]], send_ref, [(elo, ehi, egdn)])
+        egup[...] = s1g[...] + egdn[...]
+
+    @pl.when(grp != 0)
     def _():
         base_ref[...] = x_ref[...]
         integ_ref[...] = fl_ref[...]
         own_ref[...] = t1l_ref[...]
-        s2lo[...] = sllo[...]
-        s2hi[...] = slhi[...]
-        s2g[...] = slg[...]
-
-
-def _kernel_c(flag_ref, base_ref, integ_ref, own_ref, r1lo, r1hi, r1glo, r1ghi,
-              r2lo, r2hi, r2glo, r2ghi, slot_ref, face_ref, star_ref, fo_ref, fn_ref,
-              stiff_ref, lift_ref,
+        elo[...] = plo[...]
+        ehi[...] = phi[...]
+        egup[...] = pg[...]
+
+    @pl.when(grp == 1)
+    def _():
+        egdn[...] = slg[...]
+
+    @pl.when(grp > 1)
+    def _():
+        egdn[...] = pg[...]
+
+
+def _kernel_c(base_ref, integ_ref, own_ref, r2lo, r2hi, r2glo, r2ghi, slot_ref, face_ref,
+              star_ref, fo_ref, fn_ref, stiff_ref, lift_ref,
               out_ref, a_ref, v_ref, yf_ref, g_ref, lt_ref):
-    keep = (1 - flag_ref[0]).astype(F32)
-    comb = jnp.concatenate(
-        [own_ref[...], r2lo[...] + keep * r1lo[...], r2hi[...] + keep * r1hi[...],
-         r2glo[...] + keep * r1glo[...], r2ghi[...] + keep * r1ghi[...]], axis=1)
+    comb = jnp.concatenate([own_ref[...], r2lo[...], r2hi[...], r2glo[...], r2ghi[...]], axis=1)
     _gather(comb, slot_ref, face_ref, g_ref)
     out = _update(_load_field(base_ref), _load_field(integ_ref), own_ref, g_ref, star_ref, fo_ref, fn_ref,
                   stiff_ref, _lift_parts(lift_ref, lt_ref), a_ref, v_ref, yf_ref)
@@ -228,18 +237,27 @@
     return jax.ShapeDtypeStruct(shape, F32)
 
 
-def exchange(lo, hi, g):
+def exchange(lo, hi, gup, gdn):
     n_dom = lax.axis_size("dom")
     n_grp = lax.axis_size("grp")
     from_lo = lax.ppermute(hi, "dom", [(i, i + 1) for i in range(n_dom - 1)])
     from_hi = lax.ppermute(lo, "dom", [(i + 1, i) for i in range(n_dom - 1)])
-    from_glo = lax.ppermute(g, "grp", [(i, i + 1) for i in range(n_grp - 1)])
-    from_ghi = lax.ppermute(g, "grp", [(i + 1, i) for i in range(n_grp - 1)])
+    from_glo = lax.ppermute(gup, "grp", [(i, i + 1) for i in range(n_grp - 1)])
+    from_ghi = lax.ppermute(gdn, "grp", [(i + 1, i) for i in range(n_grp - 1)])
     return from_lo, from_hi, from_glo, from_ghi
 
 
+def exchange_fault(lo, hi, g):
+    n_dom = lax.axis_size("dom")
+    axes = ("grp", "dom")
+    from_lo = lax.ppermute(hi, axes, [(i, i + 1) for i in range(n_dom - 1)])
+    from_hi = lax.ppermute(lo, axes, [(i + 1, i) for i in range(n_dom - 1)])
+    from_ghi = lax.ppermute(g, axes, [(n_dom + i, i) for i in range(n_dom)])
+    return from_lo, from_hi, from_ghi
+
+
 def local(state, star, flux_own, flux_nbr, stiff, trace, lift, nbr_slot, nbr_face, send_slot):
-    flag = (lax.axis_index("grp") == 0).astype(jnp.int32).reshape(1)
+    grp = lax.axis_index("grp").astype(jnp.int32).reshape(1)
     x0 = jnp.transpose(state, (1, 0, 2))
     star = jnp.transpose(star, (1, 2, 0, 3))
     flux_own = jnp.transpose(flux_own, (1, 2, 0, 3))
@@ -254,38 +272,38 @@
     wide = pltpu.VMEM((NB, LN), F32)
     outs_a = pl.pallas_call(
         _kernel_a,
-        out_shape=(field, field, table, table, part, part, part, part, part, part),
+        out_shape=(field, field, table, table) + (part,) * 7,
         in_specs=[_vmem()] * 5,
-        out_specs=tuple([_vmem()] * 10),
+        out_specs=tuple([_vmem()] * 11),
         scratch_shapes=[wide, pltpu.VMEM((3 * NB, LN), F32), wide, wide, pltpu.VMEM((TR, 4 * E), F32),
-                        pltpu.VMEM((NQ, 4 * NF, E), F32)],
+                        pltpu.VMEM((NQ, 4 * NF, E), F32), pltpu.VMEM((TR, E), F32), pltpu.VMEM((TR, E), F32)],
     )(x0, star, stiff, trace, send)
-    first, fl, t1, t1l, s1lo, s1hi, s1g, sllo, slhi, slg = outs_a
-
-    r1 = exchange(s1lo, s1hi, s1g)
+    first, fl, t1, t1l, s1lo, s1hi, s1g, plo, phi, pg, slg = outs_a
+
+    r1 = exchange_fault(s1lo, s1hi, s1g)
 
     outs_b = pl.pallas_call(
         _kernel_b,
-        out_shape=(field, field, table, part, part, part),
-        in_specs=[_smem()] + [_vmem()] * 21,
-        out_specs=tuple([_vmem()] * 6),
+        out_shape=(field, field, table, part, part, part, part),
+        in_specs=[_smem()] + [_vmem()] * 22,
+        out_specs=tuple([_vmem()] * 7),
         scratch_shapes=[wide, pltpu.VMEM((3 * NB, LN), F32), wide, pltpu.VMEM((4 * FP, LN), F32),
                         pltpu.VMEM((TR, 4 * E), F32), wide, pltpu.VMEM((NQ, 4 * NF, E), F32),
                         pltpu.VMEM((4 * NF, E), F32)],
-    )(flag, x0, first, fl, t1, t1l, sllo, slhi, slg, *r1, nbr_slot, nbr_face, star, flux_own, flux_nbr,
+    )(grp, x0, first, fl, t1, t1l, s1g, plo, phi, pg, slg, *r1, nbr_slot, nbr_face, star, flux_own, flux_nbr,
       stiff, lift, trace, send)
-    base, integ, own, s2lo, s2hi, s2g = outs_b
-
-    r2 = exchange(s2lo, s2hi, s2g)
+    base, integ, own, elo, ehi, egup, egdn = outs_b
+
+    r2 = exchange(elo, ehi, egup, egdn)
 
     out = pl.pallas_call(
         _kernel_c,
         out_shape=field,
-        in_specs=[_smem()] + [_vmem()] * 18,
+        in_specs=[_vmem()] * 14,
         out_specs=_vmem(),
         scratch_shapes=[pltpu.VMEM((3 * NB, LN), F32), wide, pltpu.VMEM((4 * FP, LN), F32),
                         pltpu.VMEM((TR, 4 * E), F32), pltpu.VMEM((4 * NF, E), F32)],
-    )(flag, base, integ, own, *r1, *r2, nbr_slot, nbr_face, star, flux_own, flux_nbr, stiff, lift)
+    )(base, integ, own, *r2, nbr_slot, nbr_face, star, flux_own, flux_nbr, stiff, lift)
     return jnp.transpose(out, (1, 0, 2))
 
 

time: 68.1 us -> 64.8 us (0.952)
  the two profiles are of different devices: /device:TPU:24 before, /device:TPU:16 now
where the time goes in v3:
time: 64.8 us; the launch traced here: 64.5 us
  starting transfers between devices  25.6 us (40%)
  Pallas kernels  25.2 us (39%)
  waiting for transfers between devices  11 us (17%)
  local copies, waits for them, and re-layouts  2.55 us (4%)
    pallas_call x1, Pallas kernels, local(): pl.pallas_call(_kernel_b, out_shape=(field, field, table, part, part, par...  11.6 us
    ppermute x1, starting transfers between devices, exchange_fault(): from_hi = lax.ppermute(lo, axes, [(i + 1, i) for i in range(n_dom - 1)])  10.6 us
    pallas_call x1, Pallas kernels, local(): pl.pallas_call(_kernel_a, out_shape=(field, field, table, table) + (part,...  8.3 us
    ppermute x1, starting transfers between devices, exchange(): from_hi = lax.ppermute(lo, 'dom', [(i + 1, i) for i in range(n_dom - 1)])  7.26 us
    pallas_call x1, Pallas kernels, local(): pl.pallas_call(_kernel_c, out_shape=field, in_specs=[_vmem()] * 14, out_s...  5.27 us
    ppermute x1, waiting for transfers between devices, exchange(): from_ghi = lax.ppermute(gdn, 'grp', [(i + 1, i) for i in range(n_grp - 1)])  4.23 us
    ppermute x1, waiting for transfers between devices, exchange_fault(): from_ghi = lax.ppermute(g, axes, [(n_dom + i, i) for i in range(n_dom)])  4.23 us
    ppermute x1, starting transfers between devices, exchange(): from_lo = lax.ppermute(hi, 'dom', [(i, i + 1) for i in range(n_dom - 1)])  1.92 us
  transfers between devices with their start and end apart: 7, of which 4 were waited for; matrix products, arithmetic and copies ran while one was open for 0% of the time, Pallas kernels for 0%

profile of v3, /device:TPU:16, one launch (start us, length us, event | category | flops | bytes accessed | tf_op | source)
XLA Modules:
  0.0 64.5 jit_solution(13812632987849745077)
XLA Ops:
  0.0 1.3 %reshape.7.send_ref = s32[1,384]{1,0:T(1,128)} reshape(s32[384]{0:T(512)} %param.19) | data formatting | bytes 3072 | tf_op jit(solution)/shard_map/reshape | solution.py:267
  1.3 8.3 %shard_map.100 = (f32[9,56,128]{2,1,0:T(8,128)}, f32[9,56,128]{2,1,0:T(8,128)}, f32[216,512]{1,0:T(8,128)}, f32[216,512]{1,0:T(8,128)}, f32[216,128]{1,0:T(8,128...) custom-call(f32[9,56,128]{2,1,0:T(8,128)} %bitcast.11, ...), custom_call_target="tpu_custom_call" | custom-call | tf_op jit(solution)/shard_map/pallas_call | solution.py:273
  9.6 1.9 %collective-permute-start = (f32[216,128]{1,0:T(8,128)}, f32[216,128]{1,0:T(8,128)S(1)}, u32[]{:S(2)}, u32[]{:S(2)}) collective-permute-start(f32[216,128]{1,0:T(8,128)} %get-tuple-element.32), channel_id=1, source_target_pairs={{0,1},{1,2},{2,3},{3,4},{4,5},{5,6},{6,7},{7,8},{8,9},{9,10},{10,1... | collective-permute-start | bytes 331784 | tf_op jit(solution)/shard_map/ppermute | solution.py:253
  11.5 10.6 %collective-permute-start.1 = (f32[216,128]{1,0:T(8,128)}, f32[216,128]{1,0:T(8,128)S(1)}, u32[]{:S(2)}, u32[]{:S(2)}) collective-permute-start(f32[216,128]{1,0:T(8,128)} %get-tuple-element.33), channel_id=1, source_target_pairs={{1,0},{2,1},{3,2},{4,3},{5,4},{6,5},{7,6},{8,7},{9,8},{10,9},{11,1... | collective-permute-start | bytes 331784 | tf_op jit(solution)/shard_map/ppermute | solution.py:254
  22.1 1.3 %collective-permute-start.2 = (f32[216,128]{1,0:T(8,128)}, f32[216,128]{1,0:T(8,128)S(1)}, u32[]{:S(2)}, u32[]{:S(2)}) collective-permute-start(f32[216,128]{1,0:T(8,128)} %get-tuple-element.27.s1g), channel_id=1, source_target_pairs={{64,0},{65,1},{66,2},{67,3},{68,4},{69,5},{70,6},{71,7},{72,8},{73... | collective-permute-start | bytes 331784 | tf_op jit(solution)/shard_map/ppermute | solution.py:255
  23.4 0.0 collective-permute-done.r1lo
  23.4 0.0 copy-start
  23.4 1.3 %collective-permute-done.1.r1hi = f32[216,128]{1,0:T(8,128)S(1)} collective-permute-done((f32[216,128]{1,0:T(8,128)}, f32[216,128]{1,0:T(8,128)S(1)}, u32[]{:S(2)}, u32[]{:S(2)}) %collective-permute-start.1) | collective-permute-done | bytes 110624 | tf_op jit(solution)/shard_map/ppermute | solution.py:254
  24.7 4.2 %collective-permute-done.2.r1ghi = f32[216,128]{1,0:T(8,128)S(1)} collective-permute-done((f32[216,128]{1,0:T(8,128)}, f32[216,128]{1,0:T(8,128)S(1)}, u32[]{:S(2)}, u32[]{:S(2)}) %collective-permute-start.2) | collective-permute-done | bytes 110624 | tf_op jit(solution)/shard_map/ppermute | solution.py:255
  29.0 0.0 copy-done
  29.0 0.0 copy-done.1
  29.0 0.6 copy-done.2
  29.6 11.6 %shard_map.101 = (f32[9,56,128]{2,1,0:T(8,128)}, f32[9,56,128]{2,1,0:T(8,128)}, f32[216,512]{1,0:T(8,128)}, f32[216,128]{1,0:T(8,128)}, f32[216,128]{1,0:T(8,128...) custom-call(s32[1]{0:T(128)} %bitcast.grp_ref, f32[9,56,128]{2,1,0:T(8,128)} %bitcast.12, ...), custom_call_target="tpu_custom_call" | custom-call | tf_op jit(solution)/shard_map/pallas_call | solution.py:285
  41.2 1.9 %collective-permute-start.3 = (f32[216,128]{1,0:T(8,128)}, f32[216,128]{1,0:T(8,128)S(1)}, u32[]{:S(2)}, u32[]{:S(2)}) collective-permute-start(f32[216,128]{1,0:T(8,128)} %get-tuple-element.37), channel_id=1, source_target_pairs={{0,1},{1,2},{2,3},{3,4},{4,5},{5,6},{6,7},{7,8},{8,9},{9,10},{10,1... | collective-permute-start | bytes 331784 | tf_op jit(solution)/shard_map/ppermute | solution.py:243
  43.2 7.3 %collective-permute-start.4 = (f32[216,128]{1,0:T(8,128)}, f32[216,128]{1,0:T(8,128)S(1)}, u32[]{:S(2)}, u32[]{:S(2)}) collective-permute-start(f32[216,128]{1,0:T(8,128)} %get-tuple-element.38), channel_id=1, source_target_pairs={{1,0},{2,1},{3,2},{4,3},{5,4},{6,5},{7,6},{8,7},{9,8},{10,9},{11,1... | collective-permute-start | bytes 331784 | tf_op jit(solution)/shard_map/ppermute | solution.py:244
  50.4 1.3 %collective-permute-start.5 = (f32[216,128]{1,0:T(8,128)}, f32[216,128]{1,0:T(8,128)S(1)}, u32[]{:S(2)}, u32[]{:S(2)}) collective-permute-start(f32[216,128]{1,0:T(8,128)} %get-tuple-element.39), channel_id=1, source_target_pairs={{0,64},{64,128},{128,192},{192,256},{256,320},{320,384},{384,448},... | collective-permute-start | bytes 331784 | tf_op jit(solution)/shard_map/ppermute | solution.py:245
  51.7 1.3 %collective-permute-start.6 = (f32[216,128]{1,0:T(8,128)}, f32[216,128]{1,0:T(8,128)S(1)}, u32[]{:S(2)}, u32[]{:S(2)}) collective-permute-start(f32[216,128]{1,0:T(8,128)} %get-tuple-element.40), channel_id=1, source_target_pairs={{64,0},{128,64},{192,128},{256,192},{320,256},{384,320},{448,384},... | collective-permute-start | bytes 331784 | tf_op jit(solution)/shard_map/ppermute | solution.py:246
  53.0 0.0 collective-permute-done.3.r2lo
  53.0 0.0 collective-permute-done.4.r2hi
  53.1 0.0 copy-start.4
  53.1 1.3 %collective-permute-done.5.r2glo = f32[216,128]{1,0:T(8,128)S(1)} collective-permute-done((f32[216,128]{1,0:T(8,128)}, f32[216,128]{1,0:T(8,128)S(1)}, u32[]{:S(2)}, u32[]{:S(2)}) %collective-permute-start.5) | collective-permute-done | bytes 110624 | tf_op jit(solution)/shard_map/ppermute | solution.py:245
  54.3 4.2 %collective-permute-done.6.r2ghi = f32[216,128]{1,0:T(8,128)S(1)} collective-permute-done((f32[216,128]{1,0:T(8,128)}, f32[216,128]{1,0:T(8,128)S(1)}, u32[]{:S(2)}, u32[]{:S(2)}) %collective-permute-start.6) | collective-permute-done | bytes 110624 | tf_op jit(solution)/shard_map/ppermute | solution.py:246
  58.6 0.6 copy-done.6
  59.2 5.3 %shard_map.102 = f32[9,56,128]{2,1,0:T(8,128)} custom-call(f32[9,56,128]{2,1,0:T(8,128)} %get-tuple-element.34.base_ref, f32[9,56,128]{2,1,0:T(8,128)} %get-tuple-element.35.integ_ref, f32[216,512]{1,0:T(8,128)} %get-tuple-element.36.own_ref, f32[216,128]{1,0:T(8,128)} %copy-done.3, f32[216,128]{1,0:T(8,128)} %copy-done.4, f32[216,128]{1,0:T(8,128)} %copy-done.5, ...), custom_call_target="tpu_custom_call" | custom-call | tf_op jit(solution)/shard_map/pallas_call | solution.py:299
  (8 shorter events, 0.0 us)
Async XLA Ops:
  9.6 13.8 %collective-permute-start = (f32[216,128]{1,0:T(8,128)}, f32[216,128]{1,0:T(8,128)S(1)}, u32[]{:S(2)}, u32[]{:S(2)}) collective-permute-start(f32[216,128]{1,0:T(8,128)} %get-tuple-element.32), channel_id=1, source_target_pairs={{0,1},{1,2},{2,3},{3,4},{4,5},{5,6},{6,7},{7,8},{8,9},{9,10},{10,1... | collective-permute-start | bytes 331784 | tf_op jit(solution)/shard_map/ppermute | solution.py:253
  11.5 13.2 %collective-permute-start.1 = (f32[216,128]{1,0:T(8,128)}, f32[216,128]{1,0:T(8,128)S(1)}, u32[]{:S(2)}, u32[]{:S(2)}) collective-permute-start(f32[216,128]{1,0:T(8,128)} %get-tuple-element.33), channel_id=1, source_target_pairs={{1,0},{2,1},{3,2},{4,3},{5,4},{6,5},{7,6},{8,7},{9,8},{10,9},{11,1... | collective-permute-start | bytes 331784 | tf_op jit(solution)/shard_map/ppermute | solution.py:254
  22.1 6.9 %collective-permute-start.2 = (f32[216,128]{1,0:T(8,128)}, f32[216,128]{1,0:T(8,128)S(1)}, u32[]{:S(2)}, u32[]{:S(2)}) collective-permute-start(f32[216,128]{1,0:T(8,128)} %get-tuple-element.27.s1g), channel_id=1, source_target_pairs={{64,0},{65,1},{66,2},{67,3},{68,4},{69,5},{70,6},{71,7},{72,8},{73... | collective-permute-start | bytes 331784 | tf_op jit(solution)/shard_map/ppermute | solution.py:255
  23.4 5.5 %copy-start = (f32[216,128]{1,0:T(8,128)}, f32[216,128]{1,0:T(8,128)S(1)}, u32[]{:S(2)}) copy-start(f32[216,128]{1,0:T(8,128)S(1)} %collective-permute-done.r1lo) | copy-start | bytes 331780
  24.7 4.2 %copy-start.1 = (f32[216,128]{1,0:T(8,128)}, f32[216,128]{1,0:T(8,128)S(1)}, u32[]{:S(2)}) copy-start(f32[216,128]{1,0:T(8,128)S(1)} %collective-permute-done.1.r1hi) | copy-start | bytes 331780
  29.0 0.6 copy-start.2
  41.2 11.8 %collective-permute-start.3 = (f32[216,128]{1,0:T(8,128)}, f32[216,128]{1,0:T(8,128)S(1)}, u32[]{:S(2)}, u32[]{:S(2)}) collective-permute-start(f32[216,128]{1,0:T(8,128)} %get-tuple-element.37), channel_id=1, source_target_pairs={{0,1},{1,2},{2,3},{3,4},{4,5},{5,6},{6,7},{7,8},{8,9},{9,10},{10,1... | collective-permute-start | bytes 331784 | tf_op jit(solution)/shard_map/ppermute | solution.py:243
  43.2 9.9 %collective-permute-start.4 = (f32[216,128]{1,0:T(8,128)}, f32[216,128]{1,0:T(8,128)S(1)}, u32[]{:S(2)}, u32[]{:S(2)}) collective-permute-start(f32[216,128]{1,0:T(8,128)} %get-tuple-element.38), channel_id=1, source_target_pairs={{1,0},{2,1},{3,2},{4,3},{5,4},{6,5},{7,6},{8,7},{9,8},{10,9},{11,1... | collective-permute-start | bytes 331784 | tf_op jit(solution)/shard_map/ppermute | solution.py:244
  50.4 3.9 %collective-permute-start.5 = (f32[216,128]{1,0:T(8,128)}, f32[216,128]{1,0:T(8,128)S(1)}, u32[]{:S(2)}, u32[]{:S(2)}) collective-permute-start(f32[216,128]{1,0:T(8,128)} %get-tuple-element.39), channel_id=1, source_target_pairs={{0,64},{64,128},{128,192},{192,256},{256,320},{320,384},{384,448},... | collective-permute-start | bytes 331784 | tf_op jit(solution)/shard_map/ppermute | solution.py:245
  51.7 6.9 %collective-permute-start.6 = (f32[216,128]{1,0:T(8,128)}, f32[216,128]{1,0:T(8,128)S(1)}, u32[]{:S(2)}, u32[]{:S(2)}) collective-permute-start(f32[216,128]{1,0:T(8,128)} %get-tuple-element.40), channel_id=1, source_target_pairs={{64,0},{128,64},{192,128},{256,192},{320,256},{384,320},{448,384},... | collective-permute-start | bytes 331784 | tf_op jit(solution)/shard_map/ppermute | solution.py:246
  53.0 5.5 %copy-start.3 = (f32[216,128]{1,0:T(8,128)}, f32[216,128]{1,0:T(8,128)S(1)}, u32[]{:S(2)}) copy-start(f32[216,128]{1,0:T(8,128)S(1)} %collective-permute-done.3.r2lo) | copy-start | bytes 331780
  53.1 5.5 %copy-start.4 = (f32[216,128]{1,0:T(8,128)}, f32[216,128]{1,0:T(8,128)S(1)}, u32[]{:S(2)}) copy-start(f32[216,128]{1,0:T(8,128)S(1)} %collective-permute-done.4.r2hi) | copy-start | bytes 331780
  54.3 4.2 %copy-start.5 = (f32[216,128]{1,0:T(8,128)}, f32[216,128]{1,0:T(8,128)S(1)}, u32[]{:S(2)}) copy-start(f32[216,128]{1,0:T(8,128)S(1)} %collective-permute-done.5.r2glo) | copy-start | bytes 331780
  58.6 0.6 copy-start.6

commit v4 on v3

--- a/solution.py
+++ b/solution.py
@@ -114,16 +114,36 @@
         g_ref[...] = blk[:, 2 * E:3 * E]
 
 
-def _gather(comb, slot_ref, face_ref, g_ref):
-    rows = lax.broadcasted_iota(jnp.int32, (8 * E, E), 0)
+def _gather(comb, slot_ref, face_ref, g_ref, received):
+    rows = lax.broadcasted_iota(jnp.int32, (4 * E, E), 0)
     parts = _split3(comb)
     for f in range(4):
         v = slot_ref[f:f + 1, :]
-        nf = face_ref[f:f + 1, :]
-        s = v - E
-        src = jnp.where(v < E, nf * E + v, 4 * E + s + jnp.where(s >= 2 * E, 64, 0))
+        if received:
+            s = v - E
+            src = jnp.where(v < E, -1, s + jnp.where(s >= 2 * E, 64, 0))
+        else:
+            src = jnp.where(v < E, face_ref[f:f + 1, :] * E + v, -1)
         onehot = jnp.where(rows == src, 1.0, 0.0).astype(BF)
         g_ref[:, f * E:(f + 1) * E] = _sel(parts, onehot)
+
+
+def _fmix(pairs, yf_ref, base_ref=None):
+    for q in range(NQ):
+        accs = [None] * 4
+        for p in range(NQ):
+            rows = [fl_ref[p, q] for _, fl_ref in pairs]
+            for f in range(4):
+                t = None
+                for (t_ref, _), row in zip(pairs, rows):
+                    u = t_ref[p * FP:(p + 1) * FP, f * E:(f + 1) * E] * row[f:f + 1, :]
+                    t = u if t is None else t + u
+                accs[f] = t if accs[f] is None else accs[f] + t
+        for f in range(4):
+            acc = accs[f]
+            if base_ref is not None:
+                acc = base_ref[f * FP:(f + 1) * FP, q * E:(q + 1) * E] + acc
+            yf_ref[f * FP:(f + 1) * FP, q * E:(q + 1) * E] = acc
 
 
 def _lift_parts(lift_ref, lt_ref):
@@ -131,75 +151,87 @@
     return [_split2(lt_ref[pl.ds(f, NF, stride=4), 0:NB]) for f in range(4)]
 
 
-def _update(b, x, s_ref, g_ref, star_ref, fo_ref, fn_ref, stiff_ref, lift_p, a_ref, v_ref, yf_ref):
+def _vol(b, x, star_ref, stiff_ref, a_ref, v_ref):
     xp = _split2(x)
     for d in range(3):
         a_ref[d * NB:(d + 1) * NB, :] = _dot3_t(_split2(stiff_ref[d]), xp)
     _mix_vol(a_ref, star_ref, v_ref, 1)
-    for q in range(NQ):
-        accs = [None] * 4
-        for p in range(NQ):
-            orow = fo_ref[p, q]
-            nrow = fn_ref[p, q]
-            for f in range(4):
-                t = (s_ref[p * FP:(p + 1) * FP, f * E:(f + 1) * E] * orow[f:f + 1, :]
-                     + g_ref[p * FP:(p + 1) * FP, f * E:(f + 1) * E] * nrow[f:f + 1, :])
-                accs[f] = t if accs[f] is None else accs[f] + t
-        for f in range(4):
-            yf_ref[f * FP:(f + 1) * FP, q * E:(q + 1) * E] = accs[f]
+    return b + v_ref[...]
+
+
+def _partial(b, x, own_ref, star_ref, fo_ref, fn_ref, stiff_ref, slot_ref, face_ref,
+             a_ref, v_ref, g_ref, bv_ref, yp_ref):
+    bv_ref[...] = _vol(b, x, star_ref, stiff_ref, a_ref, v_ref)
+    _gather(own_ref[...], slot_ref, face_ref, g_ref, False)
+    _fmix([(own_ref, fo_ref), (g_ref, fn_ref)], yp_ref)
+
+
+def _finish(bv_ref, yp_ref, recv, fn_ref, lift_p, slot_ref, face_ref, g_ref, yf_ref):
+    _gather(jnp.concatenate(recv, axis=1), slot_ref, face_ref, g_ref, True)
+    _fmix([(g_ref, fn_ref)], yf_ref, yp_ref)
     ftot = None
     for f in range(4):
         t = _dot3_t(lift_p[f], _split2(yf_ref[f * FP:f * FP + NF, :]))
         ftot = t if ftot is None else ftot + t
-    return (b + v_ref[...]) - ftot
-
-
-def _kernel_a(x_ref, star_ref, stiff_ref, trace_ref, send_ref,
-              first_ref, fl_ref, t1_ref, t1l_ref, s1lo, s1hi, s1g, plo, phi, pg, slg,
-              d_ref, a_ref, acc1_ref, acc2_ref, tl_ref, yt_ref,
-              sllo, slhi):
+    return bv_ref[...] - ftot
+
+
+def _kernel_a1(x_ref, star_ref, stiff_ref, trace_ref, send_ref,
+               first_ref, later_ref, t1_ref, s1lo, s1hi, s1g,
+               d_ref, a_ref, acc1_ref, acc2_ref, yt_ref):
     x = _load_field(x_ref)
     stiff_st = jnp.concatenate([stiff_ref[d] for d in range(3)], axis=0)
     _taylor(x, star_ref, _split2(stiff_st), d_ref, a_ref, [(acc1_ref, W_FIRST), (acc2_ref, W_LATER)])
     first = acc1_ref[...]
-    later = acc2_ref[...]
-    _store_field(first_ref, first)
-    _store_field(fl_ref, first + later)
-    trace_p = _split2(_rows84(trace_ref))
-    _table(first, trace_p, yt_ref, t1_ref)
-    _table(later, trace_p, yt_ref, tl_ref)
+    first_ref[...] = first
+    later_ref[...] = acc2_ref[...]
+    _table(first, _split2(_rows84(trace_ref)), yt_ref, t1_ref)
+    _send([t1_ref[...]], send_ref, [(s1lo, s1hi, s1g)])
+
+
+def _kernel_a2(grp_ref, x_ref, first_ref, later_ref, t1_ref, s1lo, s1hi, s1g, star_ref, fo_ref, fn_ref,
+               stiff_ref, trace_ref, send_ref, slot_ref, face_ref,
+               fl_ref, t1l_ref, plo, phi, pg, slg, bv_ref, yp_ref,
+               tl_ref, yt_ref, sllo, slhi, a_ref, v_ref, g_ref):
+    later = later_ref[...]
+    fl_ref[...] = first_ref[...] + later
+    _table(later, _split2(_rows84(trace_ref)), yt_ref, tl_ref)
     t1l_ref[...] = t1_ref[...] + tl_ref[...]
-    _send([t1_ref[...], tl_ref[...]], send_ref, [(s1lo, s1hi, s1g), (sllo, slhi, slg)])
+    _send([tl_ref[...]], send_ref, [(sllo, slhi, slg)])
     plo[...] = s1lo[...] + sllo[...]
     phi[...] = s1hi[...] + slhi[...]
     pg[...] = s1g[...] + slg[...]
 
-
-def _kernel_b(grp_ref, x_ref, first_ref, fl_ref, t1_ref, t1l_ref, s1g, plo, phi, pg, slg,
-              r1lo, r1hi, r1ghi, slot_ref, face_ref, star_ref, fo_ref, fn_ref,
+    @pl.when(grp_ref[0] == 0)
+    def _():
+        _partial(_load_field(x_ref), first_ref[...], t1_ref, star_ref, fo_ref, fn_ref, stiff_ref,
+                 slot_ref, face_ref, a_ref, v_ref, g_ref, bv_ref, yp_ref)
+
+
+def _kernel_b(grp_ref, x_ref, fl_ref, t1l_ref, s1g, plo, phi, pg, slg, bv_ref, yp_ref,
+              r1lo, r1hi, r1ghi, slot_ref, face_ref, star_ref, fn_ref,
               stiff_ref, lift_ref, trace_ref, send_ref,
               base_ref, integ_ref, own_ref, elo, ehi, egup, egdn,
-              d_ref, a_ref, v_ref, yf_ref, g_ref, acc_ref, yt_ref, lt_ref):
+              d_ref, a_ref, yf_ref, g_ref, acc_ref, yt_ref, lt_ref):
     grp = grp_ref[0]
 
     @pl.when(grp == 0)
     def _():
-        comb = jnp.concatenate([t1_ref[...], r1lo[...], r1hi[...], jnp.zeros((TR, E), F32), r1ghi[...]], axis=1)
-        _gather(comb, slot_ref, face_ref, g_ref)
-        mid = _update(_load_field(x_ref), _load_field(first_ref), t1_ref, g_ref, star_ref, fo_ref, fn_ref,
-                      stiff_ref, _lift_parts(lift_ref, lt_ref), a_ref, v_ref, yf_ref)
-        _store_field(base_ref, mid)
+        recv = [r1lo[...], r1hi[...], jnp.zeros((TR, E), F32), r1ghi[...]]
+        mid = _finish(bv_ref, yp_ref, recv, fn_ref, _lift_parts(lift_ref, lt_ref), slot_ref, face_ref,
+                      g_ref, yf_ref)
+        base_ref[...] = mid
         stiff_st = jnp.concatenate([stiff_ref[d] for d in range(3)], axis=0)
         _taylor(mid, star_ref, _split2(stiff_st), d_ref, a_ref, [(acc_ref, W_FIRST)])
         second = acc_ref[...]
-        _store_field(integ_ref, second)
+        integ_ref[...] = second
         _table(second, _split2(_rows84(trace_ref)), yt_ref, own_ref)
         _send([own_ref[...]], send_ref, [(elo, ehi, egdn)])
         egup[...] = s1g[...] + egdn[...]
 
     @pl.when(grp != 0)
     def _():
-        base_ref[...] = x_ref[...]
+        base_ref[...] = _load_field(x_ref)
         integ_ref[...] = fl_ref[...]
         own_ref[...] = t1l_ref[...]
         elo[...] = plo[...]
@@ -215,13 +247,17 @@
         egdn[...] = pg[...]
 
 
-def _kernel_c(base_ref, integ_ref, own_ref, r2lo, r2hi, r2glo, r2ghi, slot_ref, face_ref,
-              star_ref, fo_ref, fn_ref, stiff_ref, lift_ref,
-              out_ref, a_ref, v_ref, yf_ref, g_ref, lt_ref):
-    comb = jnp.concatenate([own_ref[...], r2lo[...], r2hi[...], r2glo[...], r2ghi[...]], axis=1)
-    _gather(comb, slot_ref, face_ref, g_ref)
-    out = _update(_load_field(base_ref), _load_field(integ_ref), own_ref, g_ref, star_ref, fo_ref, fn_ref,
-                  stiff_ref, _lift_parts(lift_ref, lt_ref), a_ref, v_ref, yf_ref)
+def _kernel_b2(base_ref, integ_ref, own_ref, star_ref, fo_ref, fn_ref, stiff_ref, slot_ref, face_ref,
+               bv_ref, yp_ref, a_ref, v_ref, g_ref):
+    _partial(base_ref[...], integ_ref[...], own_ref, star_ref, fo_ref, fn_ref, stiff_ref,
+             slot_ref, face_ref, a_ref, v_ref, g_ref, bv_ref, yp_ref)
+
+
+def _kernel_c(bv_ref, yp_ref, r2lo, r2hi, r2glo, r2ghi, slot_ref, face_ref, fn_ref, lift_ref,
+              out_ref, yf_ref, g_ref, lt_ref):
+    recv = [r2lo[...], r2hi[...], r2glo[...], r2ghi[...]]
+    out = _finish(bv_ref, yp_ref, recv, fn_ref, _lift_parts(lift_ref, lt_ref), slot_ref, face_ref,
+                  g_ref, yf_ref)
     _store_field(out_ref, out)
 
 
@@ -267,43 +303,62 @@
     send = send_slot.reshape(1, 3 * E)
 
     field = _sds((NQ, NB, E))
+    flat = _sds((NB, LN))
     table = _sds((TR, 4 * E))
     part = _sds((TR, E))
+    yflux = _sds((4 * FP, LN))
     wide = pltpu.VMEM((NB, LN), F32)
-    outs_a = pl.pallas_call(
-        _kernel_a,
-        out_shape=(field, field, table, table) + (part,) * 7,
+    amat = pltpu.VMEM((3 * NB, LN), F32)
+    tab = pltpu.VMEM((TR, 4 * E), F32)
+    ytr = pltpu.VMEM((NQ, 4 * NF, E), F32)
+    yfs = pltpu.VMEM((4 * FP, LN), F32)
+    lts = pltpu.VMEM((4 * NF, E), F32)
+
+    first, later, t1, s1lo, s1hi, s1g = pl.pallas_call(
+        _kernel_a1,
+        out_shape=(flat, flat, table, part, part, part),
         in_specs=[_vmem()] * 5,
-        out_specs=tuple([_vmem()] * 11),
-        scratch_shapes=[wide, pltpu.VMEM((3 * NB, LN), F32), wide, wide, pltpu.VMEM((TR, 4 * E), F32),
-                        pltpu.VMEM((NQ, 4 * NF, E), F32), pltpu.VMEM((TR, E), F32), pltpu.VMEM((TR, E), F32)],
+        out_specs=tuple([_vmem()] * 6),
+        scratch_shapes=[wide, amat, wide, wide, ytr],
     )(x0, star, stiff, trace, send)
-    first, fl, t1, t1l, s1lo, s1hi, s1g, plo, phi, pg, slg = outs_a
 
     r1 = exchange_fault(s1lo, s1hi, s1g)
 
-    outs_b = pl.pallas_call(
+    fl, t1l, plo, phi, pg, slg, bv1, yp1 = pl.pallas_call(
+        _kernel_a2,
+        out_shape=(flat, table, part, part, part, part, flat, yflux),
+        in_specs=[_smem()] + [_vmem()] * 15,
+        out_specs=tuple([_vmem()] * 8),
+        scratch_shapes=[tab, ytr, pltpu.VMEM((TR, E), F32), pltpu.VMEM((TR, E), F32), amat, wide, tab],
+    )(grp, x0, first, later, t1, s1lo, s1hi, s1g, star, flux_own, flux_nbr, stiff, trace, send,
+      nbr_slot, nbr_face)
+
+    base, integ, own, elo, ehi, egup, egdn = pl.pallas_call(
         _kernel_b,
-        out_shape=(field, field, table, part, part, part, part),
-        in_specs=[_smem()] + [_vmem()] * 22,
+        out_shape=(flat, flat, table, part, part, part, part),
+        in_specs=[_smem()] + [_vmem()] * 21,
         out_specs=tuple([_vmem()] * 7),
-        scratch_shapes=[wide, pltpu.VMEM((3 * NB, LN), F32), wide, pltpu.VMEM((4 * FP, LN), F32),
-                        pltpu.VMEM((TR, 4 * E), F32), wide, pltpu.VMEM((NQ, 4 * NF, E), F32),
-                        pltpu.VMEM((4 * NF, E), F32)],
-    )(grp, x0, first, fl, t1, t1l, s1g, plo, phi, pg, slg, *r1, nbr_slot, nbr_face, star, flux_own, flux_nbr,
+        scratch_shapes=[wide, amat, yfs, tab, wide, ytr, lts],
+    )(grp, x0, fl, t1l, s1g, plo, phi, pg, slg, bv1, yp1, *r1, nbr_slot, nbr_face, star, flux_nbr,
       stiff, lift, trace, send)
-    base, integ, own, elo, ehi, egup, egdn = outs_b
 
     r2 = exchange(elo, ehi, egup, egdn)
+
+    bv2, yp2 = pl.pallas_call(
+        _kernel_b2,
+        out_shape=(flat, yflux),
+        in_specs=[_vmem()] * 9,
+        out_specs=(_vmem(), _vmem()),
+        scratch_shapes=[amat, wide, tab],
+    )(base, integ, own, star, flux_own, flux_nbr, stiff, nbr_slot, nbr_face)
 
     out = pl.pallas_call(
         _kernel_c,
         out_shape=field,
-        in_specs=[_vmem()] * 14,
+        in_specs=[_vmem()] * 10,
         out_specs=_vmem(),
-        scratch_shapes=[pltpu.VMEM((3 * NB, LN), F32), wide, pltpu.VMEM((4 * FP, LN), F32),
-                        pltpu.VMEM((TR, 4 * E), F32), pltpu.VMEM((4 * NF, E), F32)],
-    )(base, integ, own, *r2, nbr_slot, nbr_face, star, flux_own, flux_nbr, stiff, lift)
+        scratch_shapes=[yfs, tab, lts],
+    )(bv2, yp2, *r2, nbr_slot, nbr_face, flux_nbr, lift)
     return jnp.transpose(out, (1, 0, 2))
 
 

time: 64.8 us -> 62.3 us (0.961)
  the two profiles are of different devices: /device:TPU:16 before, /device:TPU:24 now
where the time goes in v4:
time: 62.3 us; the launch traced here: 61.9 us
  starting transfers between devices  37 us (59%)
  Pallas kernels  22.1 us (35%)
  local copies, waits for them, and re-layouts  2.59 us (4%)
    ppermute x1, starting transfers between devices, exchange_fault(): from_ghi = lax.ppermute(g, axes, [(n_dom + i, i) for i in range(n_dom)])  13.8 us
    ppermute x1, starting transfers between devices, exchange(): from_ghi = lax.ppermute(gdn, 'grp', [(i + 1, i) for i in range(n_grp - 1)])  10.4 us
    pallas_call x1, Pallas kernels, local(): pl.pallas_call(_kernel_a1, out_shape=(flat, flat, table, part, part, part...  7.59 us
    ppermute x1, starting transfers between devices, exchange(): from_hi = lax.ppermute(lo, 'dom', [(i + 1, i) for i in range(n_dom - 1)])  7.58 us
    pallas_call x1, Pallas kernels, local(): pl.pallas_call(_kernel_b2, out_shape=(flat, yflux), in_specs=[_vmem()] *...  4.25 us
    pallas_call x1, Pallas kernels, local(): pl.pallas_call(_kernel_a2, out_shape=(flat, table, part, part, part, part...  3.7 us
    pallas_call x1, Pallas kernels, local(): pl.pallas_call(_kernel_c, out_shape=field, in_specs=[_vmem()] * 10, out_s...  3.47 us
    pallas_call x1, Pallas kernels, local(): pl.pallas_call(_kernel_b, out_shape=(flat, flat, table, part, part, part,...  3.09 us
  transfers between devices with their start and end apart: 7, of which 0 were waited for; matrix products, arithmetic and copies ran while one was open for 0% of the time, Pallas kernels for 13%

profile of v4, /device:TPU:24, one launch (start us, length us, event | category | flops | bytes accessed | tf_op | source)
XLA Modules:
  0.0 61.9 jit_solution(18186446935732462187)
XLA Ops:
  0.0 1.2 %reshape.7.send_ref = s32[1,384]{1,0:T(1,128)} reshape(s32[384]{0:T(512)} %param.19) | data formatting | bytes 3072 | tf_op jit(solution)/shard_map/reshape | solution.py:303
  1.2 7.6 %shard_map.100 = (f32[56,1152]{1,0:T(8,128)}, f32[56,1152]{1,0:T(8,128)}, f32[216,512]{1,0:T(8,128)}, f32[216,128]{1,0:T(8,128)}, f32[216,128]{1,0:T(8,128)}, /*index=5*/f32[216,128]{1,0:T(8,128)}) custom-call(f32[9,56,128]{2,1,0:T(8,128)} %bitcast.16, f32[9,9,3,128]{3,2,1,0:T(4,128)} %bitcast.8, f32[3,56,56]{2,1,0:T(8,128)} %stiff_ref.7, ...), custom_call_target="tpu_custom_call" | custom-call | tf_op jit(solution)/shard_map/pallas_call | solution.py:317
  8.8 0.7 %collective-permute-start.1 = (f32[216,128]{1,0:T(8,128)}, f32[216,128]{1,0:T(8,128)S(1)}, u32[]{:S(2)}, u32[]{:S(2)}) collective-permute-start(f32[216,128]{1,0:T(8,128)} %get-tuple-element.31.s1lo), channel_id=1, source_target_pairs={{1,0},{2,1},{3,2},{4,3},{5,4},{6,5},{7,6},{8,7},{9,8},{10,9},{11,1... | collective-permute-start | bytes 331784 | tf_op jit(solution)/shard_map/ppermute | solution.py:290
  9.5 0.7 %collective-permute-start = (f32[216,128]{1,0:T(8,128)}, f32[216,128]{1,0:T(8,128)S(1)}, u32[]{:S(2)}, u32[]{:S(2)}) collective-permute-start(f32[216,128]{1,0:T(8,128)} %get-tuple-element.32.s1hi), channel_id=1, source_target_pairs={{0,1},{1,2},{2,3},{3,4},{4,5},{5,6},{6,7},{7,8},{8,9},{9,10},{10,1... | collective-permute-start | bytes 331784 | tf_op jit(solution)/shard_map/ppermute | solution.py:289
  10.1 13.8 %collective-permute-start.2 = (f32[216,128]{1,0:T(8,128)}, f32[216,128]{1,0:T(8,128)S(1)}, u32[]{:S(2)}, u32[]{:S(2)}) collective-permute-start(f32[216,128]{1,0:T(8,128)} %get-tuple-element.33.s1g), channel_id=1, source_target_pairs={{64,0},{65,1},{66,2},{67,3},{68,4},{69,5},{70,6},{71,7},{72,8},{73... | collective-permute-start | bytes 331784 | tf_op jit(solution)/shard_map/ppermute | solution.py:291
  24.0 3.7 %shard_map.101 = (f32[56,1152]{1,0:T(8,128)}, f32[216,512]{1,0:T(8,128)}, f32[216,128]{1,0:T(8,128)}, f32[216,128]{1,0:T(8,128)}, f32[216,128]{1,0:T(8,128)}, /*...) custom-call(s32[1]{0:T(128)} %bitcast.grp_ref, f32[9,56,128]{2,1,0:T(8,128)} %bitcast.17, ...), custom_call_target="tpu_custom_call" | custom-call | tf_op jit(solution)/shard_map/pallas_call | solution.py:327
  27.7 0.0 collective-permute-done.r1lo
  27.8 0.6 copy-done.4
  28.4 0.0 copy-done.5
  28.4 0.0 copy-done.6
  28.4 3.1 %shard_map.102 = (f32[56,1152]{1,0:T(8,128)}, f32[56,1152]{1,0:T(8,128)}, f32[216,512]{1,0:T(8,128)}, f32[216,128]{1,0:T(8,128)}, f32[216,128]{1,0:T(8,128)}, /*index=5*/f32[216,128]{1,0:T(8,128)}, f32[216,128]{1,0:T(8,128)}) custom-call(s32[1]{0:T(128)} %bitcast.grp_ref, f32[9,56,128]{2,1,0:T(8,128)} %bitcast.18, f32[56,1152]{1,0:T(8,128)} %get-tuple-element.34.fl_ref, ...), custom_call_target="tpu_custom_call" | custom-call | tf_op jit(solution)/shard_map/pallas_call | solution.py:336
  31.5 1.9 %collective-permute-start.3 = (f32[216,128]{1,0:T(8,128)}, f32[216,128]{1,0:T(8,128)S(1)}, u32[]{:S(2)}, u32[]{:S(2)}) collective-permute-start(f32[216,128]{1,0:T(8,128)} %get-tuple-element.47), channel_id=1, source_target_pairs={{0,1},{1,2},{2,3},{3,4},{4,5},{5,6},{6,7},{7,8},{8,9},{9,10},{10,1... | collective-permute-start | bytes 331784 | tf_op jit(solution)/shard_map/ppermute | solution.py:279
  33.4 7.6 %collective-permute-start.4 = (f32[216,128]{1,0:T(8,128)}, f32[216,128]{1,0:T(8,128)S(1)}, u32[]{:S(2)}, u32[]{:S(2)}) collective-permute-start(f32[216,128]{1,0:T(8,128)} %get-tuple-element.48), channel_id=1, source_target_pairs={{1,0},{2,1},{3,2},{4,3},{5,4},{6,5},{7,6},{8,7},{9,8},{10,9},{11,1... | collective-permute-start | bytes 331784 | tf_op jit(solution)/shard_map/ppermute | solution.py:280
  41.0 1.9 %collective-permute-start.5 = (f32[216,128]{1,0:T(8,128)}, f32[216,128]{1,0:T(8,128)S(1)}, u32[]{:S(2)}, u32[]{:S(2)}) collective-permute-start(f32[216,128]{1,0:T(8,128)} %get-tuple-element.49), channel_id=1, source_target_pairs={{0,64},{64,128},{128,192},{192,256},{256,320},{320,384},{384,448},... | collective-permute-start | bytes 331784 | tf_op jit(solution)/shard_map/ppermute | solution.py:281
  43.0 10.4 %collective-permute-start.6 = (f32[216,128]{1,0:T(8,128)}, f32[216,128]{1,0:T(8,128)S(1)}, u32[]{:S(2)}, u32[]{:S(2)}) collective-permute-start(f32[216,128]{1,0:T(8,128)} %get-tuple-element.50), channel_id=1, source_target_pairs={{64,0},{128,64},{192,128},{256,192},{320,256},{384,320},{448,384},... | collective-permute-start | bytes 331784 | tf_op jit(solution)/shard_map/ppermute | solution.py:282
  53.4 4.2 %shard_map.103 = (f32[56,1152]{1,0:T(8,128)}, f32[96,1152]{1,0:T(8,128)}) custom-call(f32[56,1152]{1,0:T(8,128)} %get-tuple-element.42.base_ref, f32[56,1152]{1,0:T(8,128)} %get-tuple-element.43.integ_ref, f32[216,512]{1,0:T(8,128)} %get-tuple-element.44.own_ref, f32[9,9,3,128]{3,2,1,0:T(4,128)} %bitcast.11, f32[9,9,4,128]{3,2,1,0:T(4,128)} %bitcast.20, ...), custom_call_target="tpu_custom_call" | custom-call | tf_op jit(solution)/shard_map/pallas_call | solution.py:347
  57.6 0.0 collective-permute-done.3.r2lo
  57.7 0.0 collective-permute-done.4.r2hi
  57.7 0.0 collective-permute-done.5.r2glo
  57.7 0.6 copy-done
  58.3 0.0 copy-done.1
  58.3 0.0 copy-done.2
  58.4 0.0 copy-done.3
  58.4 3.5 %shard_map.104 = f32[9,56,128]{2,1,0:T(8,128)} custom-call(f32[56,1152]{1,0:T(8,128)} %get-tuple-element.45.bv_ref, f32[96,1152]{1,0:T(8,128)} %get-tuple-element.46.yp_ref, f32[216,128]{1,0:T(8,128)} %copy-done, f32[216,128]{1,0:T(8,128)} %copy-done.1, f32[216,128]{1,0:T(8,128)} %copy-done.2, f32[216,128]{1,0:T(8,128)} %copy-done.3, s32[4,128]{1,0:T(4,128)} %slot_ref.7, ...), custom_call_target="tpu_custom_call" | custom-call | tf_op jit(solution)/shard_map/pallas_call | solution.py:355
  (10 shorter events, 0.0 us)
Async XLA Ops:
  8.8 18.9 %collective-permute-start.1 = (f32[216,128]{1,0:T(8,128)}, f32[216,128]{1,0:T(8,128)S(1)}, u32[]{:S(2)}, u32[]{:S(2)}) collective-permute-start(f32[216,128]{1,0:T(8,128)} %get-tuple-element.31.s1lo), channel_id=1, source_target_pairs={{1,0},{2,1},{3,2},{4,3},{5,4},{6,5},{7,6},{8,7},{9,8},{10,9},{11,1... | collective-permute-start | bytes 331784 | tf_op jit(solution)/shard_map/ppermute | solution.py:290
  9.5 18.3 %collective-permute-start = (f32[216,128]{1,0:T(8,128)}, f32[216,128]{1,0:T(8,128)S(1)}, u32[]{:S(2)}, u32[]{:S(2)}) collective-permute-start(f32[216,128]{1,0:T(8,128)} %get-tuple-element.32.s1hi), channel_id=1, source_target_pairs={{0,1},{1,2},{2,3},{3,4},{4,5},{5,6},{6,7},{7,8},{8,9},{9,10},{10,1... | collective-permute-start | bytes 331784 | tf_op jit(solution)/shard_map/ppermute | solution.py:289
  10.1 17.6 %collective-permute-start.2 = (f32[216,128]{1,0:T(8,128)}, f32[216,128]{1,0:T(8,128)S(1)}, u32[]{:S(2)}, u32[]{:S(2)}) collective-permute-start(f32[216,128]{1,0:T(8,128)} %get-tuple-element.33.s1g), channel_id=1, source_target_pairs={{64,0},{65,1},{66,2},{67,3},{68,4},{69,5},{70,6},{71,7},{72,8},{73... | collective-permute-start | bytes 331784 | tf_op jit(solution)/shard_map/ppermute | solution.py:291
  27.7 0.7 %copy-start.4 = (f32[216,128]{1,0:T(8,128)}, f32[216,128]{1,0:T(8,128)S(1)}, u32[]{:S(2)}) copy-start(f32[216,128]{1,0:T(8,128)S(1)} %collective-permute-done.1.r1hi) | copy-start | bytes 331780
  27.7 0.7 %copy-start.5 = (f32[216,128]{1,0:T(8,128)}, f32[216,128]{1,0:T(8,128)S(1)}, u32[]{:S(2)}) copy-start(f32[216,128]{1,0:T(8,128)S(1)} %collective-permute-done.r1lo) | copy-start | bytes 331780
  27.8 0.7 %copy-start.6 = (f32[216,128]{1,0:T(8,128)}, f32[216,128]{1,0:T(8,128)S(1)}, u32[]{:S(2)}) copy-start(f32[216,128]{1,0:T(8,128)S(1)} %collective-permute-done.2.r1ghi) | copy-start | bytes 331780
  31.5 26.1 %collective-permute-start.3 = (f32[216,128]{1,0:T(8,128)}, f32[216,128]{1,0:T(8,128)S(1)}, u32[]{:S(2)}, u32[]{:S(2)}) collective-permute-start(f32[216,128]{1,0:T(8,128)} %get-tuple-element.47), channel_id=1, source_target_pairs={{0,1},{1,2},{2,3},{3,4},{4,5},{5,6},{6,7},{7,8},{8,9},{9,10},{10,1... | collective-permute-start | bytes 331784 | tf_op jit(solution)/shard_map/ppermute | solution.py:279
  33.4 24.2 %collective-permute-start.4 = (f32[216,128]{1,0:T(8,128)}, f32[216,128]{1,0:T(8,128)S(1)}, u32[]{:S(2)}, u32[]{:S(2)}) collective-permute-start(f32[216,128]{1,0:T(8,128)} %get-tuple-element.48), channel_id=1, source_target_pairs={{1,0},{2,1},{3,2},{4,3},{5,4},{6,5},{7,6},{8,7},{9,8},{10,9},{11,1... | collective-permute-start | bytes 331784 | tf_op jit(solution)/shard_map/ppermute | solution.py:280
  41.0 16.6 %collective-permute-start.5 = (f32[216,128]{1,0:T(8,128)}, f32[216,128]{1,0:T(8,128)S(1)}, u32[]{:S(2)}, u32[]{:S(2)}) collective-permute-start(f32[216,128]{1,0:T(8,128)} %get-tuple-element.49), channel_id=1, source_target_pairs={{0,64},{64,128},{128,192},{192,256},{256,320},{320,384},{384,448},... | collective-permute-start | bytes 331784 | tf_op jit(solution)/shard_map/ppermute | solution.py:281
  43.0 14.7 %collective-permute-start.6 = (f32[216,128]{1,0:T(8,128)}, f32[216,128]{1,0:T(8,128)S(1)}, u32[]{:S(2)}, u32[]{:S(2)}) collective-permute-start(f32[216,128]{1,0:T(8,128)} %get-tuple-element.50), channel_id=1, source_target_pairs={{64,0},{128,64},{192,128},{256,192},{320,256},{384,320},{448,384},... | collective-permute-start | bytes 331784 | tf_op jit(solution)/shard_map/ppermute | solution.py:282
  57.6 0.6 %copy-start = (f32[216,128]{1,0:T(8,128)}, f32[216,128]{1,0:T(8,128)S(1)}, u32[]{:S(2)}) copy-start(f32[216,128]{1,0:T(8,128)S(1)} %collective-permute-done.3.r2lo) | copy-start | bytes 331780
  57.7 0.7 %copy-start.1 = (f32[216,128]{1,0:T(8,128)}, f32[216,128]{1,0:T(8,128)S(1)}, u32[]{:S(2)}) copy-start(f32[216,128]{1,0:T(8,128)S(1)} %collective-permute-done.4.r2hi) | copy-start | bytes 331780
  57.7 0.7 %copy-start.2 = (f32[216,128]{1,0:T(8,128)}, f32[216,128]{1,0:T(8,128)S(1)}, u32[]{:S(2)}) copy-start(f32[216,128]{1,0:T(8,128)S(1)} %collective-permute-done.5.r2glo) | copy-start | bytes 331780
  57.7 0.7 %copy-start.3 = (f32[216,128]{1,0:T(8,128)}, f32[216,128]{1,0:T(8,128)S(1)}, u32[]{:S(2)}) copy-start(f32[216,128]{1,0:T(8,128)S(1)} %collective-permute-done.6.r2ghi) | copy-start | bytes 331780

commit v5 on v4

--- a/solution.py
+++ b/solution.py
@@ -105,7 +105,7 @@
 
 def _send(tables, send_ref, outs):
     rows = lax.broadcasted_iota(jnp.int32, (4 * E, 3 * E), 0)
-    onehot = jnp.where(rows == send_ref[...], 1.0, 0.0).astype(BF)
+    onehot = jnp.where(rows == send_ref[...].reshape(1, 3 * E), 1.0, 0.0).astype(BF)
     s = _sel(_split3(jnp.concatenate(tables, axis=0)), onehot)
     for i, (lo_ref, hi_ref, g_ref) in enumerate(outs):
         blk = s[i * TR:(i + 1) * TR]
@@ -193,14 +193,16 @@
                stiff_ref, trace_ref, send_ref, slot_ref, face_ref,
                fl_ref, t1l_ref, plo, phi, pg, slg, bv_ref, yp_ref,
                tl_ref, yt_ref, sllo, slhi, a_ref, v_ref, g_ref):
-    later = later_ref[...]
-    fl_ref[...] = first_ref[...] + later
-    _table(later, _split2(_rows84(trace_ref)), yt_ref, tl_ref)
-    t1l_ref[...] = t1_ref[...] + tl_ref[...]
-    _send([tl_ref[...]], send_ref, [(sllo, slhi, slg)])
-    plo[...] = s1lo[...] + sllo[...]
-    phi[...] = s1hi[...] + slhi[...]
-    pg[...] = s1g[...] + slg[...]
+    @pl.when(grp_ref[0] != 0)
+    def _():
+        later = later_ref[...]
+        fl_ref[...] = first_ref[...] + later
+        _table(later, _split2(_rows84(trace_ref)), yt_ref, tl_ref)
+        t1l_ref[...] = t1_ref[...] + tl_ref[...]
+        _send([tl_ref[...]], send_ref, [(sllo, slhi, slg)])
+        plo[...] = s1lo[...] + sllo[...]
+        phi[...] = s1hi[...] + slhi[...]
+        pg[...] = s1g[...] + slg[...]
 
     @pl.when(grp_ref[0] == 0)
     def _():
@@ -300,7 +302,7 @@
     flux_nbr = jnp.transpose(flux_nbr, (1, 2, 0, 3))
     trace = jnp.transpose(trace, (1, 0, 2))
     lift = jnp.transpose(lift, (2, 0, 1))
-    send = send_slot.reshape(1, 3 * E)
+    send = send_slot
 
     field = _sds((NQ, NB, E))
     flat = _sds((NB, LN))

time: 62.3 us -> 61 us (0.979)
  local copies, waits for them, and re-layouts: 2.59 us -> 1.37 us
    reshape x1 -> x0, local copies, waits for them, and re-layouts: 1.22 us -> none  [local(): send = send_slot.reshape(1, 3 * E)]
where the time goes in v5:
time: 61 us; the launch traced here: 60.7 us
  starting transfers between devices  37 us (61%)
  Pallas kernels  22.1 us (36%)
  local copies, waits for them, and re-layouts  1.37 us (2%)
    ppermute x1, starting transfers between devices, exchange_fault(): from_ghi = lax.ppermute(g, axes, [(n_dom + i, i) for i in range(n_dom)])  13.9 us
    ppermute x1, starting transfers between devices, exchange(): from_ghi = lax.ppermute(gdn, 'grp', [(i + 1, i) for i in range(n_grp - 1)])  10.4 us
    ppermute x1, starting transfers between devices, exchange(): from_hi = lax.ppermute(lo, 'dom', [(i + 1, i) for i in range(n_dom - 1)])  7.59 us
    pallas_call x1, Pallas kernels, local(): pl.pallas_call(_kernel_a1, out_shape=(flat, flat, table, part, part, part...  7.58 us
    pallas_call x1, Pallas kernels, local(): pl.pallas_call(_kernel_b2, out_shape=(flat, yflux), in_specs=[_vmem()] *...  4.25 us
    pallas_call x1, Pallas kernels, local(): pl.pallas_call(_kernel_a2, out_shape=(flat, table, part, part, part, part...  3.71 us
    pallas_call x1, Pallas kernels, local(): pl.pallas_call(_kernel_c, out_shape=field, in_specs=[_vmem()] * 10, out_s...  3.47 us
    pallas_call x1, Pallas kernels, local(): pl.pallas_call(_kernel_b, out_shape=(flat, flat, table, part, part, part,...  3.09 us
  transfers between devices with their start and end apart: 7, of which 0 were waited for; matrix products, arithmetic and copies ran while one was open for 0% of the time, Pallas kernels for 13%

profile of v5, /device:TPU:24, one launch (start us, length us, event | category | flops | bytes accessed | tf_op | source)
XLA Modules:
  0.0 60.7 jit_solution(13564094288000620229)
XLA Ops:
  0.0 7.6 %shard_map.100 = (f32[56,1152]{1,0:T(8,128)}, f32[56,1152]{1,0:T(8,128)}, f32[216,512]{1,0:T(8,128)}, f32[216,128]{1,0:T(8,128)}, f32[216,128]{1,0:T(8,128)}, /*index=5*/f32[216,128]{1,0:T(8,128)}) custom-call(f32[9,56,128]{2,1,0:T(8,128)} %bitcast.16, f32[9,9,3,128]{3,2,1,0:T(4,128)} %bitcast.12, f32[3,56,56]{2,1,0:T(8,128)} %stiff_ref.7, ...), custom_call_target="tpu_custom_call" | custom-call | tf_op jit(solution)/shard_map/pallas_call | solution.py:319
  7.6 0.7 %collective-permute-start.1 = (f32[216,128]{1,0:T(8,128)}, f32[216,128]{1,0:T(8,128)S(1)}, u32[]{:S(2)}, u32[]{:S(2)}) collective-permute-start(f32[216,128]{1,0:T(8,128)} %get-tuple-element.31.s1lo), channel_id=1, source_target_pairs={{1,0},{2,1},{3,2},{4,3},{5,4},{6,5},{7,6},{8,7},{9,8},{10,9},{11,1... | collective-permute-start | bytes 331784 | tf_op jit(solution)/shard_map/ppermute | solution.py:292
  8.2 0.7 %collective-permute-start = (f32[216,128]{1,0:T(8,128)}, f32[216,128]{1,0:T(8,128)S(1)}, u32[]{:S(2)}, u32[]{:S(2)}) collective-permute-start(f32[216,128]{1,0:T(8,128)} %get-tuple-element.32.s1hi), channel_id=1, source_target_pairs={{0,1},{1,2},{2,3},{3,4},{4,5},{5,6},{6,7},{7,8},{8,9},{9,10},{10,1... | collective-permute-start | bytes 331784 | tf_op jit(solution)/shard_map/ppermute | solution.py:291
  8.9 13.9 %collective-permute-start.2 = (f32[216,128]{1,0:T(8,128)}, f32[216,128]{1,0:T(8,128)S(1)}, u32[]{:S(2)}, u32[]{:S(2)}) collective-permute-start(f32[216,128]{1,0:T(8,128)} %get-tuple-element.33.s1g), channel_id=1, source_target_pairs={{64,0},{65,1},{66,2},{67,3},{68,4},{69,5},{70,6},{71,7},{72,8},{73... | collective-permute-start | bytes 331784 | tf_op jit(solution)/shard_map/ppermute | solution.py:293
  22.8 3.7 %shard_map.101 = (f32[56,1152]{1,0:T(8,128)}, f32[216,512]{1,0:T(8,128)}, f32[216,128]{1,0:T(8,128)}, f32[216,128]{1,0:T(8,128)}, f32[216,128]{1,0:T(8,128)}, /*...) custom-call(s32[1]{0:T(128)} %bitcast.grp_ref, f32[9,56,128]{2,1,0:T(8,128)} %bitcast.17, ...), custom_call_target="tpu_custom_call" | custom-call | tf_op jit(solution)/shard_map/pallas_call | solution.py:329
  26.5 0.0 collective-permute-done.1.r1hi
  26.5 0.0 collective-permute-done.r1lo
  26.5 0.0 collective-permute-done.2.r1ghi
  26.6 0.6 %copy-done.4 = f32[216,128]{1,0:T(8,128)} copy-done((f32[216,128]{1,0:T(8,128)}, f32[216,128]{1,0:T(8,128)S(1)}, u32[]{:S(2)}) %copy-start.4) | copy-done | bytes 110616
  27.2 0.0 copy-done.5
  27.2 0.0 copy-done.6
  27.2 3.1 %shard_map.102 = (f32[56,1152]{1,0:T(8,128)}, f32[56,1152]{1,0:T(8,128)}, f32[216,512]{1,0:T(8,128)}, f32[216,128]{1,0:T(8,128)}, f32[216,128]{1,0:T(8,128)}, /*index=5*/f32[216,128]{1,0:T(8,128)}, f32[216,128]{1,0:T(8,128)}) custom-call(s32[1]{0:T(128)} %bitcast.grp_ref, f32[9,56,128]{2,1,0:T(8,128)} %bitcast.18, f32[56,1152]{1,0:T(8,128)} %get-tuple-element.34.fl_ref, ...), custom_call_target="tpu_custom_call" | custom-call | tf_op jit(solution)/shard_map/pallas_call | solution.py:338
  30.3 1.9 %collective-permute-start.3 = (f32[216,128]{1,0:T(8,128)}, f32[216,128]{1,0:T(8,128)S(1)}, u32[]{:S(2)}, u32[]{:S(2)}) collective-permute-start(f32[216,128]{1,0:T(8,128)} %get-tuple-element.47), channel_id=1, source_target_pairs={{0,1},{1,2},{2,3},{3,4},{4,5},{5,6},{6,7},{7,8},{8,9},{9,10},{10,1... | collective-permute-start | bytes 331784 | tf_op jit(solution)/shard_map/ppermute | solution.py:281
  32.2 7.6 %collective-permute-start.4 = (f32[216,128]{1,0:T(8,128)}, f32[216,128]{1,0:T(8,128)S(1)}, u32[]{:S(2)}, u32[]{:S(2)}) collective-permute-start(f32[216,128]{1,0:T(8,128)} %get-tuple-element.48), channel_id=1, source_target_pairs={{1,0},{2,1},{3,2},{4,3},{5,4},{6,5},{7,6},{8,7},{9,8},{10,9},{11,1... | collective-permute-start | bytes 331784 | tf_op jit(solution)/shard_map/ppermute | solution.py:282
  39.8 1.9 %collective-permute-start.5 = (f32[216,128]{1,0:T(8,128)}, f32[216,128]{1,0:T(8,128)S(1)}, u32[]{:S(2)}, u32[]{:S(2)}) collective-permute-start(f32[216,128]{1,0:T(8,128)} %get-tuple-element.49), channel_id=1, source_target_pairs={{0,64},{64,128},{128,192},{192,256},{256,320},{320,384},{384,448},... | collective-permute-start | bytes 331784 | tf_op jit(solution)/shard_map/ppermute | solution.py:283
  41.8 10.4 %collective-permute-start.6 = (f32[216,128]{1,0:T(8,128)}, f32[216,128]{1,0:T(8,128)S(1)}, u32[]{:S(2)}, u32[]{:S(2)}) collective-permute-start(f32[216,128]{1,0:T(8,128)} %get-tuple-element.50), channel_id=1, source_target_pairs={{64,0},{128,64},{192,128},{256,192},{320,256},{384,320},{448,384},... | collective-permute-start | bytes 331784 | tf_op jit(solution)/shard_map/ppermute | solution.py:284
  52.2 4.2 %shard_map.103 = (f32[56,1152]{1,0:T(8,128)}, f32[96,1152]{1,0:T(8,128)}) custom-call(f32[56,1152]{1,0:T(8,128)} %get-tuple-element.42.base_ref, f32[56,1152]{1,0:T(8,128)} %get-tuple-element.43.integ_ref, f32[216,512]{1,0:T(8,128)} %get-tuple-element.44.own_ref, f32[9,9,3,128]{3,2,1,0:T(4,128)} %bitcast.15, f32[9,9,4,128]{3,2,1,0:T(4,128)} %bitcast.20, ...), custom_call_target="tpu_custom_call" | custom-call | tf_op jit(solution)/shard_map/pallas_call | solution.py:349
  56.4 0.0 collective-permute-done.4.r2hi
  56.5 0.0 collective-permute-done.6.r2ghi
  56.5 0.6 copy-done
  57.1 0.0 copy-done.1
  57.1 0.0 copy-done.2
  57.2 0.0 copy-done.3
  57.2 3.5 %shard_map.104 = f32[9,56,128]{2,1,0:T(8,128)} custom-call(f32[56,1152]{1,0:T(8,128)} %get-tuple-element.45.bv_ref, f32[96,1152]{1,0:T(8,128)} %get-tuple-element.46.yp_ref, f32[216,128]{1,0:T(8,128)} %copy-done, f32[216,128]{1,0:T(8,128)} %copy-done.1, f32[216,128]{1,0:T(8,128)} %copy-done.2, f32[216,128]{1,0:T(8,128)} %copy-done.3, s32[4,128]{1,0:T(4,128)} %slot_ref.7, ...), custom_call_target="tpu_custom_call" | custom-call | tf_op jit(solution)/shard_map/pallas_call | solution.py:357
  (9 shorter events, 0.0 us)
Async XLA Ops:
  7.6 18.9 %collective-permute-start.1 = (f32[216,128]{1,0:T(8,128)}, f32[216,128]{1,0:T(8,128)S(1)}, u32[]{:S(2)}, u32[]{:S(2)}) collective-permute-start(f32[216,128]{1,0:T(8,128)} %get-tuple-element.31.s1lo), channel_id=1, source_target_pairs={{1,0},{2,1},{3,2},{4,3},{5,4},{6,5},{7,6},{8,7},{9,8},{10,9},{11,1... | collective-permute-start | bytes 331784 | tf_op jit(solution)/shard_map/ppermute | solution.py:292
  8.2 18.3 %collective-permute-start = (f32[216,128]{1,0:T(8,128)}, f32[216,128]{1,0:T(8,128)S(1)}, u32[]{:S(2)}, u32[]{:S(2)}) collective-permute-start(f32[216,128]{1,0:T(8,128)} %get-tuple-element.32.s1hi), channel_id=1, source_target_pairs={{0,1},{1,2},{2,3},{3,4},{4,5},{5,6},{6,7},{7,8},{8,9},{9,10},{10,1... | collective-permute-start | bytes 331784 | tf_op jit(solution)/shard_map/ppermute | solution.py:291
  8.9 17.6 %collective-permute-start.2 = (f32[216,128]{1,0:T(8,128)}, f32[216,128]{1,0:T(8,128)S(1)}, u32[]{:S(2)}, u32[]{:S(2)}) collective-permute-start(f32[216,128]{1,0:T(8,128)} %get-tuple-element.33.s1g), channel_id=1, source_target_pairs={{64,0},{65,1},{66,2},{67,3},{68,4},{69,5},{70,6},{71,7},{72,8},{73... | collective-permute-start | bytes 331784 | tf_op jit(solution)/shard_map/ppermute | solution.py:293
  26.5 0.7 %copy-start.4 = (f32[216,128]{1,0:T(8,128)}, f32[216,128]{1,0:T(8,128)S(1)}, u32[]{:S(2)}) copy-start(f32[216,128]{1,0:T(8,128)S(1)} %collective-permute-done.1.r1hi) | copy-start | bytes 331780
  26.5 0.7 %copy-start.5 = (f32[216,128]{1,0:T(8,128)}, f32[216,128]{1,0:T(8,128)S(1)}, u32[]{:S(2)}) copy-start(f32[216,128]{1,0:T(8,128)S(1)} %collective-permute-done.r1lo) | copy-start | bytes 331780
  26.6 0.7 %copy-start.6 = (f32[216,128]{1,0:T(8,128)}, f32[216,128]{1,0:T(8,128)S(1)}, u32[]{:S(2)}) copy-start(f32[216,128]{1,0:T(8,128)S(1)} %collective-permute-done.2.r1ghi) | copy-start | bytes 331780
  30.3 26.1 %collective-permute-start.3 = (f32[216,128]{1,0:T(8,128)}, f32[216,128]{1,0:T(8,128)S(1)}, u32[]{:S(2)}, u32[]{:S(2)}) collective-permute-start(f32[216,128]{1,0:T(8,128)} %get-tuple-element.47), channel_id=1, source_target_pairs={{0,1},{1,2},{2,3},{3,4},{4,5},{5,6},{6,7},{7,8},{8,9},{9,10},{10,1... | collective-permute-start | bytes 331784 | tf_op jit(solution)/shard_map/ppermute | solution.py:281
  32.2 24.2 %collective-permute-start.4 = (f32[216,128]{1,0:T(8,128)}, f32[216,128]{1,0:T(8,128)S(1)}, u32[]{:S(2)}, u32[]{:S(2)}) collective-permute-start(f32[216,128]{1,0:T(8,128)} %get-tuple-element.48), channel_id=1, source_target_pairs={{1,0},{2,1},{3,2},{4,3},{5,4},{6,5},{7,6},{8,7},{9,8},{10,9},{11,1... | collective-permute-start | bytes 331784 | tf_op jit(solution)/shard_map/ppermute | solution.py:282
  39.8 16.6 %collective-permute-start.5 = (f32[216,128]{1,0:T(8,128)}, f32[216,128]{1,0:T(8,128)S(1)}, u32[]{:S(2)}, u32[]{:S(2)}) collective-permute-start(f32[216,128]{1,0:T(8,128)} %get-tuple-element.49), channel_id=1, source_target_pairs={{0,64},{64,128},{128,192},{192,256},{256,320},{320,384},{384,448},... | collective-permute-start | bytes 331784 | tf_op jit(solution)/shard_map/ppermute | solution.py:283
  41.8 14.7 %collective-permute-start.6 = (f32[216,128]{1,0:T(8,128)}, f32[216,128]{1,0:T(8,128)S(1)}, u32[]{:S(2)}, u32[]{:S(2)}) collective-permute-start(f32[216,128]{1,0:T(8,128)} %get-tuple-element.50), channel_id=1, source_target_pairs={{64,0},{128,64},{192,128},{256,192},{320,256},{384,320},{448,384},... | collective-permute-start | bytes 331784 | tf_op jit(solution)/shard_map/ppermute | solution.py:284
  56.4 0.6 %copy-start = (f32[216,128]{1,0:T(8,128)}, f32[216,128]{1,0:T(8,128)S(1)}, u32[]{:S(2)}) copy-start(f32[216,128]{1,0:T(8,128)S(1)} %collective-permute-done.3.r2lo) | copy-start | bytes 331780
  56.5 0.7 %copy-start.1 = (f32[216,128]{1,0:T(8,128)}, f32[216,128]{1,0:T(8,128)S(1)}, u32[]{:S(2)}) copy-start(f32[216,128]{1,0:T(8,128)S(1)} %collective-permute-done.4.r2hi) | copy-start | bytes 331780
  56.5 0.7 %copy-start.2 = (f32[216,128]{1,0:T(8,128)}, f32[216,128]{1,0:T(8,128)S(1)}, u32[]{:S(2)}) copy-start(f32[216,128]{1,0:T(8,128)S(1)} %collective-permute-done.5.r2glo) | copy-start | bytes 331780
  56.5 0.7 %copy-start.3 = (f32[216,128]{1,0:T(8,128)}, f32[216,128]{1,0:T(8,128)S(1)}, u32[]{:S(2)}) copy-start(f32[216,128]{1,0:T(8,128)S(1)} %collective-permute-done.6.r2ghi) | copy-start | bytes 331780

commit v6 on v5

--- a/solution.py
+++ b/solution.py
@@ -48,6 +48,16 @@
 
 def _rows84(ref):
     return jnp.concatenate([ref[r] for r in range(NF)], axis=0)
+
+
+def _lhs3(a):
+    h, l = _split2(jnp.concatenate([a, jnp.zeros((a.shape[0], 8), F32)], axis=1))
+    return jnp.concatenate([h, h, l], axis=1)
+
+
+def _rhs3(x):
+    h, l = _split2(jnp.concatenate([x, jnp.zeros((8, x.shape[1]), F32)], axis=0))
+    return jnp.concatenate([h, l, h], axis=0)
 
 
 def _split3(x):
@@ -86,7 +96,7 @@
         ref[...] = w[0] * x
     d_ref[...] = x
     for k in range(ORDER - 1):
-        a_ref[...] = _dot3(stiff_p, _split2(d_ref[...]))
+        a_ref[...] = _bdot(stiff_p, _rhs3(d_ref[...]))
         _mix_vol(a_ref, star_ref, d_ref, -1)
         dn = d_ref[...]
         for ref, w in accs:
@@ -94,7 +104,7 @@
 
 
 def _table(x, trace_p, yt_ref, t_ref):
-    yt = _dot3(trace_p, _split2(x))
+    yt = _bdot(trace_p, _rhs3(x))
     for p in range(NQ):
         yt_ref[p] = yt[:, p * E:(p + 1) * E]
     t_ref[...] = jnp.zeros(t_ref.shape, F32)
@@ -181,11 +191,11 @@
                d_ref, a_ref, acc1_ref, acc2_ref, yt_ref):
     x = _load_field(x_ref)
     stiff_st = jnp.concatenate([stiff_ref[d] for d in range(3)], axis=0)
-    _taylor(x, star_ref, _split2(stiff_st), d_ref, a_ref, [(acc1_ref, W_FIRST), (acc2_ref, W_LATER)])
+    _taylor(x, star_ref, _lhs3(stiff_st), d_ref, a_ref, [(acc1_ref, W_FIRST), (acc2_ref, W_LATER)])
     first = acc1_ref[...]
     first_ref[...] = first
     later_ref[...] = acc2_ref[...]
-    _table(first, _split2(_rows84(trace_ref)), yt_ref, t1_ref)
+    _table(first, _lhs3(_rows84(trace_ref)), yt_ref, t1_ref)
     _send([t1_ref[...]], send_ref, [(s1lo, s1hi, s1g)])
 
 
@@ -197,7 +207,7 @@
     def _():
         later = later_ref[...]
         fl_ref[...] = first_ref[...] + later
-        _table(later, _split2(_rows84(trace_ref)), yt_ref, tl_ref)
+        _table(later, _lhs3(_rows84(trace_ref)), yt_ref, tl_ref)
         t1l_ref[...] = t1_ref[...] + tl_ref[...]
         _send([tl_ref[...]], send_ref, [(sllo, slhi, slg)])
         plo[...] = s1lo[...] + sllo[...]
@@ -224,10 +234,10 @@
                       g_ref, yf_ref)
         base_ref[...] = mid
         stiff_st = jnp.concatenate([stiff_ref[d] for d in range(3)], axis=0)
-        _taylor(mid, star_ref, _split2(stiff_st), d_ref, a_ref, [(acc_ref, W_FIRST)])
+        _taylor(mid, star_ref, _lhs3(stiff_st), d_ref, a_ref, [(acc_ref, W_FIRST)])
         second = acc_ref[...]
         integ_ref[...] = second
-        _table(second, _split2(_rows84(trace_ref)), yt_ref, own_ref)
+        _table(second, _lhs3(_rows84(trace_ref)), yt_ref, own_ref)
         _send([own_ref[...]], send_ref, [(elo, ehi, egdn)])
         egup[...] = s1g[...] + egdn[...]
 

time: 61 us -> 57.7 us (0.946)
  starting transfers between devices: 37 us -> 35.3 us
  Pallas kernels: 22.1 us -> 20.5 us
    ppermute x1, starting transfers between devices: 10.4 us -> 8.68 us  [exchange(): from_ghi = lax.ppermute(gdn, 'grp', [(i + 1, i) for i in range(n_grp - 1)])]
    pallas_call x1, Pallas kernels: 7.58 us -> 6.03 us  [local(): pl.pallas_call(_kernel_a1, out_shape=(flat, flat, table, part, part, part...]
  transfers between devices with their start and end apart: 7 -> 7, of which waited for: 0 -> 0; matrix products, arithmetic and copies ran while one was open for 0% -> 0% of each run, Pallas kernels for 13% -> 14%
where the time goes in v6:
time: 57.7 us; the launch traced here: 57.3 us
  starting transfers between devices  35.3 us (61%)
  Pallas kernels  20.5 us (36%)
  local copies, waits for them, and re-layouts  1.37 us (2%)
    ppermute x1, starting transfers between devices, exchange_fault(): from_ghi = lax.ppermute(g, axes, [(n_dom + i, i) for i in range(n_dom)])  13.8 us
    ppermute x1, starting transfers between devices, exchange(): from_ghi = lax.ppermute(gdn, 'grp', [(i + 1, i) for i in range(n_grp - 1)])  8.68 us
    ppermute x1, starting transfers between devices, exchange(): from_hi = lax.ppermute(lo, 'dom', [(i + 1, i) for i in range(n_dom - 1)])  7.58 us
    pallas_call x1, Pallas kernels, local(): pl.pallas_call(_kernel_a1, out_shape=(flat, flat, table, part, part, part...  6.03 us
    pallas_call x1, Pallas kernels, local(): pl.pallas_call(_kernel_b2, out_shape=(flat, yflux), in_specs=[_vmem()] *...  4.25 us
    pallas_call x1, Pallas kernels, local(): pl.pallas_call(_kernel_a2, out_shape=(flat, table, part, part, part, part...  3.66 us
    pallas_call x1, Pallas kernels, local(): pl.pallas_call(_kernel_c, out_shape=field, in_specs=[_vmem()] * 10, out_s...  3.46 us
    pallas_call x1, Pallas kernels, local(): pl.pallas_call(_kernel_b, out_shape=(flat, flat, table, part, part, part,...  3.09 us
  transfers between devices with their start and end apart: 7, of which 0 were waited for; matrix products, arithmetic and copies ran while one was open for 0% of the time, Pallas kernels for 14%

profile of v6, /device:TPU:24, one launch (start us, length us, event | category | flops | bytes accessed | tf_op | source)
XLA Modules:
  0.0 57.3 jit_solution(459117193143919107)
XLA Ops:
  0.0 6.0 %shard_map.100 = (f32[56,1152]{1,0:T(8,128)}, f32[56,1152]{1,0:T(8,128)}, f32[216,512]{1,0:T(8,128)}, f32[216,128]{1,0:T(8,128)}, f32[216,128]{1,0:T(8,128)}, /*index=5*/f32[216,128]{1,0:T(8,128)}) custom-call(f32[9,56,128]{2,1,0:T(8,128)} %bitcast.16, f32[9,9,3,128]{3,2,1,0:T(4,128)} %bitcast.12, f32[3,56,56]{2,1,0:T(8,128)} %stiff_ref.7, ...), custom_call_target="tpu_custom_call" | custom-call | tf_op jit(solution)/shard_map/pallas_call | solution.py:329
  6.0 0.7 %collective-permute-start.1 = (f32[216,128]{1,0:T(8,128)}, f32[216,128]{1,0:T(8,128)S(1)}, u32[]{:S(2)}, u32[]{:S(2)}) collective-permute-start(f32[216,128]{1,0:T(8,128)} %get-tuple-element.31.s1lo), channel_id=1, source_target_pairs={{1,0},{2,1},{3,2},{4,3},{5,4},{6,5},{7,6},{8,7},{9,8},{10,9},{11,1... | collective-permute-start | bytes 331784 | tf_op jit(solution)/shard_map/ppermute | solution.py:302
  6.7 0.7 %collective-permute-start = (f32[216,128]{1,0:T(8,128)}, f32[216,128]{1,0:T(8,128)S(1)}, u32[]{:S(2)}, u32[]{:S(2)}) collective-permute-start(f32[216,128]{1,0:T(8,128)} %get-tuple-element.32.s1hi), channel_id=1, source_target_pairs={{0,1},{1,2},{2,3},{3,4},{4,5},{5,6},{6,7},{7,8},{8,9},{9,10},{10,1... | collective-permute-start | bytes 331784 | tf_op jit(solution)/shard_map/ppermute | solution.py:301
  7.4 13.8 %collective-permute-start.2 = (f32[216,128]{1,0:T(8,128)}, f32[216,128]{1,0:T(8,128)S(1)}, u32[]{:S(2)}, u32[]{:S(2)}) collective-permute-start(f32[216,128]{1,0:T(8,128)} %get-tuple-element.33.s1g), channel_id=1, source_target_pairs={{64,0},{65,1},{66,2},{67,3},{68,4},{69,5},{70,6},{71,7},{72,8},{73... | collective-permute-start | bytes 331784 | tf_op jit(solution)/shard_map/ppermute | solution.py:303
  21.2 3.7 %shard_map.101 = (f32[56,1152]{1,0:T(8,128)}, f32[216,512]{1,0:T(8,128)}, f32[216,128]{1,0:T(8,128)}, f32[216,128]{1,0:T(8,128)}, f32[216,128]{1,0:T(8,128)}, /*...) custom-call(s32[1]{0:T(128)} %bitcast.grp_ref, f32[9,56,128]{2,1,0:T(8,128)} %bitcast.17, ...), custom_call_target="tpu_custom_call" | custom-call | tf_op jit(solution)/shard_map/pallas_call | solution.py:339
  24.9 0.0 collective-permute-done.1.r1hi
  24.9 0.0 collective-permute-done.r1lo
  24.9 0.0 collective-permute-done.2.r1ghi
  24.9 0.6 %copy-done.4 = f32[216,128]{1,0:T(8,128)} copy-done((f32[216,128]{1,0:T(8,128)}, f32[216,128]{1,0:T(8,128)S(1)}, u32[]{:S(2)}) %copy-start.4) | copy-done | bytes 110616
  25.6 0.0 copy-done.5
  25.6 0.0 copy-done.6
  25.6 3.1 %shard_map.102 = (f32[56,1152]{1,0:T(8,128)}, f32[56,1152]{1,0:T(8,128)}, f32[216,512]{1,0:T(8,128)}, f32[216,128]{1,0:T(8,128)}, f32[216,128]{1,0:T(8,128)}, /*index=5*/f32[216,128]{1,0:T(8,128)}, f32[216,128]{1,0:T(8,128)}) custom-call(s32[1]{0:T(128)} %bitcast.grp_ref, f32[9,56,128]{2,1,0:T(8,128)} %bitcast.18, f32[56,1152]{1,0:T(8,128)} %get-tuple-element.34.fl_ref, ...), custom_call_target="tpu_custom_call" | custom-call | tf_op jit(solution)/shard_map/pallas_call | solution.py:348
  28.7 1.9 %collective-permute-start.3 = (f32[216,128]{1,0:T(8,128)}, f32[216,128]{1,0:T(8,128)S(1)}, u32[]{:S(2)}, u32[]{:S(2)}) collective-permute-start(f32[216,128]{1,0:T(8,128)} %get-tuple-element.47), channel_id=1, source_target_pairs={{0,1},{1,2},{2,3},{3,4},{4,5},{5,6},{6,7},{7,8},{8,9},{9,10},{10,1... | collective-permute-start | bytes 331784 | tf_op jit(solution)/shard_map/ppermute | solution.py:291
  30.6 7.6 %collective-permute-start.4 = (f32[216,128]{1,0:T(8,128)}, f32[216,128]{1,0:T(8,128)S(1)}, u32[]{:S(2)}, u32[]{:S(2)}) collective-permute-start(f32[216,128]{1,0:T(8,128)} %get-tuple-element.48), channel_id=1, source_target_pairs={{1,0},{2,1},{3,2},{4,3},{5,4},{6,5},{7,6},{8,7},{9,8},{10,9},{11,1... | collective-permute-start | bytes 331784 | tf_op jit(solution)/shard_map/ppermute | solution.py:292
  38.2 1.9 %collective-permute-start.5 = (f32[216,128]{1,0:T(8,128)}, f32[216,128]{1,0:T(8,128)S(1)}, u32[]{:S(2)}, u32[]{:S(2)}) collective-permute-start(f32[216,128]{1,0:T(8,128)} %get-tuple-element.49), channel_id=1, source_target_pairs={{0,64},{64,128},{128,192},{192,256},{256,320},{320,384},{384,448},... | collective-permute-start | bytes 331784 | tf_op jit(solution)/shard_map/ppermute | solution.py:293
  40.1 8.7 %collective-permute-start.6 = (f32[216,128]{1,0:T(8,128)}, f32[216,128]{1,0:T(8,128)S(1)}, u32[]{:S(2)}, u32[]{:S(2)}) collective-permute-start(f32[216,128]{1,0:T(8,128)} %get-tuple-element.50), channel_id=1, source_target_pairs={{64,0},{128,64},{192,128},{256,192},{320,256},{384,320},{448,384},... | collective-permute-start | bytes 331784 | tf_op jit(solution)/shard_map/ppermute | solution.py:294
  48.8 4.2 %shard_map.103 = (f32[56,1152]{1,0:T(8,128)}, f32[96,1152]{1,0:T(8,128)}) custom-call(f32[56,1152]{1,0:T(8,128)} %get-tuple-element.42.base_ref, f32[56,1152]{1,0:T(8,128)} %get-tuple-element.43.integ_ref, f32[216,512]{1,0:T(8,128)} %get-tuple-element.44.own_ref, f32[9,9,3,128]{3,2,1,0:T(4,128)} %bitcast.15, f32[9,9,4,128]{3,2,1,0:T(4,128)} %bitcast.20, ...), custom_call_target="tpu_custom_call" | custom-call | tf_op jit(solution)/shard_map/pallas_call | solution.py:359
  53.1 0.0 collective-permute-done.3.r2lo
  53.1 0.0 collective-permute-done.4.r2hi
  53.1 0.6 %copy-done = f32[216,128]{1,0:T(8,128)} copy-done((f32[216,128]{1,0:T(8,128)}, f32[216,128]{1,0:T(8,128)S(1)}, u32[]{:S(2)}) %copy-start) | copy-done | bytes 110616
  53.7 0.0 copy-done.1
  53.8 0.0 copy-done.2
  53.8 0.0 copy-done.3
  53.8 3.5 %shard_map.104 = f32[9,56,128]{2,1,0:T(8,128)} custom-call(f32[56,1152]{1,0:T(8,128)} %get-tuple-element.45.bv_ref, f32[96,1152]{1,0:T(8,128)} %get-tuple-element.46.yp_ref, f32[216,128]{1,0:T(8,128)} %copy-done, f32[216,128]{1,0:T(8,128)} %copy-done.1, f32[216,128]{1,0:T(8,128)} %copy-done.2, f32[216,128]{1,0:T(8,128)} %copy-done.3, s32[4,128]{1,0:T(4,128)} %slot_ref.7, ...), custom_call_target="tpu_custom_call" | custom-call | tf_op jit(solution)/shard_map/pallas_call | solution.py:367
  (9 shorter events, 0.0 us)
Async XLA Ops:
  6.0 18.9 %collective-permute-start.1 = (f32[216,128]{1,0:T(8,128)}, f32[216,128]{1,0:T(8,128)S(1)}, u32[]{:S(2)}, u32[]{:S(2)}) collective-permute-start(f32[216,128]{1,0:T(8,128)} %get-tuple-element.31.s1lo), channel_id=1, source_target_pairs={{1,0},{2,1},{3,2},{4,3},{5,4},{6,5},{7,6},{8,7},{9,8},{10,9},{11,1... | collective-permute-start | bytes 331784 | tf_op jit(solution)/shard_map/ppermute | solution.py:302
  6.7 18.2 %collective-permute-start = (f32[216,128]{1,0:T(8,128)}, f32[216,128]{1,0:T(8,128)S(1)}, u32[]{:S(2)}, u32[]{:S(2)}) collective-permute-start(f32[216,128]{1,0:T(8,128)} %get-tuple-element.32.s1hi), channel_id=1, source_target_pairs={{0,1},{1,2},{2,3},{3,4},{4,5},{5,6},{6,7},{7,8},{8,9},{9,10},{10,1... | collective-permute-start | bytes 331784 | tf_op jit(solution)/shard_map/ppermute | solution.py:301
  7.4 17.6 %collective-permute-start.2 = (f32[216,128]{1,0:T(8,128)}, f32[216,128]{1,0:T(8,128)S(1)}, u32[]{:S(2)}, u32[]{:S(2)}) collective-permute-start(f32[216,128]{1,0:T(8,128)} %get-tuple-element.33.s1g), channel_id=1, source_target_pairs={{64,0},{65,1},{66,2},{67,3},{68,4},{69,5},{70,6},{71,7},{72,8},{73... | collective-permute-start | bytes 331784 | tf_op jit(solution)/shard_map/ppermute | solution.py:303
  24.9 0.7 %copy-start.4 = (f32[216,128]{1,0:T(8,128)}, f32[216,128]{1,0:T(8,128)S(1)}, u32[]{:S(2)}) copy-start(f32[216,128]{1,0:T(8,128)S(1)} %collective-permute-done.1.r1hi) | copy-start | bytes 331780
  24.9 0.7 %copy-start.5 = (f32[216,128]{1,0:T(8,128)}, f32[216,128]{1,0:T(8,128)S(1)}, u32[]{:S(2)}) copy-start(f32[216,128]{1,0:T(8,128)S(1)} %collective-permute-done.r1lo) | copy-start | bytes 331780
  24.9 0.7 %copy-start.6 = (f32[216,128]{1,0:T(8,128)}, f32[216,128]{1,0:T(8,128)S(1)}, u32[]{:S(2)}) copy-start(f32[216,128]{1,0:T(8,128)S(1)} %collective-permute-done.2.r1ghi) | copy-start | bytes 331780
  28.7 24.4 %collective-permute-start.3 = (f32[216,128]{1,0:T(8,128)}, f32[216,128]{1,0:T(8,128)S(1)}, u32[]{:S(2)}, u32[]{:S(2)}) collective-permute-start(f32[216,128]{1,0:T(8,128)} %get-tuple-element.47), channel_id=1, source_target_pairs={{0,1},{1,2},{2,3},{3,4},{4,5},{5,6},{6,7},{7,8},{8,9},{9,10},{10,1... | collective-permute-start | bytes 331784 | tf_op jit(solution)/shard_map/ppermute | solution.py:291
  30.6 22.5 %collective-permute-start.4 = (f32[216,128]{1,0:T(8,128)}, f32[216,128]{1,0:T(8,128)S(1)}, u32[]{:S(2)}, u32[]{:S(2)}) collective-permute-start(f32[216,128]{1,0:T(8,128)} %get-tuple-element.48), channel_id=1, source_target_pairs={{1,0},{2,1},{3,2},{4,3},{5,4},{6,5},{7,6},{8,7},{9,8},{10,9},{11,1... | collective-permute-start | bytes 331784 | tf_op jit(solution)/shard_map/ppermute | solution.py:292
  38.2 14.9 %collective-permute-start.5 = (f32[216,128]{1,0:T(8,128)}, f32[216,128]{1,0:T(8,128)S(1)}, u32[]{:S(2)}, u32[]{:S(2)}) collective-permute-start(f32[216,128]{1,0:T(8,128)} %get-tuple-element.49), channel_id=1, source_target_pairs={{0,64},{64,128},{128,192},{192,256},{256,320},{320,384},{384,448},... | collective-permute-start | bytes 331784 | tf_op jit(solution)/shard_map/ppermute | solution.py:293
  40.1 13.0 %collective-permute-start.6 = (f32[216,128]{1,0:T(8,128)}, f32[216,128]{1,0:T(8,128)S(1)}, u32[]{:S(2)}, u32[]{:S(2)}) collective-permute-start(f32[216,128]{1,0:T(8,128)} %get-tuple-element.50), channel_id=1, source_target_pairs={{64,0},{128,64},{192,128},{256,192},{320,256},{384,320},{448,384},... | collective-permute-start | bytes 331784 | tf_op jit(solution)/shard_map/ppermute | solution.py:294
  53.1 0.6 %copy-start = (f32[216,128]{1,0:T(8,128)}, f32[216,128]{1,0:T(8,128)S(1)}, u32[]{:S(2)}) copy-start(f32[216,128]{1,0:T(8,128)S(1)} %collective-permute-done.3.r2lo) | copy-start | bytes 331780
  53.1 0.7 %copy-start.1 = (f32[216,128]{1,0:T(8,128)}, f32[216,128]{1,0:T(8,128)S(1)}, u32[]{:S(2)}) copy-start(f32[216,128]{1,0:T(8,128)S(1)} %collective-permute-done.4.r2hi) | copy-start | bytes 331780
  53.1 0.7 %copy-start.2 = (f32[216,128]{1,0:T(8,128)}, f32[216,128]{1,0:T(8,128)S(1)}, u32[]{:S(2)}) copy-start(f32[216,128]{1,0:T(8,128)S(1)} %collective-permute-done.5.r2glo) | copy-start | bytes 331780
  53.1 0.7 %copy-start.3 = (f32[216,128]{1,0:T(8,128)}, f32[216,128]{1,0:T(8,128)S(1)}, u32[]{:S(2)}) copy-start(f32[216,128]{1,0:T(8,128)S(1)} %collective-permute-done.6.r2ghi) | copy-start | bytes 331780

commit v7 on v6

--- a/solution.py
+++ b/solution.py
@@ -67,8 +67,28 @@
     return hi, mid, (r - mid.astype(F32)).astype(BF)
 
 
-def _sel(parts, onehot):
-    return (_bdot(parts[0], onehot) + _bdot(parts[1], onehot)) + _bdot(parts[2], onehot)
+def _sel(p3, onehot):
+    return _bdot(p3, jnp.concatenate([onehot, onehot, onehot], axis=0))
+
+
+def _pad_rows(x, n):
+    return jnp.concatenate([x, jnp.zeros((n - x.shape[0], x.shape[1]), x.dtype)], axis=0)
+
+
+def _lhs3_t(blocks, n):
+    out = []
+    for b in blocks:
+        h, l = _split2(_pad_rows(b, n))
+        out += [h, h, l]
+    return jnp.concatenate(out, axis=0)
+
+
+def _rhs3_rows(blocks, n):
+    out = []
+    for b in blocks:
+        h, l = _split2(_pad_rows(b, n))
+        out += [h, l, h]
+    return jnp.concatenate(out, axis=0)
 
 
 def _load_field(ref):
@@ -116,7 +136,7 @@
 def _send(tables, send_ref, outs):
     rows = lax.broadcasted_iota(jnp.int32, (4 * E, 3 * E), 0)
     onehot = jnp.where(rows == send_ref[...].reshape(1, 3 * E), 1.0, 0.0).astype(BF)
-    s = _sel(_split3(jnp.concatenate(tables, axis=0)), onehot)
+    s = _sel(jnp.concatenate(_split3(jnp.concatenate(tables, axis=0)), axis=1), onehot)
     for i, (lo_ref, hi_ref, g_ref) in enumerate(outs):
         blk = s[i * TR:(i + 1) * TR]
         lo_ref[...] = blk[:, 0:E]
@@ -126,7 +146,7 @@
 
 def _gather(comb, slot_ref, face_ref, g_ref, received):
     rows = lax.broadcasted_iota(jnp.int32, (4 * E, E), 0)
-    parts = _split3(comb)
+    parts = jnp.concatenate(_split3(comb), axis=1)
     for f in range(4):
         v = slot_ref[f:f + 1, :]
         if received:
@@ -158,13 +178,13 @@
 
 def _lift_parts(lift_ref, lt_ref):
     lt_ref[:, 0:NB] = _rows84(lift_ref)
-    return [_split2(lt_ref[pl.ds(f, NF, stride=4), 0:NB]) for f in range(4)]
+    return _lhs3_t([lt_ref[pl.ds(f, NF, stride=4), 0:NB] for f in range(4)], 32)
 
 
 def _vol(b, x, star_ref, stiff_ref, a_ref, v_ref):
-    xp = _split2(x)
+    xr = _rhs3(x)
     for d in range(3):
-        a_ref[d * NB:(d + 1) * NB, :] = _dot3_t(_split2(stiff_ref[d]), xp)
+        a_ref[d * NB:(d + 1) * NB, :] = _tdot(_lhs3_t([stiff_ref[d]], 64), xr)
     _mix_vol(a_ref, star_ref, v_ref, 1)
     return b + v_ref[...]
 
@@ -179,10 +199,7 @@
 def _finish(bv_ref, yp_ref, recv, fn_ref, lift_p, slot_ref, face_ref, g_ref, yf_ref):
     _gather(jnp.concatenate(recv, axis=1), slot_ref, face_ref, g_ref, True)
     _fmix([(g_ref, fn_ref)], yf_ref, yp_ref)
-    ftot = None
-    for f in range(4):
-        t = _dot3_t(lift_p[f], _split2(yf_ref[f * FP:f * FP + NF, :]))
-        ftot = t if ftot is None else ftot + t
+    ftot = _tdot(lift_p, _rhs3_rows([yf_ref[f * FP:(f + 1) * FP, :] for f in range(4)], 32))
     return bv_ref[...] - ftot
 
 

time: 57.7 us -> 57 us (0.988)
  no operation moved by 1% of the time
where the time goes in v7:
time: 57 us; the launch traced here: 56.6 us
  starting transfers between devices  34.9 us (61%)
  Pallas kernels  20.2 us (35%)
  local copies, waits for them, and re-layouts  1.37 us (2%)
    ppermute x1, starting transfers between devices, exchange_fault(): from_ghi = lax.ppermute(g, axes, [(n_dom + i, i) for i in range(n_dom)])  13.8 us
    ppermute x1, starting transfers between devices, exchange(): from_ghi = lax.ppermute(gdn, 'grp', [(i + 1, i) for i in range(n_grp - 1)])  8.31 us
    ppermute x1, starting transfers between devices, exchange(): from_hi = lax.ppermute(lo, 'dom', [(i + 1, i) for i in range(n_dom - 1)])  7.58 us
    pallas_call x1, Pallas kernels, local(): pl.pallas_call(_kernel_a1, out_shape=(flat, flat, table, part, part, part...  6.01 us
    pallas_call x1, Pallas kernels, local(): pl.pallas_call(_kernel_b2, out_shape=(flat, yflux), in_specs=[_vmem()] *...  4.23 us
    pallas_call x1, Pallas kernels, local(): pl.pallas_call(_kernel_a2, out_shape=(flat, table, part, part, part, part...  3.66 us
    pallas_call x1, Pallas kernels, local(): pl.pallas_call(_kernel_c, out_shape=field, in_specs=[_vmem()] * 10, out_s...  3.19 us
    pallas_call x1, Pallas kernels, local(): pl.pallas_call(_kernel_b, out_shape=(flat, flat, table, part, part, part,...  3.09 us
  transfers between devices with their start and end apart: 7, of which 0 were waited for; matrix products, arithmetic and copies ran while one was open for 0% of the time, Pallas kernels for 14%

profile of v7, /device:TPU:24, one launch (start us, length us, event | category | flops | bytes accessed | tf_op | source)
XLA Modules:
  0.0 56.6 jit_solution(8478011823468633584)
XLA Ops:
  0.0 6.0 %shard_map.100 = (f32[56,1152]{1,0:T(8,128)}, f32[56,1152]{1,0:T(8,128)}, f32[216,512]{1,0:T(8,128)}, f32[216,128]{1,0:T(8,128)}, f32[216,128]{1,0:T(8,128)}, /*index=5*/f32[216,128]{1,0:T(8,128)}) custom-call(f32[9,56,128]{2,1,0:T(8,128)} %bitcast.16, f32[9,9,3,128]{3,2,1,0:T(4,128)} %bitcast.12, f32[3,56,56]{2,1,0:T(8,128)} %stiff_ref.7, ...), custom_call_target="tpu_custom_call" | custom-call | tf_op jit(solution)/shard_map/pallas_call | solution.py:346
  6.0 0.7 %collective-permute-start.1 = (f32[216,128]{1,0:T(8,128)}, f32[216,128]{1,0:T(8,128)S(1)}, u32[]{:S(2)}, u32[]{:S(2)}) collective-permute-start(f32[216,128]{1,0:T(8,128)} %get-tuple-element.31.s1lo), channel_id=1, source_target_pairs={{1,0},{2,1},{3,2},{4,3},{5,4},{6,5},{7,6},{8,7},{9,8},{10,9},{11,1... | collective-permute-start | bytes 331784 | tf_op jit(solution)/shard_map/ppermute | solution.py:319
  6.7 0.7 %collective-permute-start = (f32[216,128]{1,0:T(8,128)}, f32[216,128]{1,0:T(8,128)S(1)}, u32[]{:S(2)}, u32[]{:S(2)}) collective-permute-start(f32[216,128]{1,0:T(8,128)} %get-tuple-element.32.s1hi), channel_id=1, source_target_pairs={{0,1},{1,2},{2,3},{3,4},{4,5},{5,6},{6,7},{7,8},{8,9},{9,10},{10,1... | collective-permute-start | bytes 331784 | tf_op jit(solution)/shard_map/ppermute | solution.py:318
  7.3 13.8 %collective-permute-start.2 = (f32[216,128]{1,0:T(8,128)}, f32[216,128]{1,0:T(8,128)S(1)}, u32[]{:S(2)}, u32[]{:S(2)}) collective-permute-start(f32[216,128]{1,0:T(8,128)} %get-tuple-element.33.s1g), channel_id=1, source_target_pairs={{64,0},{65,1},{66,2},{67,3},{68,4},{69,5},{70,6},{71,7},{72,8},{73... | collective-permute-start | bytes 331784 | tf_op jit(solution)/shard_map/ppermute | solution.py:320
  21.2 3.7 %shard_map.101 = (f32[56,1152]{1,0:T(8,128)}, f32[216,512]{1,0:T(8,128)}, f32[216,128]{1,0:T(8,128)}, f32[216,128]{1,0:T(8,128)}, f32[216,128]{1,0:T(8,128)}, /*...) custom-call(s32[1]{0:T(128)} %bitcast.grp_ref, f32[9,56,128]{2,1,0:T(8,128)} %bitcast.17, ...), custom_call_target="tpu_custom_call" | custom-call | tf_op jit(solution)/shard_map/pallas_call | solution.py:356
  24.9 0.0 collective-permute-done.1.r1hi
  24.9 0.0 collective-permute-done.r1lo
  24.9 0.0 collective-permute-done.2.r1ghi
  24.9 0.6 %copy-done.4 = f32[216,128]{1,0:T(8,128)} copy-done((f32[216,128]{1,0:T(8,128)}, f32[216,128]{1,0:T(8,128)S(1)}, u32[]{:S(2)}) %copy-start.4) | copy-done | bytes 110616
  25.5 0.0 copy-done.5
  25.6 0.0 copy-done.6
  25.6 3.1 %shard_map.102 = (f32[56,1152]{1,0:T(8,128)}, f32[56,1152]{1,0:T(8,128)}, f32[216,512]{1,0:T(8,128)}, f32[216,128]{1,0:T(8,128)}, f32[216,128]{1,0:T(8,128)}, /*index=5*/f32[216,128]{1,0:T(8,128)}, f32[216,128]{1,0:T(8,128)}) custom-call(s32[1]{0:T(128)} %bitcast.grp_ref, f32[9,56,128]{2,1,0:T(8,128)} %bitcast.18, f32[56,1152]{1,0:T(8,128)} %get-tuple-element.34.fl_ref, ...), custom_call_target="tpu_custom_call" | custom-call | tf_op jit(solution)/shard_map/pallas_call | solution.py:365
  28.7 1.9 %collective-permute-start.3 = (f32[216,128]{1,0:T(8,128)}, f32[216,128]{1,0:T(8,128)S(1)}, u32[]{:S(2)}, u32[]{:S(2)}) collective-permute-start(f32[216,128]{1,0:T(8,128)} %get-tuple-element.47), channel_id=1, source_target_pairs={{0,1},{1,2},{2,3},{3,4},{4,5},{5,6},{6,7},{7,8},{8,9},{9,10},{10,1... | collective-permute-start | bytes 331784 | tf_op jit(solution)/shard_map/ppermute | solution.py:308
  30.6 7.6 %collective-permute-start.4 = (f32[216,128]{1,0:T(8,128)}, f32[216,128]{1,0:T(8,128)S(1)}, u32[]{:S(2)}, u32[]{:S(2)}) collective-permute-start(f32[216,128]{1,0:T(8,128)} %get-tuple-element.48), channel_id=1, source_target_pairs={{1,0},{2,1},{3,2},{4,3},{5,4},{6,5},{7,6},{8,7},{9,8},{10,9},{11,1... | collective-permute-start | bytes 331784 | tf_op jit(solution)/shard_map/ppermute | solution.py:309
  38.2 1.9 %collective-permute-start.5 = (f32[216,128]{1,0:T(8,128)}, f32[216,128]{1,0:T(8,128)S(1)}, u32[]{:S(2)}, u32[]{:S(2)}) collective-permute-start(f32[216,128]{1,0:T(8,128)} %get-tuple-element.49), channel_id=1, source_target_pairs={{0,64},{64,128},{128,192},{192,256},{256,320},{320,384},{384,448},... | collective-permute-start | bytes 331784 | tf_op jit(solution)/shard_map/ppermute | solution.py:310
  40.1 8.3 %collective-permute-start.6 = (f32[216,128]{1,0:T(8,128)}, f32[216,128]{1,0:T(8,128)S(1)}, u32[]{:S(2)}, u32[]{:S(2)}) collective-permute-start(f32[216,128]{1,0:T(8,128)} %get-tuple-element.50), channel_id=1, source_target_pairs={{64,0},{128,64},{192,128},{256,192},{320,256},{384,320},{448,384},... | collective-permute-start | bytes 331784 | tf_op jit(solution)/shard_map/ppermute | solution.py:311
  48.4 4.2 %shard_map.103 = (f32[56,1152]{1,0:T(8,128)}, f32[96,1152]{1,0:T(8,128)}) custom-call(f32[56,1152]{1,0:T(8,128)} %get-tuple-element.42.base_ref, f32[56,1152]{1,0:T(8,128)} %get-tuple-element.43.integ_ref, f32[216,512]{1,0:T(8,128)} %get-tuple-element.44.own_ref, f32[9,9,3,128]{3,2,1,0:T(4,128)} %bitcast.15, f32[9,9,4,128]{3,2,1,0:T(4,128)} %bitcast.20, ...), custom_call_target="tpu_custom_call" | custom-call | tf_op jit(solution)/shard_map/pallas_call | solution.py:376
  52.7 0.0 collective-permute-done.3.r2lo
  52.7 0.0 collective-permute-done.4.r2hi
  52.7 0.6 %copy-done = f32[216,128]{1,0:T(8,128)} copy-done((f32[216,128]{1,0:T(8,128)}, f32[216,128]{1,0:T(8,128)S(1)}, u32[]{:S(2)}) %copy-start) | copy-done | bytes 110616
  53.3 0.0 copy-done.1
  53.4 0.0 copy-done.2
  53.4 0.0 copy-done.3
  53.4 3.2 %shard_map.104 = f32[9,56,128]{2,1,0:T(8,128)} custom-call(f32[56,1152]{1,0:T(8,128)} %get-tuple-element.45.bv_ref, f32[96,1152]{1,0:T(8,128)} %get-tuple-element.46.yp_ref, f32[216,128]{1,0:T(8,128)} %copy-done, f32[216,128]{1,0:T(8,128)} %copy-done.1, f32[216,128]{1,0:T(8,128)} %copy-done.2, f32[216,128]{1,0:T(8,128)} %copy-done.3, s32[4,128]{1,0:T(4,128)} %slot_ref.7, ...), custom_call_target="tpu_custom_call" | custom-call | tf_op jit(solution)/shard_map/pallas_call | solution.py:384
  (9 shorter events, 0.0 us)
Async XLA Ops:
  6.0 18.9 %collective-permute-start.1 = (f32[216,128]{1,0:T(8,128)}, f32[216,128]{1,0:T(8,128)S(1)}, u32[]{:S(2)}, u32[]{:S(2)}) collective-permute-start(f32[216,128]{1,0:T(8,128)} %get-tuple-element.31.s1lo), channel_id=1, source_target_pairs={{1,0},{2,1},{3,2},{4,3},{5,4},{6,5},{7,6},{8,7},{9,8},{10,9},{11,1... | collective-permute-start | bytes 331784 | tf_op jit(solution)/shard_map/ppermute | solution.py:319
  6.7 18.2 %collective-permute-start = (f32[216,128]{1,0:T(8,128)}, f32[216,128]{1,0:T(8,128)S(1)}, u32[]{:S(2)}, u32[]{:S(2)}) collective-permute-start(f32[216,128]{1,0:T(8,128)} %get-tuple-element.32.s1hi), channel_id=1, source_target_pairs={{0,1},{1,2},{2,3},{3,4},{4,5},{5,6},{6,7},{7,8},{8,9},{9,10},{10,1... | collective-permute-start | bytes 331784 | tf_op jit(solution)/shard_map/ppermute | solution.py:318
  7.3 17.6 %collective-permute-start.2 = (f32[216,128]{1,0:T(8,128)}, f32[216,128]{1,0:T(8,128)S(1)}, u32[]{:S(2)}, u32[]{:S(2)}) collective-permute-start(f32[216,128]{1,0:T(8,128)} %get-tuple-element.33.s1g), channel_id=1, source_target_pairs={{64,0},{65,1},{66,2},{67,3},{68,4},{69,5},{70,6},{71,7},{72,8},{73... | collective-permute-start | bytes 331784 | tf_op jit(solution)/shard_map/ppermute | solution.py:320
  24.9 0.7 %copy-start.4 = (f32[216,128]{1,0:T(8,128)}, f32[216,128]{1,0:T(8,128)S(1)}, u32[]{:S(2)}) copy-start(f32[216,128]{1,0:T(8,128)S(1)} %collective-permute-done.1.r1hi) | copy-start | bytes 331780
  24.9 0.7 %copy-start.5 = (f32[216,128]{1,0:T(8,128)}, f32[216,128]{1,0:T(8,128)S(1)}, u32[]{:S(2)}) copy-start(f32[216,128]{1,0:T(8,128)S(1)} %collective-permute-done.r1lo) | copy-start | bytes 331780
  24.9 0.7 %copy-start.6 = (f32[216,128]{1,0:T(8,128)}, f32[216,128]{1,0:T(8,128)S(1)}, u32[]{:S(2)}) copy-start(f32[216,128]{1,0:T(8,128)S(1)} %collective-permute-done.2.r1ghi) | copy-start | bytes 331780
  28.7 24.0 %collective-permute-start.3 = (f32[216,128]{1,0:T(8,128)}, f32[216,128]{1,0:T(8,128)S(1)}, u32[]{:S(2)}, u32[]{:S(2)}) collective-permute-start(f32[216,128]{1,0:T(8,128)} %get-tuple-element.47), channel_id=1, source_target_pairs={{0,1},{1,2},{2,3},{3,4},{4,5},{5,6},{6,7},{7,8},{8,9},{9,10},{10,1... | collective-permute-start | bytes 331784 | tf_op jit(solution)/shard_map/ppermute | solution.py:308
  30.6 22.1 %collective-permute-start.4 = (f32[216,128]{1,0:T(8,128)}, f32[216,128]{1,0:T(8,128)S(1)}, u32[]{:S(2)}, u32[]{:S(2)}) collective-permute-start(f32[216,128]{1,0:T(8,128)} %get-tuple-element.48), channel_id=1, source_target_pairs={{1,0},{2,1},{3,2},{4,3},{5,4},{6,5},{7,6},{8,7},{9,8},{10,9},{11,1... | collective-permute-start | bytes 331784 | tf_op jit(solution)/shard_map/ppermute | solution.py:309
  38.2 14.5 %collective-permute-start.5 = (f32[216,128]{1,0:T(8,128)}, f32[216,128]{1,0:T(8,128)S(1)}, u32[]{:S(2)}, u32[]{:S(2)}) collective-permute-start(f32[216,128]{1,0:T(8,128)} %get-tuple-element.49), channel_id=1, source_target_pairs={{0,64},{64,128},{128,192},{192,256},{256,320},{320,384},{384,448},... | collective-permute-start | bytes 331784 | tf_op jit(solution)/shard_map/ppermute | solution.py:310
  40.1 12.6 %collective-permute-start.6 = (f32[216,128]{1,0:T(8,128)}, f32[216,128]{1,0:T(8,128)S(1)}, u32[]{:S(2)}, u32[]{:S(2)}) collective-permute-start(f32[216,128]{1,0:T(8,128)} %get-tuple-element.50), channel_id=1, source_target_pairs={{64,0},{128,64},{192,128},{256,192},{320,256},{384,320},{448,384},... | collective-permute-start | bytes 331784 | tf_op jit(solution)/shard_map/ppermute | solution.py:311
  52.7 0.6 %copy-start = (f32[216,128]{1,0:T(8,128)}, f32[216,128]{1,0:T(8,128)S(1)}, u32[]{:S(2)}) copy-start(f32[216,128]{1,0:T(8,128)S(1)} %collective-permute-done.3.r2lo) | copy-start | bytes 331780
  52.7 0.7 %copy-start.1 = (f32[216,128]{1,0:T(8,128)}, f32[216,128]{1,0:T(8,128)S(1)}, u32[]{:S(2)}) copy-start(f32[216,128]{1,0:T(8,128)S(1)} %collective-permute-done.4.r2hi) | copy-start | bytes 331780
  52.7 0.7 %copy-start.2 = (f32[216,128]{1,0:T(8,128)}, f32[216,128]{1,0:T(8,128)S(1)}, u32[]{:S(2)}) copy-start(f32[216,128]{1,0:T(8,128)S(1)} %collective-permute-done.5.r2glo) | copy-start | bytes 331780
  52.7 0.7 %copy-start.3 = (f32[216,128]{1,0:T(8,128)}, f32[216,128]{1,0:T(8,128)S(1)}, u32[]{:S(2)}) copy-start(f32[216,128]{1,0:T(8,128)S(1)} %collective-permute-done.6.r2ghi) | copy-start | bytes 331780

commit v8 on v7

--- a/solution.py
+++ b/solution.py
@@ -6,6 +6,7 @@
 from jax.experimental import pallas as pl
 from jax.experimental.pallas import tpu as pltpu
 from jax.sharding import PartitionSpec as P
+
 
 ORDER = 6
 NB = 56
@@ -34,16 +35,8 @@
     return hi, (x - hi.astype(F32)).astype(BF)
 
 
-def _dot3(a, b):
-    return _bdot(a[0], b[0]) + (_bdot(a[0], b[1]) + _bdot(a[1], b[0]))
-
-
 def _tdot(a, b):
     return lax.dot_general(a, b, (((0,), (0,)), ((), ())), preferred_element_type=F32)
-
-
-def _dot3_t(a, b):
-    return _tdot(a[0], b[0]) + (_tdot(a[0], b[1]) + _tdot(a[1], b[0]))
 
 
 def _rows84(ref):
@@ -305,23 +298,23 @@
 def exchange(lo, hi, gup, gdn):
     n_dom = lax.axis_size("dom")
     n_grp = lax.axis_size("grp")
+    from_ghi = lax.ppermute(gdn, "grp", [(i + 1, i) for i in range(n_grp - 1)])
+    from_glo = lax.ppermute(gup, "grp", [(i, i + 1) for i in range(n_grp - 1)])
     from_lo = lax.ppermute(hi, "dom", [(i, i + 1) for i in range(n_dom - 1)])
     from_hi = lax.ppermute(lo, "dom", [(i + 1, i) for i in range(n_dom - 1)])
-    from_glo = lax.ppermute(gup, "grp", [(i, i + 1) for i in range(n_grp - 1)])
-    from_ghi = lax.ppermute(gdn, "grp", [(i + 1, i) for i in range(n_grp - 1)])
     return from_lo, from_hi, from_glo, from_ghi
 
 
 def exchange_fault(lo, hi, g):
     n_dom = lax.axis_size("dom")
     axes = ("grp", "dom")
+    from_ghi = lax.ppermute(g, axes, [(n_dom + i, i) for i in range(n_dom)])
     from_lo = lax.ppermute(hi, axes, [(i, i + 1) for i in range(n_dom - 1)])
     from_hi = lax.ppermute(lo, axes, [(i + 1, i) for i in range(n_dom - 1)])
-    from_ghi = lax.ppermute(g, axes, [(n_dom + i, i) for i in range(n_dom)])
     return from_lo, from_hi, from_ghi
 
 
-def local(state, star, flux_own, flux_nbr, stiff, trace, lift, nbr_slot, nbr_face, send_slot):
+def _local(state, star, flux_own, flux_nbr, stiff, trace, lift, nbr_slot, nbr_face, send_slot):
     grp = lax.axis_index("grp").astype(jnp.int32).reshape(1)
     x0 = jnp.transpose(state, (1, 0, 2))
     star = jnp.transpose(star, (1, 2, 0, 3))
@@ -405,4 +398,4 @@
         P(("grp", "dom")),
     )
     out_specs = P(None, None, ("grp", "dom"))
-    return jax.shard_map(local, mesh=mesh, in_specs=in_specs, out_specs=out_specs, check_vma=False)
+    return jax.shard_map(_local, mesh=mesh, in_specs=in_specs, out_specs=out_specs, check_vma=False)

time: 57 us -> 57 us (level)
  no operation moved by 1% of the time
where the time goes in v8:
time: 57 us; the launch traced here: 56.6 us
  starting transfers between devices  34.9 us (61%)
  Pallas kernels  20.2 us (35%)
  local copies, waits for them, and re-layouts  1.37 us (2%)
    ppermute x1, starting transfers between devices, exchange_fault(): from_ghi = lax.ppermute(g, axes, [(n_dom + i, i) for i in range(n_dom)])  13.8 us
    ppermute x1, starting transfers between devices, exchange(): from_ghi = lax.ppermute(gdn, 'grp', [(i + 1, i) for i in range(n_grp - 1)])  8.31 us
    ppermute x1, starting transfers between devices, exchange(): from_hi = lax.ppermute(lo, 'dom', [(i + 1, i) for i in range(n_dom - 1)])  7.58 us
    pallas_call x1, Pallas kernels, _local(): pl.pallas_call(_kernel_a1, out_shape=(flat, flat, table, part, part, part...  6.01 us
    pallas_call x1, Pallas kernels, _local(): pl.pallas_call(_kernel_b2, out_shape=(flat, yflux), in_specs=[_vmem()] *...  4.23 us
    pallas_call x1, Pallas kernels, _local(): pl.pallas_call(_kernel_a2, out_shape=(flat, table, part, part, part, part...  3.66 us
    pallas_call x1, Pallas kernels, _local(): pl.pallas_call(_kernel_c, out_shape=field, in_specs=[_vmem()] * 10, out_s...  3.19 us
    pallas_call x1, Pallas kernels, _local(): pl.pallas_call(_kernel_b, out_shape=(flat, flat, table, part, part, part,...  3.09 us
  transfers between devices with their start and end apart: 7, of which 0 were waited for; matrix products, arithmetic and copies ran while one was open for 0% of the time, Pallas kernels for 14%

profile of v8, /device:TPU:24, one launch (start us, length us, event | category | flops | bytes accessed | tf_op | source)
XLA Modules:
  0.0 56.6 jit_solution(8478011823468633584)
XLA Ops:
  0.0 6.0 %shard_map.100 = (f32[56,1152]{1,0:T(8,128)}, f32[56,1152]{1,0:T(8,128)}, f32[216,512]{1,0:T(8,128)}, f32[216,128]{1,0:T(8,128)}, f32[216,128]{1,0:T(8,128)}, /*index=5*/f32[216,128]{1,0:T(8,128)}) custom-call(f32[9,56,128]{2,1,0:T(8,128)} %bitcast.16, f32[9,9,3,128]{3,2,1,0:T(4,128)} %bitcast.12, f32[3,56,56]{2,1,0:T(8,128)} %stiff_ref.7, ...), custom_call_target="tpu_custom_call" | custom-call | tf_op jit(solution)/shard_map/pallas_call | solution.py:339
  6.0 0.7 %collective-permute-start.1 = (f32[216,128]{1,0:T(8,128)}, f32[216,128]{1,0:T(8,128)S(1)}, u32[]{:S(2)}, u32[]{:S(2)}) collective-permute-start(f32[216,128]{1,0:T(8,128)} %get-tuple-element.31.s1lo), channel_id=1, source_target_pairs={{1,0},{2,1},{3,2},{4,3},{5,4},{6,5},{7,6},{8,7},{9,8},{10,9},{11,1... | collective-permute-start | bytes 331784 | tf_op jit(solution)/shard_map/ppermute | solution.py:313
  6.7 0.7 %collective-permute-start = (f32[216,128]{1,0:T(8,128)}, f32[216,128]{1,0:T(8,128)S(1)}, u32[]{:S(2)}, u32[]{:S(2)}) collective-permute-start(f32[216,128]{1,0:T(8,128)} %get-tuple-element.32.s1hi), channel_id=1, source_target_pairs={{0,1},{1,2},{2,3},{3,4},{4,5},{5,6},{6,7},{7,8},{8,9},{9,10},{10,1... | collective-permute-start | bytes 331784 | tf_op jit(solution)/shard_map/ppermute | solution.py:312
  7.3 13.8 %collective-permute-start.2 = (f32[216,128]{1,0:T(8,128)}, f32[216,128]{1,0:T(8,128)S(1)}, u32[]{:S(2)}, u32[]{:S(2)}) collective-permute-start(f32[216,128]{1,0:T(8,128)} %get-tuple-element.33.s1g), channel_id=1, source_target_pairs={{64,0},{65,1},{66,2},{67,3},{68,4},{69,5},{70,6},{71,7},{72,8},{73... | collective-permute-start | bytes 331784 | tf_op jit(solution)/shard_map/ppermute | solution.py:311
  21.2 3.7 %shard_map.101 = (f32[56,1152]{1,0:T(8,128)}, f32[216,512]{1,0:T(8,128)}, f32[216,128]{1,0:T(8,128)}, f32[216,128]{1,0:T(8,128)}, f32[216,128]{1,0:T(8,128)}, /*...) custom-call(s32[1]{0:T(128)} %bitcast.grp_ref, f32[9,56,128]{2,1,0:T(8,128)} %bitcast.17, ...), custom_call_target="tpu_custom_call" | custom-call | tf_op jit(solution)/shard_map/pallas_call | solution.py:349
  24.9 0.0 collective-permute-done.1.r1hi
  24.9 0.0 collective-permute-done.r1lo
  24.9 0.6 %copy-done.4 = f32[216,128]{1,0:T(8,128)} copy-done((f32[216,128]{1,0:T(8,128)}, f32[216,128]{1,0:T(8,128)S(1)}, u32[]{:S(2)}) %copy-start.4) | copy-done | bytes 110616
  25.5 0.0 copy-done.5
  25.6 0.0 copy-done.6
  25.6 3.1 %shard_map.102 = (f32[56,1152]{1,0:T(8,128)}, f32[56,1152]{1,0:T(8,128)}, f32[216,512]{1,0:T(8,128)}, f32[216,128]{1,0:T(8,128)}, f32[216,128]{1,0:T(8,128)}, /*index=5*/f32[216,128]{1,0:T(8,128)}, f32[216,128]{1,0:T(8,128)}) custom-call(s32[1]{0:T(128)} %bitcast.grp_ref, f32[9,56,128]{2,1,0:T(8,128)} %bitcast.18, f32[56,1152]{1,0:T(8,128)} %get-tuple-element.34.fl_ref, ...), custom_call_target="tpu_custom_call" | custom-call | tf_op jit(solution)/shard_map/pallas_call | solution.py:358
  28.7 1.9 %collective-permute-start.3 = (f32[216,128]{1,0:T(8,128)}, f32[216,128]{1,0:T(8,128)S(1)}, u32[]{:S(2)}, u32[]{:S(2)}) collective-permute-start(f32[216,128]{1,0:T(8,128)} %get-tuple-element.47), channel_id=1, source_target_pairs={{0,1},{1,2},{2,3},{3,4},{4,5},{5,6},{6,7},{7,8},{8,9},{9,10},{10,1... | collective-permute-start | bytes 331784 | tf_op jit(solution)/shard_map/ppermute | solution.py:303
  30.6 7.6 %collective-permute-start.4 = (f32[216,128]{1,0:T(8,128)}, f32[216,128]{1,0:T(8,128)S(1)}, u32[]{:S(2)}, u32[]{:S(2)}) collective-permute-start(f32[216,128]{1,0:T(8,128)} %get-tuple-element.48), channel_id=1, source_target_pairs={{1,0},{2,1},{3,2},{4,3},{5,4},{6,5},{7,6},{8,7},{9,8},{10,9},{11,1... | collective-permute-start | bytes 331784 | tf_op jit(solution)/shard_map/ppermute | solution.py:304
  38.2 1.9 %collective-permute-start.5 = (f32[216,128]{1,0:T(8,128)}, f32[216,128]{1,0:T(8,128)S(1)}, u32[]{:S(2)}, u32[]{:S(2)}) collective-permute-start(f32[216,128]{1,0:T(8,128)} %get-tuple-element.49), channel_id=1, source_target_pairs={{0,64},{64,128},{128,192},{192,256},{256,320},{320,384},{384,448},... | collective-permute-start | bytes 331784 | tf_op jit(solution)/shard_map/ppermute | solution.py:302
  40.1 8.3 %collective-permute-start.6 = (f32[216,128]{1,0:T(8,128)}, f32[216,128]{1,0:T(8,128)S(1)}, u32[]{:S(2)}, u32[]{:S(2)}) collective-permute-start(f32[216,128]{1,0:T(8,128)} %get-tuple-element.50), channel_id=1, source_target_pairs={{64,0},{128,64},{192,128},{256,192},{320,256},{384,320},{448,384},... | collective-permute-start | bytes 331784 | tf_op jit(solution)/shard_map/ppermute | solution.py:301
  48.4 4.2 %shard_map.103 = (f32[56,1152]{1,0:T(8,128)}, f32[96,1152]{1,0:T(8,128)}) custom-call(f32[56,1152]{1,0:T(8,128)} %get-tuple-element.42.base_ref, f32[56,1152]{1,0:T(8,128)} %get-tuple-element.43.integ_ref, f32[216,512]{1,0:T(8,128)} %get-tuple-element.44.own_ref, f32[9,9,3,128]{3,2,1,0:T(4,128)} %bitcast.15, f32[9,9,4,128]{3,2,1,0:T(4,128)} %bitcast.20, ...), custom_call_target="tpu_custom_call" | custom-call | tf_op jit(solution)/shard_map/pallas_call | solution.py:369
  52.7 0.0 collective-permute-done.3.r2lo
  52.7 0.0 collective-permute-done.4.r2hi
  52.7 0.0 collective-permute-done.5.r2glo
  52.7 0.6 %copy-done = f32[216,128]{1,0:T(8,128)} copy-done((f32[216,128]{1,0:T(8,128)}, f32[216,128]{1,0:T(8,128)S(1)}, u32[]{:S(2)}) %copy-start) | copy-done | bytes 110616
  53.3 0.0 copy-done.1
  53.4 0.0 copy-done.2
  53.4 0.0 copy-done.3
  53.4 3.2 %shard_map.104 = f32[9,56,128]{2,1,0:T(8,128)} custom-call(f32[56,1152]{1,0:T(8,128)} %get-tuple-element.45.bv_ref, f32[96,1152]{1,0:T(8,128)} %get-tuple-element.46.yp_ref, f32[216,128]{1,0:T(8,128)} %copy-done, f32[216,128]{1,0:T(8,128)} %copy-done.1, f32[216,128]{1,0:T(8,128)} %copy-done.2, f32[216,128]{1,0:T(8,128)} %copy-done.3, s32[4,128]{1,0:T(4,128)} %slot_ref.7, ...), custom_call_target="tpu_custom_call" | custom-call | tf_op jit(solution)/shard_map/pallas_call | solution.py:377
  (9 shorter events, 0.0 us)
Async XLA Ops:
  6.0 18.9 %collective-permute-start.1 = (f32[216,128]{1,0:T(8,128)}, f32[216,128]{1,0:T(8,128)S(1)}, u32[]{:S(2)}, u32[]{:S(2)}) collective-permute-start(f32[216,128]{1,0:T(8,128)} %get-tuple-element.31.s1lo), channel_id=1, source_target_pairs={{1,0},{2,1},{3,2},{4,3},{5,4},{6,5},{7,6},{8,7},{9,8},{10,9},{11,1... | collective-permute-start | bytes 331784 | tf_op jit(solution)/shard_map/ppermute | solution.py:313
  6.7 18.2 %collective-permute-start = (f32[216,128]{1,0:T(8,128)}, f32[216,128]{1,0:T(8,128)S(1)}, u32[]{:S(2)}, u32[]{:S(2)}) collective-permute-start(f32[216,128]{1,0:T(8,128)} %get-tuple-element.32.s1hi), channel_id=1, source_target_pairs={{0,1},{1,2},{2,3},{3,4},{4,5},{5,6},{6,7},{7,8},{8,9},{9,10},{10,1... | collective-permute-start | bytes 331784 | tf_op jit(solution)/shard_map/ppermute | solution.py:312
  7.3 17.6 %collective-permute-start.2 = (f32[216,128]{1,0:T(8,128)}, f32[216,128]{1,0:T(8,128)S(1)}, u32[]{:S(2)}, u32[]{:S(2)}) collective-permute-start(f32[216,128]{1,0:T(8,128)} %get-tuple-element.33.s1g), channel_id=1, source_target_pairs={{64,0},{65,1},{66,2},{67,3},{68,4},{69,5},{70,6},{71,7},{72,8},{73... | collective-permute-start | bytes 331784 | tf_op jit(solution)/shard_map/ppermute | solution.py:311
  24.9 0.7 %copy-start.4 = (f32[216,128]{1,0:T(8,128)}, f32[216,128]{1,0:T(8,128)S(1)}, u32[]{:S(2)}) copy-start(f32[216,128]{1,0:T(8,128)S(1)} %collective-permute-done.1.r1hi) | copy-start | bytes 331780
  24.9 0.7 %copy-start.5 = (f32[216,128]{1,0:T(8,128)}, f32[216,128]{1,0:T(8,128)S(1)}, u32[]{:S(2)}) copy-start(f32[216,128]{1,0:T(8,128)S(1)} %collective-permute-done.r1lo) | copy-start | bytes 331780
  24.9 0.7 %copy-start.6 = (f32[216,128]{1,0:T(8,128)}, f32[216,128]{1,0:T(8,128)S(1)}, u32[]{:S(2)}) copy-start(f32[216,128]{1,0:T(8,128)S(1)} %collective-permute-done.2.r1ghi) | copy-start | bytes 331780
  28.7 24.0 %collective-permute-start.3 = (f32[216,128]{1,0:T(8,128)}, f32[216,128]{1,0:T(8,128)S(1)}, u32[]{:S(2)}, u32[]{:S(2)}) collective-permute-start(f32[216,128]{1,0:T(8,128)} %get-tuple-element.47), channel_id=1, source_target_pairs={{0,1},{1,2},{2,3},{3,4},{4,5},{5,6},{6,7},{7,8},{8,9},{9,10},{10,1... | collective-permute-start | bytes 331784 | tf_op jit(solution)/shard_map/ppermute | solution.py:303
  30.6 22.1 %collective-permute-start.4 = (f32[216,128]{1,0:T(8,128)}, f32[216,128]{1,0:T(8,128)S(1)}, u32[]{:S(2)}, u32[]{:S(2)}) collective-permute-start(f32[216,128]{1,0:T(8,128)} %get-tuple-element.48), channel_id=1, source_target_pairs={{1,0},{2,1},{3,2},{4,3},{5,4},{6,5},{7,6},{8,7},{9,8},{10,9},{11,1... | collective-permute-start | bytes 331784 | tf_op jit(solution)/shard_map/ppermute | solution.py:304
  38.2 14.5 %collective-permute-start.5 = (f32[216,128]{1,0:T(8,128)}, f32[216,128]{1,0:T(8,128)S(1)}, u32[]{:S(2)}, u32[]{:S(2)}) collective-permute-start(f32[216,128]{1,0:T(8,128)} %get-tuple-element.49), channel_id=1, source_target_pairs={{0,64},{64,128},{128,192},{192,256},{256,320},{320,384},{384,448},... | collective-permute-start | bytes 331784 | tf_op jit(solution)/shard_map/ppermute | solution.py:302
  40.1 12.6 %collective-permute-start.6 = (f32[216,128]{1,0:T(8,128)}, f32[216,128]{1,0:T(8,128)S(1)}, u32[]{:S(2)}, u32[]{:S(2)}) collective-permute-start(f32[216,128]{1,0:T(8,128)} %get-tuple-element.50), channel_id=1, source_target_pairs={{64,0},{128,64},{192,128},{256,192},{320,256},{384,320},{448,384},... | collective-permute-start | bytes 331784 | tf_op jit(solution)/shard_map/ppermute | solution.py:301
  52.7 0.6 %copy-start = (f32[216,128]{1,0:T(8,128)}, f32[216,128]{1,0:T(8,128)S(1)}, u32[]{:S(2)}) copy-start(f32[216,128]{1,0:T(8,128)S(1)} %collective-permute-done.3.r2lo) | copy-start | bytes 331780
  52.7 0.7 %copy-start.1 = (f32[216,128]{1,0:T(8,128)}, f32[216,128]{1,0:T(8,128)S(1)}, u32[]{:S(2)}) copy-start(f32[216,128]{1,0:T(8,128)S(1)} %collective-permute-done.4.r2hi) | copy-start | bytes 331780
  52.7 0.7 %copy-start.2 = (f32[216,128]{1,0:T(8,128)}, f32[216,128]{1,0:T(8,128)S(1)}, u32[]{:S(2)}) copy-start(f32[216,128]{1,0:T(8,128)S(1)} %collective-permute-done.5.r2glo) | copy-start | bytes 331780
  52.7 0.7 %copy-start.3 = (f32[216,128]{1,0:T(8,128)}, f32[216,128]{1,0:T(8,128)S(1)}, u32[]{:S(2)}) copy-start(f32[216,128]{1,0:T(8,128)S(1)} %collective-permute-done.6.r2ghi) | copy-start | bytes 331780

commit v9 on v7

--- a/solution.py
+++ b/solution.py
@@ -20,6 +20,8 @@
 
 W_FIRST = [0.5 ** (k + 1) / math.factorial(k + 1) for k in range(ORDER)]
 W_LATER = [(1.0 - 0.5 ** (k + 1)) / math.factorial(k + 1) for k in range(ORDER)]
+W_FIRST = [w * (-1) ** k for k, w in enumerate(W_FIRST)]
+W_LATER = [w * (-1) ** k for k, w in enumerate(W_LATER)]
 
 
 BF = jnp.bfloat16
@@ -117,7 +119,7 @@
     d_ref[...] = x
     for k in range(ORDER - 1):
         a_ref[...] = _bdot(stiff_p, _rhs3(d_ref[...]))
-        _mix_vol(a_ref, star_ref, d_ref, -1)
+        _mix_vol(a_ref, star_ref, d_ref, 1)
         dn = d_ref[...]
         for ref, w in accs:
             ref[...] = ref[...] + w[k + 1] * dn
@@ -203,15 +205,23 @@
     return bv_ref[...] - ftot
 
 
-def _kernel_a1(x_ref, star_ref, stiff_ref, trace_ref, send_ref,
+def _kernel_a1(grp_ref, x_ref, star_ref, stiff_ref, trace_ref, send_ref,
                first_ref, later_ref, t1_ref, s1lo, s1hi, s1g,
                d_ref, a_ref, acc1_ref, acc2_ref, yt_ref):
     x = _load_field(x_ref)
-    stiff_st = jnp.concatenate([stiff_ref[d] for d in range(3)], axis=0)
-    _taylor(x, star_ref, _lhs3(stiff_st), d_ref, a_ref, [(acc1_ref, W_FIRST), (acc2_ref, W_LATER)])
+    stiff_p = _lhs3(jnp.concatenate([stiff_ref[d] for d in range(3)], axis=0))
+
+    @pl.when(grp_ref[0] == 0)
+    def _():
+        _taylor(x, star_ref, stiff_p, d_ref, a_ref, [(acc1_ref, W_FIRST)])
+
+    @pl.when(grp_ref[0] != 0)
+    def _():
+        _taylor(x, star_ref, stiff_p, d_ref, a_ref, [(acc1_ref, W_FIRST), (acc2_ref, W_LATER)])
+        later_ref[...] = acc2_ref[...]
+
     first = acc1_ref[...]
     first_ref[...] = first
-    later_ref[...] = acc2_ref[...]
     _table(first, _lhs3(_rows84(trace_ref)), yt_ref, t1_ref)
     _send([t1_ref[...]], send_ref, [(s1lo, s1hi, s1g)])
 
@@ -346,10 +356,10 @@
     first, later, t1, s1lo, s1hi, s1g = pl.pallas_call(
         _kernel_a1,
         out_shape=(flat, flat, table, part, part, part),
-        in_specs=[_vmem()] * 5,
+        in_specs=[_smem()] + [_vmem()] * 5,
         out_specs=tuple([_vmem()] * 6),
         scratch_shapes=[wide, amat, wide, wide, ytr],
-    )(x0, star, stiff, trace, send)
+    )(grp, x0, star, stiff, trace, send)
 
     r1 = exchange_fault(s1lo, s1hi, s1g)
 

time: 57 us -> 57.2 us (level)
  no operation moved by 1% of the time
where the time goes in v9:
time: 57.2 us; the launch traced here: 56.8 us
  starting transfers between devices  34.8 us (61%)
  Pallas kernels  20.5 us (36%)
  local copies, waits for them, and re-layouts  1.37 us (2%)
    ppermute x1, starting transfers between devices, exchange_fault(): from_ghi = lax.ppermute(g, axes, [(n_dom + i, i) for i in range(n_dom)])  13.8 us
    ppermute x1, starting transfers between devices, exchange(): from_ghi = lax.ppermute(gdn, 'grp', [(i + 1, i) for i in range(n_grp - 1)])  8.27 us
    ppermute x1, starting transfers between devices, exchange(): from_hi = lax.ppermute(lo, 'dom', [(i + 1, i) for i in range(n_dom - 1)])  7.58 us
    pallas_call x1, Pallas kernels, local(): pl.pallas_call(_kernel_a1, out_shape=(flat, flat, table, part, part, part...  6.31 us
    pallas_call x1, Pallas kernels, local(): pl.pallas_call(_kernel_b2, out_shape=(flat, yflux), in_specs=[_vmem()] *...  4.23 us
    pallas_call x1, Pallas kernels, local(): pl.pallas_call(_kernel_a2, out_shape=(flat, table, part, part, part, part...  3.66 us
    pallas_call x1, Pallas kernels, local(): pl.pallas_call(_kernel_c, out_shape=field, in_specs=[_vmem()] * 10, out_s...  3.19 us
    pallas_call x1, Pallas kernels, local(): pl.pallas_call(_kernel_b, out_shape=(flat, flat, table, part, part, part,...  3.09 us
  transfers between devices with their start and end apart: 7, of which 0 were waited for; matrix products, arithmetic and copies ran while one was open for 0% of the time, Pallas kernels for 14%

profile of v9, /device:TPU:24, one launch (start us, length us, event | category | flops | bytes accessed | tf_op | source)
XLA Modules:
  0.0 56.8 jit_solution(9908050367002334749)
XLA Ops:
  0.0 6.3 %shard_map.100 = (f32[56,1152]{1,0:T(8,128)}, f32[56,1152]{1,0:T(8,128)}, f32[216,512]{1,0:T(8,128)}, f32[216,128]{1,0:T(8,128)}, f32[216,128]{1,0:T(8,128)}, /*index=5*/f32[216,128]{1,0:T(8,128)}) custom-call(s32[1]{0:T(128)} %bitcast.grp_ref, f32[9,56,128]{2,1,0:T(8,128)} %bitcast.16, f32[9,9,3,128]{3,2,1,0:T(4,128)} %bitcast.8, f32[3,56,56]{2,1,0:T(8,128)} %stiff_ref.7, ...), custom_call_target="tpu_custom_call" | custom-call | tf_op jit(solution)/shard_map/pallas_call | solution.py:356
  6.3 0.7 %collective-permute-start.1 = (f32[216,128]{1,0:T(8,128)}, f32[216,128]{1,0:T(8,128)S(1)}, u32[]{:S(2)}, u32[]{:S(2)}) collective-permute-start(f32[216,128]{1,0:T(8,128)} %get-tuple-element.31.s1lo), channel_id=1, source_target_pairs={{1,0},{2,1},{3,2},{4,3},{5,4},{6,5},{7,6},{8,7},{9,8},{10,9},{11,1... | collective-permute-start | bytes 331784 | tf_op jit(solution)/shard_map/ppermute | solution.py:329
  7.0 0.7 %collective-permute-start = (f32[216,128]{1,0:T(8,128)}, f32[216,128]{1,0:T(8,128)S(1)}, u32[]{:S(2)}, u32[]{:S(2)}) collective-permute-start(f32[216,128]{1,0:T(8,128)} %get-tuple-element.32.s1hi), channel_id=1, source_target_pairs={{0,1},{1,2},{2,3},{3,4},{4,5},{5,6},{6,7},{7,8},{8,9},{9,10},{10,1... | collective-permute-start | bytes 331784 | tf_op jit(solution)/shard_map/ppermute | solution.py:328
  7.6 13.8 %collective-permute-start.2 = (f32[216,128]{1,0:T(8,128)}, f32[216,128]{1,0:T(8,128)S(1)}, u32[]{:S(2)}, u32[]{:S(2)}) collective-permute-start(f32[216,128]{1,0:T(8,128)} %get-tuple-element.33.s1g), channel_id=1, source_target_pairs={{64,0},{65,1},{66,2},{67,3},{68,4},{69,5},{70,6},{71,7},{72,8},{73... | collective-permute-start | bytes 331784 | tf_op jit(solution)/shard_map/ppermute | solution.py:330
  21.4 3.7 %shard_map.101 = (f32[56,1152]{1,0:T(8,128)}, f32[216,512]{1,0:T(8,128)}, f32[216,128]{1,0:T(8,128)}, f32[216,128]{1,0:T(8,128)}, f32[216,128]{1,0:T(8,128)}, /*...) custom-call(s32[1]{0:T(128)} %bitcast.grp_ref, f32[9,56,128]{2,1,0:T(8,128)} %bitcast.17, ...), custom_call_target="tpu_custom_call" | custom-call | tf_op jit(solution)/shard_map/pallas_call | solution.py:366
  25.1 0.0 collective-permute-done.1.r1hi
  25.1 0.0 collective-permute-done.r1lo
  25.1 0.0 collective-permute-done.2.r1ghi
  25.2 0.6 %copy-done.4 = f32[216,128]{1,0:T(8,128)} copy-done((f32[216,128]{1,0:T(8,128)}, f32[216,128]{1,0:T(8,128)S(1)}, u32[]{:S(2)}) %copy-start.4) | copy-done | bytes 110616
  25.8 0.0 copy-done.5
  25.8 0.0 copy-done.6
  25.8 3.1 %shard_map.102 = (f32[56,1152]{1,0:T(8,128)}, f32[56,1152]{1,0:T(8,128)}, f32[216,512]{1,0:T(8,128)}, f32[216,128]{1,0:T(8,128)}, f32[216,128]{1,0:T(8,128)}, /*index=5*/f32[216,128]{1,0:T(8,128)}, f32[216,128]{1,0:T(8,128)}) custom-call(s32[1]{0:T(128)} %bitcast.grp_ref, f32[9,56,128]{2,1,0:T(8,128)} %bitcast.18, f32[56,1152]{1,0:T(8,128)} %get-tuple-element.34.fl_ref, ...), custom_call_target="tpu_custom_call" | custom-call | tf_op jit(solution)/shard_map/pallas_call | solution.py:375
  28.9 1.9 %collective-permute-start.3 = (f32[216,128]{1,0:T(8,128)}, f32[216,128]{1,0:T(8,128)S(1)}, u32[]{:S(2)}, u32[]{:S(2)}) collective-permute-start(f32[216,128]{1,0:T(8,128)} %get-tuple-element.47), channel_id=1, source_target_pairs={{0,1},{1,2},{2,3},{3,4},{4,5},{5,6},{6,7},{7,8},{8,9},{9,10},{10,1... | collective-permute-start | bytes 331784 | tf_op jit(solution)/shard_map/ppermute | solution.py:318
  30.8 7.6 %collective-permute-start.4 = (f32[216,128]{1,0:T(8,128)}, f32[216,128]{1,0:T(8,128)S(1)}, u32[]{:S(2)}, u32[]{:S(2)}) collective-permute-start(f32[216,128]{1,0:T(8,128)} %get-tuple-element.48), channel_id=1, source_target_pairs={{1,0},{2,1},{3,2},{4,3},{5,4},{6,5},{7,6},{8,7},{9,8},{10,9},{11,1... | collective-permute-start | bytes 331784 | tf_op jit(solution)/shard_map/ppermute | solution.py:319
  38.4 1.9 %collective-permute-start.5 = (f32[216,128]{1,0:T(8,128)}, f32[216,128]{1,0:T(8,128)S(1)}, u32[]{:S(2)}, u32[]{:S(2)}) collective-permute-start(f32[216,128]{1,0:T(8,128)} %get-tuple-element.49), channel_id=1, source_target_pairs={{0,64},{64,128},{128,192},{192,256},{256,320},{320,384},{384,448},... | collective-permute-start | bytes 331784 | tf_op jit(solution)/shard_map/ppermute | solution.py:320
  40.4 8.3 %collective-permute-start.6 = (f32[216,128]{1,0:T(8,128)}, f32[216,128]{1,0:T(8,128)S(1)}, u32[]{:S(2)}, u32[]{:S(2)}) collective-permute-start(f32[216,128]{1,0:T(8,128)} %get-tuple-element.50), channel_id=1, source_target_pairs={{64,0},{128,64},{192,128},{256,192},{320,256},{384,320},{448,384},... | collective-permute-start | bytes 331784 | tf_op jit(solution)/shard_map/ppermute | solution.py:321
  48.6 4.2 %shard_map.103 = (f32[56,1152]{1,0:T(8,128)}, f32[96,1152]{1,0:T(8,128)}) custom-call(f32[56,1152]{1,0:T(8,128)} %get-tuple-element.42.base_ref, f32[56,1152]{1,0:T(8,128)} %get-tuple-element.43.integ_ref, f32[216,512]{1,0:T(8,128)} %get-tuple-element.44.own_ref, f32[9,9,3,128]{3,2,1,0:T(4,128)} %bitcast.11, f32[9,9,4,128]{3,2,1,0:T(4,128)} %bitcast.20, ...), custom_call_target="tpu_custom_call" | custom-call | tf_op jit(solution)/shard_map/pallas_call | solution.py:386
  52.9 0.0 collective-permute-done.4.r2hi
  52.9 0.0 collective-permute-done.6.r2ghi
  52.9 0.6 %copy-done = f32[216,128]{1,0:T(8,128)} copy-done((f32[216,128]{1,0:T(8,128)}, f32[216,128]{1,0:T(8,128)S(1)}, u32[]{:S(2)}) %copy-start) | copy-done | bytes 110616
  53.5 0.0 copy-done.1
  53.5 0.0 copy-done.2
  53.6 0.0 copy-done.3
  53.6 3.2 %shard_map.104 = f32[9,56,128]{2,1,0:T(8,128)} custom-call(f32[56,1152]{1,0:T(8,128)} %get-tuple-element.45.bv_ref, f32[96,1152]{1,0:T(8,128)} %get-tuple-element.46.yp_ref, f32[216,128]{1,0:T(8,128)} %copy-done, f32[216,128]{1,0:T(8,128)} %copy-done.1, f32[216,128]{1,0:T(8,128)} %copy-done.2, f32[216,128]{1,0:T(8,128)} %copy-done.3, s32[4,128]{1,0:T(4,128)} %slot_ref.7, ...), custom_call_target="tpu_custom_call" | custom-call | tf_op jit(solution)/shard_map/pallas_call | solution.py:394
  (9 shorter events, 0.0 us)
Async XLA Ops:
  6.3 18.8 %collective-permute-start.1 = (f32[216,128]{1,0:T(8,128)}, f32[216,128]{1,0:T(8,128)S(1)}, u32[]{:S(2)}, u32[]{:S(2)}) collective-permute-start(f32[216,128]{1,0:T(8,128)} %get-tuple-element.31.s1lo), channel_id=1, source_target_pairs={{1,0},{2,1},{3,2},{4,3},{5,4},{6,5},{7,6},{8,7},{9,8},{10,9},{11,1... | collective-permute-start | bytes 331784 | tf_op jit(solution)/shard_map/ppermute | solution.py:329
  7.0 18.2 %collective-permute-start = (f32[216,128]{1,0:T(8,128)}, f32[216,128]{1,0:T(8,128)S(1)}, u32[]{:S(2)}, u32[]{:S(2)}) collective-permute-start(f32[216,128]{1,0:T(8,128)} %get-tuple-element.32.s1hi), channel_id=1, source_target_pairs={{0,1},{1,2},{2,3},{3,4},{4,5},{5,6},{6,7},{7,8},{8,9},{9,10},{10,1... | collective-permute-start | bytes 331784 | tf_op jit(solution)/shard_map/ppermute | solution.py:328
  7.6 17.5 %collective-permute-start.2 = (f32[216,128]{1,0:T(8,128)}, f32[216,128]{1,0:T(8,128)S(1)}, u32[]{:S(2)}, u32[]{:S(2)}) collective-permute-start(f32[216,128]{1,0:T(8,128)} %get-tuple-element.33.s1g), channel_id=1, source_target_pairs={{64,0},{65,1},{66,2},{67,3},{68,4},{69,5},{70,6},{71,7},{72,8},{73... | collective-permute-start | bytes 331784 | tf_op jit(solution)/shard_map/ppermute | solution.py:330
  25.1 0.7 %copy-start.4 = (f32[216,128]{1,0:T(8,128)}, f32[216,128]{1,0:T(8,128)S(1)}, u32[]{:S(2)}) copy-start(f32[216,128]{1,0:T(8,128)S(1)} %collective-permute-done.1.r1hi) | copy-start | bytes 331780
  25.1 0.7 %copy-start.5 = (f32[216,128]{1,0:T(8,128)}, f32[216,128]{1,0:T(8,128)S(1)}, u32[]{:S(2)}) copy-start(f32[216,128]{1,0:T(8,128)S(1)} %collective-permute-done.r1lo) | copy-start | bytes 331780
  25.2 0.7 %copy-start.6 = (f32[216,128]{1,0:T(8,128)}, f32[216,128]{1,0:T(8,128)S(1)}, u32[]{:S(2)}) copy-start(f32[216,128]{1,0:T(8,128)S(1)} %collective-permute-done.2.r1ghi) | copy-start | bytes 331780
  28.9 23.9 %collective-permute-start.3 = (f32[216,128]{1,0:T(8,128)}, f32[216,128]{1,0:T(8,128)S(1)}, u32[]{:S(2)}, u32[]{:S(2)}) collective-permute-start(f32[216,128]{1,0:T(8,128)} %get-tuple-element.47), channel_id=1, source_target_pairs={{0,1},{1,2},{2,3},{3,4},{4,5},{5,6},{6,7},{7,8},{8,9},{9,10},{10,1... | collective-permute-start | bytes 331784 | tf_op jit(solution)/shard_map/ppermute | solution.py:318
  30.8 22.0 %collective-permute-start.4 = (f32[216,128]{1,0:T(8,128)}, f32[216,128]{1,0:T(8,128)S(1)}, u32[]{:S(2)}, u32[]{:S(2)}) collective-permute-start(f32[216,128]{1,0:T(8,128)} %get-tuple-element.48), channel_id=1, source_target_pairs={{1,0},{2,1},{3,2},{4,3},{5,4},{6,5},{7,6},{8,7},{9,8},{10,9},{11,1... | collective-permute-start | bytes 331784 | tf_op jit(solution)/shard_map/ppermute | solution.py:319
  38.4 14.5 %collective-permute-start.5 = (f32[216,128]{1,0:T(8,128)}, f32[216,128]{1,0:T(8,128)S(1)}, u32[]{:S(2)}, u32[]{:S(2)}) collective-permute-start(f32[216,128]{1,0:T(8,128)} %get-tuple-element.49), channel_id=1, source_target_pairs={{0,64},{64,128},{128,192},{192,256},{256,320},{320,384},{384,448},... | collective-permute-start | bytes 331784 | tf_op jit(solution)/shard_map/ppermute | solution.py:320
  40.4 12.6 %collective-permute-start.6 = (f32[216,128]{1,0:T(8,128)}, f32[216,128]{1,0:T(8,128)S(1)}, u32[]{:S(2)}, u32[]{:S(2)}) collective-permute-start(f32[216,128]{1,0:T(8,128)} %get-tuple-element.50), channel_id=1, source_target_pairs={{64,0},{128,64},{192,128},{256,192},{320,256},{384,320},{448,384},... | collective-permute-start | bytes 331784 | tf_op jit(solution)/shard_map/ppermute | solution.py:321
  52.9 0.6 %copy-start = (f32[216,128]{1,0:T(8,128)}, f32[216,128]{1,0:T(8,128)S(1)}, u32[]{:S(2)}) copy-start(f32[216,128]{1,0:T(8,128)S(1)} %collective-permute-done.3.r2lo) | copy-start | bytes 331780
  52.9 0.7 %copy-start.1 = (f32[216,128]{1,0:T(8,128)}, f32[216,128]{1,0:T(8,128)S(1)}, u32[]{:S(2)}) copy-start(f32[216,128]{1,0:T(8,128)S(1)} %collective-permute-done.4.r2hi) | copy-start | bytes 331780
  52.9 0.7 %copy-start.2 = (f32[216,128]{1,0:T(8,128)}, f32[216,128]{1,0:T(8,128)S(1)}, u32[]{:S(2)}) copy-start(f32[216,128]{1,0:T(8,128)S(1)} %collective-permute-done.5.r2glo) | copy-start | bytes 331780
  52.9 0.7 %copy-start.3 = (f32[216,128]{1,0:T(8,128)}, f32[216,128]{1,0:T(8,128)S(1)}, u32[]{:S(2)}) copy-start(f32[216,128]{1,0:T(8,128)S(1)} %collective-permute-done.6.r2ghi) | copy-start | bytes 331780

commit v10 on v7

--- a/solution.py
+++ b/solution.py
@@ -149,7 +149,11 @@
     parts = jnp.concatenate(_split3(comb), axis=1)
     for f in range(4):
         v = slot_ref[f:f + 1, :]
-        if received:
+        if received == "fault":
+            s = v - E
+            src = jnp.where((v < E) | ((s >= 2 * E) & (s < 2 * E + 64)), -1, s - jnp.where(s >= 2 * E, 64, 0))
+            rows = lax.broadcasted_iota(jnp.int32, (3 * E, E), 0)
+        elif received:
             s = v - E
             src = jnp.where(v < E, -1, s + jnp.where(s >= 2 * E, 64, 0))
         else:
@@ -196,8 +200,8 @@
     _fmix([(own_ref, fo_ref), (g_ref, fn_ref)], yp_ref)
 
 
-def _finish(bv_ref, yp_ref, recv, fn_ref, lift_p, slot_ref, face_ref, g_ref, yf_ref):
-    _gather(jnp.concatenate(recv, axis=1), slot_ref, face_ref, g_ref, True)
+def _finish(bv_ref, yp_ref, recv, fn_ref, lift_p, slot_ref, face_ref, g_ref, yf_ref, received=True):
+    _gather(jnp.concatenate(recv, axis=1), slot_ref, face_ref, g_ref, received)
     _fmix([(g_ref, fn_ref)], yf_ref, yp_ref)
     ftot = _tdot(lift_p, _rhs3_rows([yf_ref[f * FP:(f + 1) * FP, :] for f in range(4)], 32))
     return bv_ref[...] - ftot
@@ -246,9 +250,9 @@
 
     @pl.when(grp == 0)
     def _():
-        recv = [r1lo[...], r1hi[...], jnp.zeros((TR, E), F32), r1ghi[...]]
+        recv = [r1lo[...], r1hi[...], r1ghi[...]]
         mid = _finish(bv_ref, yp_ref, recv, fn_ref, _lift_parts(lift_ref, lt_ref), slot_ref, face_ref,
-                      g_ref, yf_ref)
+                      g_ref, yf_ref, "fault")
         base_ref[...] = mid
         stiff_st = jnp.concatenate([stiff_ref[d] for d in range(3)], axis=0)
         _taylor(mid, star_ref, _lhs3(stiff_st), d_ref, a_ref, [(acc_ref, W_FIRST)])

time: 57 us -> 57 us (level)
  no operation moved by 1% of the time
where the time goes in v10:
time: 57 us; the launch traced here: 56.6 us
  starting transfers between devices  34.7 us (61%)
  Pallas kernels  20.4 us (36%)
  local copies, waits for them, and re-layouts  1.37 us (2%)
    ppermute x1, starting transfers between devices, exchange_fault(): from_ghi = lax.ppermute(g, axes, [(n_dom + i, i) for i in range(n_dom)])  13.8 us
    ppermute x1, starting transfers between devices, exchange(): from_ghi = lax.ppermute(gdn, 'grp', [(i + 1, i) for i in range(n_grp - 1)])  8.13 us
    ppermute x1, starting transfers between devices, exchange(): from_hi = lax.ppermute(lo, 'dom', [(i + 1, i) for i in range(n_dom - 1)])  7.58 us
    pallas_call x1, Pallas kernels, local(): pl.pallas_call(_kernel_a1, out_shape=(flat, flat, table, part, part, part...  6.01 us
    pallas_call x1, Pallas kernels, local(): pl.pallas_call(_kernel_b2, out_shape=(flat, yflux), in_specs=[_vmem()] *...  4.23 us
    pallas_call x1, Pallas kernels, local(): pl.pallas_call(_kernel_a2, out_shape=(flat, table, part, part, part, part...  3.66 us
    pallas_call x1, Pallas kernels, local(): pl.pallas_call(_kernel_b, out_shape=(flat, flat, table, part, part, part,...  3.27 us
    pallas_call x1, Pallas kernels, local(): pl.pallas_call(_kernel_c, out_shape=field, in_specs=[_vmem()] * 10, out_s...  3.19 us
  transfers between devices with their start and end apart: 7, of which 0 were waited for; matrix products, arithmetic and copies ran while one was open for 0% of the time, Pallas kernels for 14%

profile of v10, /device:TPU:24, one launch (start us, length us, event | category | flops | bytes accessed | tf_op | source)
XLA Modules:
  0.0 56.6 jit_solution(12447381955510309139)
XLA Ops:
  0.0 6.0 %shard_map.100 = (f32[56,1152]{1,0:T(8,128)}, f32[56,1152]{1,0:T(8,128)}, f32[216,512]{1,0:T(8,128)}, f32[216,128]{1,0:T(8,128)}, f32[216,128]{1,0:T(8,128)}, /*index=5*/f32[216,128]{1,0:T(8,128)}) custom-call(f32[9,56,128]{2,1,0:T(8,128)} %bitcast.16, f32[9,9,3,128]{3,2,1,0:T(4,128)} %bitcast.12, f32[3,56,56]{2,1,0:T(8,128)} %stiff_ref.7, ...), custom_call_target="tpu_custom_call" | custom-call | tf_op jit(solution)/shard_map/pallas_call | solution.py:350
  6.0 0.7 %collective-permute-start.1 = (f32[216,128]{1,0:T(8,128)}, f32[216,128]{1,0:T(8,128)S(1)}, u32[]{:S(2)}, u32[]{:S(2)}) collective-permute-start(f32[216,128]{1,0:T(8,128)} %get-tuple-element.31.s1lo), channel_id=1, source_target_pairs={{1,0},{2,1},{3,2},{4,3},{5,4},{6,5},{7,6},{8,7},{9,8},{10,9},{11,1... | collective-permute-start | bytes 331784 | tf_op jit(solution)/shard_map/ppermute | solution.py:323
  6.7 0.7 %collective-permute-start = (f32[216,128]{1,0:T(8,128)}, f32[216,128]{1,0:T(8,128)S(1)}, u32[]{:S(2)}, u32[]{:S(2)}) collective-permute-start(f32[216,128]{1,0:T(8,128)} %get-tuple-element.32.s1hi), channel_id=1, source_target_pairs={{0,1},{1,2},{2,3},{3,4},{4,5},{5,6},{6,7},{7,8},{8,9},{9,10},{10,1... | collective-permute-start | bytes 331784 | tf_op jit(solution)/shard_map/ppermute | solution.py:322
  7.3 13.8 %collective-permute-start.2 = (f32[216,128]{1,0:T(8,128)}, f32[216,128]{1,0:T(8,128)S(1)}, u32[]{:S(2)}, u32[]{:S(2)}) collective-permute-start(f32[216,128]{1,0:T(8,128)} %get-tuple-element.33.s1g), channel_id=1, source_target_pairs={{64,0},{65,1},{66,2},{67,3},{68,4},{69,5},{70,6},{71,7},{72,8},{73... | collective-permute-start | bytes 331784 | tf_op jit(solution)/shard_map/ppermute | solution.py:324
  21.2 3.7 %shard_map.101 = (f32[56,1152]{1,0:T(8,128)}, f32[216,512]{1,0:T(8,128)}, f32[216,128]{1,0:T(8,128)}, f32[216,128]{1,0:T(8,128)}, f32[216,128]{1,0:T(8,128)}, /*...) custom-call(s32[1]{0:T(128)} %bitcast.grp_ref, f32[9,56,128]{2,1,0:T(8,128)} %bitcast.17, ...), custom_call_target="tpu_custom_call" | custom-call | tf_op jit(solution)/shard_map/pallas_call | solution.py:360
  24.9 0.0 collective-permute-done.1.r1hi
  24.9 0.0 collective-permute-done.r1lo
  24.9 0.0 collective-permute-done.2.r1ghi
  24.9 0.6 %copy-done.4 = f32[216,128]{1,0:T(8,128)} copy-done((f32[216,128]{1,0:T(8,128)}, f32[216,128]{1,0:T(8,128)S(1)}, u32[]{:S(2)}) %copy-start.4) | copy-done | bytes 110616
  25.5 0.0 copy-done.5
  25.6 0.0 copy-done.6
  25.6 3.3 %shard_map.102 = (f32[56,1152]{1,0:T(8,128)}, f32[56,1152]{1,0:T(8,128)}, f32[216,512]{1,0:T(8,128)}, f32[216,128]{1,0:T(8,128)}, f32[216,128]{1,0:T(8,128)}, /*index=5*/f32[216,128]{1,0:T(8,128)}, f32[216,128]{1,0:T(8,128)}) custom-call(s32[1]{0:T(128)} %bitcast.grp_ref, f32[9,56,128]{2,1,0:T(8,128)} %bitcast.18, f32[56,1152]{1,0:T(8,128)} %get-tuple-element.34.fl_ref, ...), custom_call_target="tpu_custom_call" | custom-call | tf_op jit(solution)/shard_map/pallas_call | solution.py:369
  28.9 1.9 %collective-permute-start.3 = (f32[216,128]{1,0:T(8,128)}, f32[216,128]{1,0:T(8,128)S(1)}, u32[]{:S(2)}, u32[]{:S(2)}) collective-permute-start(f32[216,128]{1,0:T(8,128)} %get-tuple-element.47), channel_id=1, source_target_pairs={{0,1},{1,2},{2,3},{3,4},{4,5},{5,6},{6,7},{7,8},{8,9},{9,10},{10,1... | collective-permute-start | bytes 331784 | tf_op jit(solution)/shard_map/ppermute | solution.py:312
  30.8 7.6 %collective-permute-start.4 = (f32[216,128]{1,0:T(8,128)}, f32[216,128]{1,0:T(8,128)S(1)}, u32[]{:S(2)}, u32[]{:S(2)}) collective-permute-start(f32[216,128]{1,0:T(8,128)} %get-tuple-element.48), channel_id=1, source_target_pairs={{1,0},{2,1},{3,2},{4,3},{5,4},{6,5},{7,6},{8,7},{9,8},{10,9},{11,1... | collective-permute-start | bytes 331784 | tf_op jit(solution)/shard_map/ppermute | solution.py:313
  38.4 1.9 %collective-permute-start.5 = (f32[216,128]{1,0:T(8,128)}, f32[216,128]{1,0:T(8,128)S(1)}, u32[]{:S(2)}, u32[]{:S(2)}) collective-permute-start(f32[216,128]{1,0:T(8,128)} %get-tuple-element.49), channel_id=1, source_target_pairs={{0,64},{64,128},{128,192},{192,256},{256,320},{320,384},{384,448},... | collective-permute-start | bytes 331784 | tf_op jit(solution)/shard_map/ppermute | solution.py:314
  40.3 8.1 %collective-permute-start.6 = (f32[216,128]{1,0:T(8,128)}, f32[216,128]{1,0:T(8,128)S(1)}, u32[]{:S(2)}, u32[]{:S(2)}) collective-permute-start(f32[216,128]{1,0:T(8,128)} %get-tuple-element.50), channel_id=1, source_target_pairs={{64,0},{128,64},{192,128},{256,192},{320,256},{384,320},{448,384},... | collective-permute-start | bytes 331784 | tf_op jit(solution)/shard_map/ppermute | solution.py:315
  48.4 4.2 %shard_map.103 = (f32[56,1152]{1,0:T(8,128)}, f32[96,1152]{1,0:T(8,128)}) custom-call(f32[56,1152]{1,0:T(8,128)} %get-tuple-element.42.base_ref, f32[56,1152]{1,0:T(8,128)} %get-tuple-element.43.integ_ref, f32[216,512]{1,0:T(8,128)} %get-tuple-element.44.own_ref, f32[9,9,3,128]{3,2,1,0:T(4,128)} %bitcast.15, f32[9,9,4,128]{3,2,1,0:T(4,128)} %bitcast.20, ...), custom_call_target="tpu_custom_call" | custom-call | tf_op jit(solution)/shard_map/pallas_call | solution.py:380
  52.7 0.0 collective-permute-done.3.r2lo
  52.7 0.0 collective-permute-done.4.r2hi
  52.7 0.6 %copy-done = f32[216,128]{1,0:T(8,128)} copy-done((f32[216,128]{1,0:T(8,128)}, f32[216,128]{1,0:T(8,128)S(1)}, u32[]{:S(2)}) %copy-start) | copy-done | bytes 110616
  53.3 0.0 copy-done.1
  53.4 0.0 copy-done.2
  53.4 0.0 copy-done.3
  53.4 3.2 %shard_map.104 = f32[9,56,128]{2,1,0:T(8,128)} custom-call(f32[56,1152]{1,0:T(8,128)} %get-tuple-element.45.bv_ref, f32[96,1152]{1,0:T(8,128)} %get-tuple-element.46.yp_ref, f32[216,128]{1,0:T(8,128)} %copy-done, f32[216,128]{1,0:T(8,128)} %copy-done.1, f32[216,128]{1,0:T(8,128)} %copy-done.2, f32[216,128]{1,0:T(8,128)} %copy-done.3, s32[4,128]{1,0:T(4,128)} %slot_ref.7, ...), custom_call_target="tpu_custom_call" | custom-call | tf_op jit(solution)/shard_map/pallas_call | solution.py:388
  (9 shorter events, 0.0 us)
Async XLA Ops:
  6.0 18.9 %collective-permute-start.1 = (f32[216,128]{1,0:T(8,128)}, f32[216,128]{1,0:T(8,128)S(1)}, u32[]{:S(2)}, u32[]{:S(2)}) collective-permute-start(f32[216,128]{1,0:T(8,128)} %get-tuple-element.31.s1lo), channel_id=1, source_target_pairs={{1,0},{2,1},{3,2},{4,3},{5,4},{6,5},{7,6},{8,7},{9,8},{10,9},{11,1... | collective-permute-start | bytes 331784 | tf_op jit(solution)/shard_map/ppermute | solution.py:323
  6.7 18.2 %collective-permute-start = (f32[216,128]{1,0:T(8,128)}, f32[216,128]{1,0:T(8,128)S(1)}, u32[]{:S(2)}, u32[]{:S(2)}) collective-permute-start(f32[216,128]{1,0:T(8,128)} %get-tuple-element.32.s1hi), channel_id=1, source_target_pairs={{0,1},{1,2},{2,3},{3,4},{4,5},{5,6},{6,7},{7,8},{8,9},{9,10},{10,1... | collective-permute-start | bytes 331784 | tf_op jit(solution)/shard_map/ppermute | solution.py:322
  7.3 17.6 %collective-permute-start.2 = (f32[216,128]{1,0:T(8,128)}, f32[216,128]{1,0:T(8,128)S(1)}, u32[]{:S(2)}, u32[]{:S(2)}) collective-permute-start(f32[216,128]{1,0:T(8,128)} %get-tuple-element.33.s1g), channel_id=1, source_target_pairs={{64,0},{65,1},{66,2},{67,3},{68,4},{69,5},{70,6},{71,7},{72,8},{73... | collective-permute-start | bytes 331784 | tf_op jit(solution)/shard_map/ppermute | solution.py:324
  24.9 0.7 %copy-start.4 = (f32[216,128]{1,0:T(8,128)}, f32[216,128]{1,0:T(8,128)S(1)}, u32[]{:S(2)}) copy-start(f32[216,128]{1,0:T(8,128)S(1)} %collective-permute-done.1.r1hi) | copy-start | bytes 331780
  24.9 0.7 %copy-start.5 = (f32[216,128]{1,0:T(8,128)}, f32[216,128]{1,0:T(8,128)S(1)}, u32[]{:S(2)}) copy-start(f32[216,128]{1,0:T(8,128)S(1)} %collective-permute-done.r1lo) | copy-start | bytes 331780
  24.9 0.7 %copy-start.6 = (f32[216,128]{1,0:T(8,128)}, f32[216,128]{1,0:T(8,128)S(1)}, u32[]{:S(2)}) copy-start(f32[216,128]{1,0:T(8,128)S(1)} %collective-permute-done.2.r1ghi) | copy-start | bytes 331780
  28.9 23.8 %collective-permute-start.3 = (f32[216,128]{1,0:T(8,128)}, f32[216,128]{1,0:T(8,128)S(1)}, u32[]{:S(2)}, u32[]{:S(2)}) collective-permute-start(f32[216,128]{1,0:T(8,128)} %get-tuple-element.47), channel_id=1, source_target_pairs={{0,1},{1,2},{2,3},{3,4},{4,5},{5,6},{6,7},{7,8},{8,9},{9,10},{10,1... | collective-permute-start | bytes 331784 | tf_op jit(solution)/shard_map/ppermute | solution.py:312
  30.8 21.9 %collective-permute-start.4 = (f32[216,128]{1,0:T(8,128)}, f32[216,128]{1,0:T(8,128)S(1)}, u32[]{:S(2)}, u32[]{:S(2)}) collective-permute-start(f32[216,128]{1,0:T(8,128)} %get-tuple-element.48), channel_id=1, source_target_pairs={{1,0},{2,1},{3,2},{4,3},{5,4},{6,5},{7,6},{8,7},{9,8},{10,9},{11,1... | collective-permute-start | bytes 331784 | tf_op jit(solution)/shard_map/ppermute | solution.py:313
  38.4 14.3 %collective-permute-start.5 = (f32[216,128]{1,0:T(8,128)}, f32[216,128]{1,0:T(8,128)S(1)}, u32[]{:S(2)}, u32[]{:S(2)}) collective-permute-start(f32[216,128]{1,0:T(8,128)} %get-tuple-element.49), channel_id=1, source_target_pairs={{0,64},{64,128},{128,192},{192,256},{256,320},{320,384},{384,448},... | collective-permute-start | bytes 331784 | tf_op jit(solution)/shard_map/ppermute | solution.py:314
  40.3 12.4 %collective-permute-start.6 = (f32[216,128]{1,0:T(8,128)}, f32[216,128]{1,0:T(8,128)S(1)}, u32[]{:S(2)}, u32[]{:S(2)}) collective-permute-start(f32[216,128]{1,0:T(8,128)} %get-tuple-element.50), channel_id=1, source_target_pairs={{64,0},{128,64},{192,128},{256,192},{320,256},{384,320},{448,384},... | collective-permute-start | bytes 331784 | tf_op jit(solution)/shard_map/ppermute | solution.py:315
  52.7 0.6 %copy-start = (f32[216,128]{1,0:T(8,128)}, f32[216,128]{1,0:T(8,128)S(1)}, u32[]{:S(2)}) copy-start(f32[216,128]{1,0:T(8,128)S(1)} %collective-permute-done.3.r2lo) | copy-start | bytes 331780
  52.7 0.7 %copy-start.1 = (f32[216,128]{1,0:T(8,128)}, f32[216,128]{1,0:T(8,128)S(1)}, u32[]{:S(2)}) copy-start(f32[216,128]{1,0:T(8,128)S(1)} %collective-permute-done.4.r2hi) | copy-start | bytes 331780
  52.7 0.7 %copy-start.2 = (f32[216,128]{1,0:T(8,128)}, f32[216,128]{1,0:T(8,128)S(1)}, u32[]{:S(2)}) copy-start(f32[216,128]{1,0:T(8,128)S(1)} %collective-permute-done.5.r2glo) | copy-start | bytes 331780
  52.7 0.7 %copy-start.3 = (f32[216,128]{1,0:T(8,128)}, f32[216,128]{1,0:T(8,128)S(1)}, u32[]{:S(2)}) copy-start(f32[216,128]{1,0:T(8,128)S(1)} %collective-permute-done.6.r2ghi) | copy-start | bytes 331780
